TPU v7x, 32 devices: a whole 2x2x4 slice. The times are simulated.
32 devices in a mesh: dp: 8 (over z, x), tensor: 4 (over y, core).
Axes of the slice: x: 2, y: 2, z: 4, core: 2. Of those that a mesh axis runs over, the one named last changes fastest.
Arguments:
- tokens: bfloat16 [25088, 768], P(('dp', 'tensor')), may hold values from -6 to 6
- cotangent: bfloat16 [25088, 768], P(('dp', 'tensor')), may hold values from -6 to 6
- norm_gains: float32 [3, 768], replicated, may hold values from 0.5 to 1.5
- qkv_time: float32 [768, 3, 768], P('dp', None, 'tensor'), may hold values from -0.21875 to 0.21875
- proj_time: float32 [768, 768], P('tensor', 'dp'), may hold values from -0.625 to 0.625
- qkv_space: float32 [768, 3, 768], P('dp', None, 'tensor'), may hold values from -0.21875 to 0.21875
- proj_space: float32 [768, 768], P('tensor', 'dp'), may hold values from -1.75 to 1.75
- up_weight: float32 [768, 3072], P('dp', 'tensor'), may hold values from -0.21875 to 0.21875
- down_weight: float32 [3072, 768], P('tensor', 'dp'), may hold values from -0.109375 to 0.109375
Outputs:
- output: bfloat16 [25088, 768], P(('dp', 'tensor'))
- grad_tokens: float32 [25088, 768], P(('dp', 'tensor'))
- grad_gains: float32 [3, 768], replicated
- grad_qkv_time: float32 [768, 3, 768], P('dp', None, 'tensor')
- grad_proj_time: float32 [768, 768], P('tensor', 'dp')
- grad_qkv_space: float32 [768, 3, 768], P('dp', None, 'tensor')
- grad_proj_space: float32 [768, 768], P('tensor', 'dp')
- grad_up: float32 [768, 3072], P('dp', 'tensor')
- grad_down: float32 [3072, 768], P('tensor', 'dp')
All inputs are finite; a program needn't handle non-finite values.
Results may differ from a plain program's by a relative error of at most 0.035.
Values may be sent and summed in bfloat16 or wider, within the bound.
No kernel may reach another device: no remote copies, remote signals or barrier semaphores. Data moves between devices by JAX's collectives and lax.ppermute only.
A program may use at most 192 MiB of HBM per device.

v0:
```python
from functools import partial
import math

import jax
import jax.numpy as jnp
from jax import lax
from jax.sharding import PartitionSpec as P

HD = 64
FRAMES = 8
PATCH = 196


epsilon = 1e-06


def normalize(values, gain_row):
    center = values - jnp.mean(values, axis=-1, keepdims=True)
    spread = jnp.mean(center * center, axis=-1, keepdims=True)
    return center * lax.rsqrt(spread + epsilon) * gain_row


def to_groups(values, temporal):
    trailing = values.shape[1:]
    if temporal:
        clip_count = values.shape[0] // (FRAMES * PATCH)
        shaped = values.reshape((clip_count, FRAMES, PATCH) + trailing)
        shaped = jnp.swapaxes(shaped, 1, 2)
        return shaped.reshape((clip_count * PATCH, FRAMES) + trailing)
    return values.reshape((-1, PATCH) + trailing)


def from_groups(values, temporal):
    trailing = values.shape[2:]
    if temporal:
        clip_count = values.shape[0] // PATCH
        values = jnp.swapaxes(values.reshape((clip_count, PATCH, FRAMES) + trailing), 1, 2)
    return values.reshape((-1,) + trailing)


def attend_forward(normed, w_qkv, temporal):
    factor = 1.0 / math.sqrt(HD)
    width_here = w_qkv.shape[2]
    mixed_qkv = jnp.dot(
        normed, w_qkv.reshape(w_qkv.shape[0], 3 * width_here), preferred_element_type=jnp.float32
    )
    mixed_qkv = mixed_qkv.astype(jnp.bfloat16).reshape(normed.shape[0], 3, width_here // HD, HD)
    grouped = to_groups(mixed_qkv, temporal)
    scores = (
        jnp.einsum(
            "blhe,bmhe->bhlm",
            grouped[:, :, 0],
            grouped[:, :, 1],
            preferred_element_type=jnp.float32,
        )
        * factor
    )
    row_top = jnp.max(scores, axis=-1, keepdims=True)
    shifted = jnp.exp(scores - row_top)
    row_total = jnp.sum(shifted, axis=-1, keepdims=True)
    attn_probs = (shifted / row_total).astype(jnp.bfloat16)
    attended = jnp.einsum(
        "bhlm,bmhe->blhe", attn_probs, grouped[:, :, 2], preferred_element_type=jnp.float32
    )
    merged = from_groups(attended.astype(jnp.bfloat16), temporal).reshape(
        normed.shape[0], width_here
    )
    return (grouped, row_top + jnp.log(row_total), merged)


def attend_backward(normed, w_qkv, w_proj, grouped, summary, merged, grad_rows, temporal):
    factor = 1.0 / math.sqrt(HD)
    width_here = merged.shape[1]
    grad_proj = jnp.dot(merged.T, grad_rows, preferred_element_type=jnp.float32)
    grad_merged = jnp.dot(grad_rows, w_proj.T, preferred_element_type=jnp.float32).astype(
        jnp.bfloat16
    )
    grad_attended = to_groups(grad_merged.reshape(normed.shape[0], width_here // HD, HD), temporal)
    query_rows = grouped[:, :, 0]
    key_rows = grouped[:, :, 1]
    value_rows = grouped[:, :, 2]
    scores = (
        jnp.einsum("blhe,bmhe->bhlm", query_rows, key_rows, preferred_element_type=jnp.float32)
        * factor
    )
    attn_probs = jnp.exp(scores - summary)
    grad_value = jnp.einsum(
        "bhlm,blhe->bmhe",
        attn_probs.astype(jnp.bfloat16),
        grad_attended,
        preferred_element_type=jnp.float32,
    )
    grad_probs = jnp.einsum(
        "blhe,bmhe->bhlm", grad_attended, value_rows, preferred_element_type=jnp.float32
    )
    grad_scores = attn_probs * (
        grad_probs - jnp.sum(grad_probs * attn_probs, axis=-1, keepdims=True)
    )
    grad_scores = grad_scores.astype(jnp.bfloat16)
    grad_query = (
        jnp.einsum("bhlm,bmhe->blhe", grad_scores, key_rows, preferred_element_type=jnp.float32)
        * factor
    )
    grad_key = (
        jnp.einsum("bhlm,blhe->bmhe", grad_scores, query_rows, preferred_element_type=jnp.float32)
        * factor
    )
    stacked = jnp.stack([grad_query, grad_key, grad_value], axis=2).astype(jnp.bfloat16)
    grad_mixed = from_groups(stacked, temporal).reshape(normed.shape[0], 3 * width_here)
    grad_qkv = jnp.dot(normed.T, grad_mixed, preferred_element_type=jnp.float32).reshape(
        normed.shape[1], 3, width_here
    )
    grad_normed = jnp.dot(
        grad_mixed,
        w_qkv.reshape(w_qkv.shape[0], 3 * width_here).T,
        preferred_element_type=jnp.float32,
    )
    return (grad_qkv, grad_proj, grad_normed)


def per_device(
    tokens,
    cotangent,
    norm_gains,
    qkv_time,
    proj_time,
    qkv_space,
    proj_space,
    up_weight,
    down_weight,
):
    gathered = (
        lax.all_gather(qkv_time.astype(jnp.bfloat16), "dp", axis=0, tiled=True),
        lax.all_gather(qkv_space.astype(jnp.bfloat16), "dp", axis=0, tiled=True),
        lax.all_gather(up_weight.astype(jnp.bfloat16), "dp", axis=0, tiled=True),
        lax.all_gather(proj_time.astype(jnp.bfloat16), "dp", axis=1, tiled=True),
        lax.all_gather(proj_space.astype(jnp.bfloat16), "dp", axis=1, tiled=True),
        lax.all_gather(down_weight.astype(jnp.bfloat16), "dp", axis=1, tiled=True),
    )
    time_qkv, space_qkv, up_full, time_proj, space_proj, down_full = gathered

    def spread_rows(values):
        return lax.all_gather(values, "tensor", axis=0, tiled=True)

    def sum_rows(values):
        return lax.psum_scatter(
            values.astype(jnp.bfloat16), "tensor", scatter_dimension=0, tiled=True
        ).astype(jnp.float32)

    def spread_grads(values):
        return lax.all_gather(values, "tensor", axis=0, tiled=True)

    def sum_grads(values):
        return lax.psum_scatter(
            values.astype(jnp.bfloat16), "tensor", scatter_dimension=0, tiled=True
        ).astype(jnp.float32)

    inputs = tokens.astype(jnp.float32)
    normed_time = spread_rows(normalize(inputs, norm_gains[0]).astype(jnp.bfloat16))
    grouped_time, summary_time, merged_time = attend_forward(normed_time, time_qkv, True)
    after_time = inputs + sum_rows(
        jnp.dot(merged_time, time_proj, preferred_element_type=jnp.float32)
    )
    normed_space = spread_rows(normalize(after_time, norm_gains[1]).astype(jnp.bfloat16))
    grouped_space, summary_space, merged_space = attend_forward(normed_space, space_qkv, False)
    after_space = after_time + sum_rows(
        jnp.dot(merged_space, space_proj, preferred_element_type=jnp.float32)
    )
    normed_mlp = spread_rows(normalize(after_space, norm_gains[2]).astype(jnp.bfloat16))
    hidden_pre = jnp.dot(normed_mlp, up_full, preferred_element_type=jnp.float32)
    hidden = jax.nn.gelu(hidden_pre, approximate=False).astype(jnp.bfloat16)
    output = (
        after_space + sum_rows(jnp.dot(hidden, down_full, preferred_element_type=jnp.float32))
    ).astype(jnp.bfloat16)
    gathered = (
        lax.all_gather(qkv_time.astype(jnp.bfloat16), "dp", axis=0, tiled=True),
        lax.all_gather(qkv_space.astype(jnp.bfloat16), "dp", axis=0, tiled=True),
        lax.all_gather(up_weight.astype(jnp.bfloat16), "dp", axis=0, tiled=True),
        lax.all_gather(proj_time.astype(jnp.bfloat16), "dp", axis=1, tiled=True),
        lax.all_gather(proj_space.astype(jnp.bfloat16), "dp", axis=1, tiled=True),
        lax.all_gather(down_weight.astype(jnp.bfloat16), "dp", axis=1, tiled=True),
    )
    time_qkv, space_qkv, up_full, time_proj, space_proj, down_full = gathered
    grad_after = cotangent.astype(jnp.float32)
    down_rows = spread_grads(grad_after.astype(jnp.bfloat16))
    grad_down = jnp.dot(hidden.T, down_rows, preferred_element_type=jnp.float32)
    grad_hidden = jnp.dot(down_rows, down_full.T, preferred_element_type=jnp.float32)
    _, gelu_back = jax.vjp(partial(jax.nn.gelu, approximate=False), hidden_pre)
    grad_pre = gelu_back(grad_hidden)[0].astype(jnp.bfloat16)
    grad_up = jnp.dot(normed_mlp.T, grad_pre, preferred_element_type=jnp.float32)
    _, norm_back = jax.vjp(normalize, after_space, norm_gains[2])
    back_rows, gain_mlp = norm_back(
        sum_grads(jnp.dot(grad_pre, up_full.T, preferred_element_type=jnp.float32))
    )
    grad_after = grad_after + back_rows
    _, norm_back = jax.vjp(normalize, after_time, norm_gains[1])
    space_rows = spread_grads(grad_after.astype(jnp.bfloat16))
    grad_qkv_space, grad_proj_space, grad_normed = attend_backward(
        normed_space,
        space_qkv,
        space_proj,
        grouped_space,
        summary_space,
        merged_space,
        space_rows,
        False,
    )
    back_rows, gain_space = norm_back(sum_grads(grad_normed))
    grad_after = grad_after + back_rows
    time_rows = spread_grads(grad_after.astype(jnp.bfloat16))
    grad_qkv_time, grad_proj_time, grad_normed = attend_backward(
        normed_time, time_qkv, time_proj, grouped_time, summary_time, merged_time, time_rows, True
    )
    _, norm_back = jax.vjp(normalize, inputs, norm_gains[0])
    back_rows, gain_time = norm_back(sum_grads(grad_normed))
    grad_tokens = grad_after + back_rows
    shared = (
        lax.psum_scatter(grad_qkv_time, "dp", scatter_dimension=0, tiled=True),
        lax.psum_scatter(grad_qkv_space, "dp", scatter_dimension=0, tiled=True),
        lax.psum_scatter(grad_up, "dp", scatter_dimension=0, tiled=True),
        lax.psum_scatter(grad_proj_time, "dp", scatter_dimension=1, tiled=True),
        lax.psum_scatter(grad_proj_space, "dp", scatter_dimension=1, tiled=True),
        lax.psum_scatter(grad_down, "dp", scatter_dimension=1, tiled=True),
    )
    grad_qkv_time, grad_qkv_space, grad_up, grad_proj_time, grad_proj_space, grad_down = shared
    grad_gains = lax.psum(jnp.stack([gain_time, gain_space, gain_mlp]), ("dp", "tensor"))
    return (
        output,
        grad_tokens,
        grad_gains,
        grad_qkv_time,
        grad_proj_time,
        grad_qkv_space,
        grad_proj_space,
        grad_up,
        grad_down,
    )


def solution(mesh):
    return jax.shard_map(
        per_device,
        mesh=mesh,
        in_specs=(
            P(("dp", "tensor"), None),
            P(("dp", "tensor"), None),
            P(),
            P("dp", None, "tensor"),
            P("tensor", "dp"),
            P("dp", None, "tensor"),
            P("tensor", "dp"),
            P("dp", "tensor"),
            P("tensor", "dp"),
        ),
        out_specs=(
            P(("dp", "tensor"), None),
            P(("dp", "tensor"), None),
            P(),
            P("dp", None, "tensor"),
            P("tensor", "dp"),
            P("dp", None, "tensor"),
            P("tensor", "dp"),
            P("dp", "tensor"),
            P("tensor", "dp"),
        ),
        check_vma=False,
    )
```

profile of v0, /device:TPU:0, one launch (start us, length us, event | category | flops | bytes accessed | tf_op | source)
XLA Modules:
  0.0 1281.6 jit_solution(17860545573894718845)
XLA Ops:
  14.6 39.0 %all_gather.43 = bf16[768,3,192]{2,1,0:T(4,128)(2,1)S(1)} all-gather(bf16[96,3,192]{2,1,0:T(4,128)(2,1)S(1)} %copy.77), channel_id=1, replica_groups=mesh['dp'=8,'tensor'=4] {'dp'}, dimensions={0}, use_global_device_ids=true | all-gather | bytes 995328 | tf_op jit(solution)/shard_map/all_gather | solution.py:133
  55.7 31.0 %all_gather.44 = bf16[192,768]{0,1:T(8,128)(2,1)S(1)} all-gather(bf16[192,96]{0,1:T(8,128)(2,1)S(1)} %copy.82), channel_id=1, replica_groups=mesh['dp'=8,'tensor'=4] {'dp'}, dimensions={1}, use_global_device_ids=true | all-gather | bytes 331776 | tf_op jit(solution)/shard_map/all_gather | solution.py:136
  94.5 15.6 %reshape_reshape.22 = bf16[2,8,196,3,3,64]{2,1,0,5,4,3:T(8,128)(2,1)} reshape(bf16[3136,576]{0,1:T(8,128)(2,1)} %convolution_convert_fusion.7) | data formatting | bytes 7225344 | tf_op jit(solution)/shard_map/reshape;reshape | solution.py:27
  110.1 12.3 copy.79
  146.9 47.3 %reduce-scatter.17.cloned.1.call-done = bf16[784,768]{1,0:T(8,128)(2,1)} async-done(((bf16[3136,768]{1,0:T(8,128)(2,1)}), bf16[784,768]{1,0:T(8,128)(2,1)}) %reduce-scatter.17.cloned.1.call-update) | async-done | bytes 1204240 | tf_op jit(solution)/shard_map/reduce_scatter | solution.py:146
  198.6 38.6 %all_gather.46 = bf16[768,3,192]{2,1,0:T(4,128)(2,1)} all-gather(bf16[96,3,192]{2,1,0:T(4,128)(2,1)S(1)} %copy.83), channel_id=1, replica_groups=mesh['dp'=8,'tensor'=4] {'dp'}, dimensions={0}, use_global_device_ids=true | all-gather | bytes 995328 | tf_op jit(solution)/shard_map/all_gather | solution.py:134
  240.6 30.9 %all_gather.47 = bf16[192,768]{0,1:T(8,128)(2,1)S(1)} all-gather(bf16[192,96]{0,1:T(8,128)(2,1)S(1)} %copy.90), channel_id=1, replica_groups=mesh['dp'=8,'tensor'=4] {'dp'}, dimensions={1}, use_global_device_ids=true | all-gather | bytes 331776 | tf_op jit(solution)/shard_map/all_gather | solution.py:137
  279.1 15.5 %reshape_reshape.24 = bf16[16,196,3,3,64]{1,0,4,3,2:T(8,128)(2,1)} reshape(bf16[3136,576]{0,1:T(8,128)(2,1)} %convolution_convert_fusion.6) | data formatting | bytes 7225344 | tf_op jit(solution)/shard_map/reshape;reshape | solution.py:30
  320.5 45.8 %reduce-scatter.19.cloned.1.call-done = bf16[784,768]{1,0:T(8,128)(2,1)} async-done(((bf16[3136,768]{1,0:T(8,128)(2,1)}), bf16[784,768]{1,0:T(8,128)(2,1)}) %reduce-scatter.19.cloned.1.call-update) | async-done | bytes 1204240 | tf_op jit(solution)/shard_map/reduce_scatter | solution.py:146
  372.5 36.4 %all-gather.13.cloned.1.call-done = bf16[3136,768]{1,0:T(8,128)(2,1)} async-done(((bf16[784,768]{1,0:T(8,128)(2,1)}), bf16[3136,768]{1,0:T(8,128)(2,1)}) %all-gather.13.cloned.1.call-update) | async-done | bytes 4816912 | tf_op jit(solution)/shard_map/all_gather | solution.py:143
  419.3 33.7 %all-gather.17.cloned.1.call-done = bf16[768,768]{0,1:T(8,128)(2,1)} async-done(((bf16[768,96]{0,1:T(8,128)(2,1)}), bf16[768,768]{0,1:T(8,128)(2,1)}) %all-gather.17.cloned.1.call-update) | async-done | bytes 1179664 | tf_op jit(solution)/shard_map/all_gather | solution.py:138
  453.0 37.8 %all-gather.19.cloned.1.call-done = bf16[3136,768]{1,0:T(8,128)(2,1)} async-done(((bf16[784,768]{1,0:T(8,128)(2,1)}), bf16[3136,768]{1,0:T(8,128)(2,1)}) %all-gather.19.cloned.1.call-update) | async-done | bytes 4816912 | tf_op jit(solution)/shard_map/all_gather | solution.py:151
  490.8 28.6 %add_convert_fusion = (bf16[3136,768]{1,0:T(8,128)(2,1)S(1)}, f32[3136,768]{1,0:T(8,128)}) fusion(f32[3136,768]{1,0:T(8,128)} %fusion.74, bf16[3136,768]{1,0:T(8,128)(2,1)} %all-gather.19.cloned.1.call-done, bf16[768,768]{0,1:T(8,128)(2,1)} %all-gather.17.cloned.1.call-done), kind=kOutput, calls=%fused_computation.7 | convolution fusion | flops 3872784384 | bytes 30081024 | tf_op jit(solution)/shard_map/dot_general | solution.py:187
  546.7 29.1 %reduce-scatter.23.cloned.1.call-done = bf16[784,768]{1,0:T(8,128)(2,1)} async-done(((bf16[3136,768]{1,0:T(8,128)(2,1)}), bf16[784,768]{1,0:T(8,128)(2,1)}) %reduce-scatter.23.cloned.1.call-update) | async-done | bytes 1204240 | tf_op jit(solution)/shard_map/reduce_scatter | solution.py:154
  578.2 48.7 %reduce-scatter.21.cloned.1.call-done = bf16[784,768]{1,0:T(8,128)(2,1)} async-done(((bf16[3136,768]{1,0:T(8,128)(2,1)}), bf16[784,768]{1,0:T(8,128)(2,1)}) %reduce-scatter.21.cloned.1.call-update) | async-done | bytes 1204240 | tf_op jit(solution)/shard_map/reduce_scatter | solution.py:146
  633.6 38.1 %all-gather.21.cloned.1.call-done = bf16[3136,768]{1,0:T(8,128)(2,1)} async-done(((bf16[784,768]{1,0:T(8,128)(2,1)}), bf16[3136,768]{1,0:T(8,128)(2,1)}) %all-gather.21.cloned.1.call-update) | async-done | bytes 4816912 | tf_op jit(solution)/shard_map/all_gather | solution.py:151
  737.1 48.5 %reduce-scatter.25.cloned.1.call-done = bf16[784,768]{1,0:T(8,128)(2,1)} async-done(((bf16[3136,768]{1,0:T(8,128)(2,1)}), bf16[784,768]{1,0:T(8,128)(2,1)}) %reduce-scatter.25.cloned.1.call-update) | async-done | bytes 1204240 | tf_op jit(solution)/shard_map/reduce_scatter | solution.py:154
  800.0 30.7 %all-gather.23.cloned.1.call-done = bf16[3136,768]{1,0:T(8,128)(2,1)} async-done(((bf16[784,768]{1,0:T(8,128)(2,1)}), bf16[3136,768]{1,0:T(8,128)(2,1)}) %all-gather.23.cloned.1.call-update) | async-done | bytes 4816912 | tf_op jit(solution)/shard_map/all_gather | solution.py:151
  950.6 29.1 %reduce-scatter.27.cloned.1.call-done = bf16[784,768]{1,0:T(8,128)(2,1)} async-done(((bf16[3136,768]{1,0:T(8,128)(2,1)}), bf16[784,768]{1,0:T(8,128)(2,1)}) %reduce-scatter.27.cloned.1.call-update) | async-done | bytes 1204240 | tf_op jit(solution)/shard_map/reduce_scatter | solution.py:154
  983.2 40.4 %psum.7 = f32[3,768]{1,0:T(4,128)} all-reduce(f32[3,768]{1,0:T(4,128)S(1)} %pad_maximum_fusion), channel_id=1, replica_groups=mesh['dp'=8,'tensor'=4] {'dp','tensor'}, use_global_device_ids=true, to_apply=%region_27.0 | all-reduce | flops 2304 | bytes 18432 | tf_op jit(solution)/shard_map/psum | solution.py:226
  1027.0 26.9 %reduce-scatter.35.cloned.1.call-done = f32[768,96]{0,1:T(8,128)} async-done(((f32[768,768]{0,1:T(8,128)}), f32[768,96]{0,1:T(8,128)}) %reduce-scatter.35.cloned.1.call-update) | async-done | bytes 294928 | tf_op jit(solution)/shard_map/reduce_scatter | solution.py:223
  1053.9 73.3 %reduce-scatter.33.cloned.1.call-done = f32[96,768]{1,0:T(8,128)} async-done(((f32[768,768]{1,0:T(8,128)}), f32[96,768]{1,0:T(8,128)}) %reduce-scatter.33.cloned.1.call-update) | async-done | bytes 294928 | tf_op jit(solution)/shard_map/reduce_scatter | solution.py:220
  1127.1 73.3 %reduce-scatter.31.cloned.1.call-done = f32[96,3,192]{2,0,1:T(8,128)} async-done(((f32[768,3,192]{2,0,1:T(8,128)}), f32[96,3,192]{2,0,1:T(8,128)}) %reduce-scatter.31.cloned.1.call-update) | async-done | bytes 221200 | tf_op jit(solution)/shard_map/reduce_scatter | solution.py:219
  1200.4 73.3 %reduce-scatter.29.cloned.1.call-done = f32[96,3,192]{2,0,1:T(8,128)} async-done(((f32[768,3,192]{2,0,1:T(8,128)}), f32[96,3,192]{2,0,1:T(8,128)}) %reduce-scatter.29.cloned.1.call-update) | async-done | bytes 221200 | tf_op jit(solution)/shard_map/reduce_scatter | solution.py:218
  (268 shorter events, 340.7 us)
Async XLA Ops:
  8.0 78.6 %all-gather.9.cloned.1.call-start = ((), (), s32[]{:S(2)}) async-start(), calls=%async_computation.12 | async-start | bytes 6021120 | tf_op jit(solution)/shard_map/all_gather | solution.py:143
  12.2 184.4 %copy-start.41 = (f32[768]{0:T(1024)}, f32[768]{0:T(1024)S(1)}, u32[]{:S(2)}) copy-start(f32[768]{0:T(1024)S(1)} %get-tuple-element.17) | copy-start | bytes 9220
  14.3 179.9 %reduce-scatter.17.cloned.1.call-start = ((), (), s32[]{:S(2)}) async-start(), calls=%async_computation.13 | async-start | bytes 6021120 | tf_op jit(solution)/shard_map/reduce_scatter | solution.py:146
  86.6 56.1 %copy-start.27 = (bf16[192,768]{0,1:T(8,128)(2,1)}, bf16[192,768]{0,1:T(8,128)(2,1)S(1)}, u32[]{:S(2)}) copy-start(bf16[192,768]{0,1:T(8,128)(2,1)S(1)} %all_gather.44) | copy-start | bytes 884740
  146.4 125.2 %all-gather.11.cloned.1.call-start = ((), (), s32[]{:S(2)}) async-start(), calls=%async_computation.14 | async-start | bytes 6021120 | tf_op jit(solution)/shard_map/all_gather | solution.py:143
  198.3 168.0 %reduce-scatter.19.cloned.1.call-start = ((), (), s32[]{:S(2)}) async-start(), calls=%async_computation.15 | async-start | bytes 6021120 | tf_op jit(solution)/shard_map/reduce_scatter | solution.py:146
  318.7 53.9 %all-gather.15.cloned.1.call-start = ((), (), s32[]{:S(2)}) async-start(), calls=%async_computation.17 | async-start | bytes 1327104 | tf_op jit(solution)/shard_map/all_gather | solution.py:135
  320.3 88.6 %all-gather.13.cloned.1.call-start = ((), (), s32[]{:S(2)}) async-start(), calls=%async_computation.16 | async-start | bytes 6021120 | tf_op jit(solution)/shard_map/all_gather | solution.py:143
  370.9 82.1 %all-gather.17.cloned.1.call-start = ((), (), s32[]{:S(2)}) async-start(), calls=%async_computation.18 | async-start | bytes 1327104 | tf_op jit(solution)/shard_map/all_gather | solution.py:138
  371.7 119.1 %all-gather.19.cloned.1.call-start = ((), (), s32[]{:S(2)}) async-start(), calls=%async_computation.20 | async-start | bytes 6021120 | tf_op jit(solution)/shard_map/all_gather | solution.py:151
  372.4 203.4 %reduce-scatter.23.cloned.1.call-start = ((), (), s32[]{:S(2)}) async-start(), calls=%async_computation.21 | async-start | bytes 6021120 | tf_op jit(solution)/shard_map/reduce_scatter | solution.py:154
  419.3 102.3 %copy-start.54 = (bf16[768,768]{1,0:T(8,128)(2,1)S(1)}, bf16[768,768]{1,0:T(8,128)(2,1)}, u32[]{:S(2)}) copy-start(bf16[768,768]{1,0:T(8,128)(2,1)} %all-gather.15.cloned.1.call-done) | copy-start | bytes 3538948
  527.2 99.7 %reduce-scatter.21.cloned.1.call-start = ((), (), s32[]{:S(2)}) async-start(), calls=%async_computation.19 | async-start | bytes 6021120 | tf_op jit(solution)/shard_map/reduce_scatter | solution.py:146
  546.7 125.0 %all-gather.21.cloned.1.call-start = ((), (), s32[]{:S(2)}) async-start(), calls=%async_computation.22 | async-start | bytes 6021120 | tf_op jit(solution)/shard_map/all_gather | solution.py:151
  633.5 152.1 %reduce-scatter.25.cloned.1.call-start = ((), (), s32[]{:S(2)}) async-start(), calls=%async_computation.23 | async-start | bytes 6021120 | tf_op jit(solution)/shard_map/reduce_scatter | solution.py:154
  737.0 50.8 %copy-start.48 = (f32[784]{0:T(1024)S(1)}, f32[784]{0:T(1024)}, u32[]{:S(2)}) copy-start(f32[784]{0:T(1024)} %copy-done.47) | copy-start | bytes 9412
  737.0 93.7 %all-gather.23.cloned.1.call-start = ((), (), s32[]{:S(2)}) async-start(), calls=%async_computation.24 | async-start | bytes 6021120 | tf_op jit(solution)/shard_map/all_gather | solution.py:151
  792.6 154.7 %reduce-scatter.39.cloned.1.call-start = ((), (), s32[]{:S(2)}) async-start(), calls=%async_computation.31 | async-start | bytes 884736
  799.8 149.1 %reduce-scatter.37.cloned.1.call-start = ((), (), s32[]{:S(2)}) async-start(), calls=%async_computation.30 | async-start | bytes 884736
  866.2 113.5 %reduce-scatter.27.cloned.1.call-start = ((), (), s32[]{:S(2)}) async-start(), calls=%async_computation.25 | async-start | bytes 6021120 | tf_op jit(solution)/shard_map/reduce_scatter | solution.py:154
  908.0 145.9 %reduce-scatter.35.cloned.1.call-start = ((), (), s32[]{:S(2)}) async-start(), calls=%async_computation.29 | async-start | bytes 2654208 | tf_op jit(solution)/shard_map/reduce_scatter | solution.py:223
  917.6 209.6 %reduce-scatter.33.cloned.1.call-start = ((), (), s32[]{:S(2)}) async-start(), calls=%async_computation.28 | async-start | bytes 2654208 | tf_op jit(solution)/shard_map/reduce_scatter | solution.py:220
  927.4 273.0 %reduce-scatter.31.cloned.1.call-start = ((), (), s32[]{:S(2)}) async-start(), calls=%async_computation.27 | async-start | bytes 2654208 | tf_op jit(solution)/shard_map/reduce_scatter | solution.py:219
  936.6 337.1 %reduce-scatter.29.cloned.1.call-start = ((), (), s32[]{:S(2)}) async-start(), calls=%async_computation.26 | async-start | bytes 2654208 | tf_op jit(solution)/shard_map/reduce_scatter | solution.py:218
  (57 other events, 590.8 us)
Sparse Core Ops, SparseCore 0:
  14.4 40.7 all-gather.8
  146.5 47.5 reduce-scatter.16
  198.4 37.9 all-gather.10
  318.8 47.4 reduce-scatter.18
  633.6 37.9 all-gather.20
  792.7 37.9 all-gather.22
Sparse Core Ops, SparseCore 1:
  321.9 40.2 all-gather.14
  371.0 37.8 all-gather.12
  411.6 41.4 all-gather.16
  454.6 36.2 all-gather.18
  527.3 48.4 reduce-scatter.22
  578.4 48.4 reduce-scatter.20
  737.1 48.4 reduce-scatter.24
  799.9 63.3 reduce-scatter.38
  866.4 63.2 reduce-scatter.36
  932.2 47.5 reduce-scatter.26
  983.6 70.2 reduce-scatter.34
  1058.0 69.1 reduce-scatter.32
  1131.1 69.3 reduce-scatter.30
  1204.5 69.2 reduce-scatter.28
where the time goes:
time: 1290 us; the launch traced here: 1280 us
  waiting for transfers between devices  673 us (52%)
  matrix products  204 us (16%)
  blocking collectives  180 us (14%)
  local copies, waits for them, and re-layouts  136 us (11%)
  other arithmetic  69.9 us (5%)
  between operations  17 us (1%)
    reduce_scatter x3, waiting for transfers between devices, sum_rows(): lax.psum_scatter(values.astype(jnp.bfloat16), 'tensor', scatter_dimension...  142 us
    reduce_scatter x3, waiting for transfers between devices, sum_grads(): lax.psum_scatter(values.astype(jnp.bfloat16), 'tensor', scatter_dimension...  107 us
    all_gather x3, waiting for transfers between devices, spread_grads(): return lax.all_gather(values, 'tensor', axis=0, tiled=True)  107 us
    reduce_scatter x1, waiting for transfers between devices, per_device(): lax.psum_scatter(grad_qkv_time, 'dp', scatter_dimension=0, tiled=True)  73.3 us
    reduce_scatter x1, waiting for transfers between devices, per_device(): lax.psum_scatter(grad_up, 'dp', scatter_dimension=0, tiled=True)  73.3 us
    reduce_scatter x1, waiting for transfers between devices, per_device(): lax.psum_scatter(grad_qkv_space, 'dp', scatter_dimension=0, tiled=True)  73.3 us
    psum x1, blocking collectives, per_device(): lax.psum(jnp.stack([gain_time, gain_space, gain_mlp]), ('dp', 'tensor'))  40.4 us
    all_gather x1, blocking collectives, per_device(): lax.all_gather(qkv_time.astype(jnp.bfloat16), 'dp', axis=0, tiled=True)  39 us
  transfers between devices with their start and end apart: 20, of which 15 were waited for; matrix products, arithmetic and copies ran while one was open for 14% of the time, Pallas kernels for 0%

commit v1 on v0

--- a/solution.py
+++ b/solution.py
@@ -4,7 +4,7 @@
 import jax
 import jax.numpy as jnp
 from jax import lax
-from jax.sharding import PartitionSpec as P
+from jax.sharding import Mesh, PartitionSpec as P
 
 HD = 64
 FRAMES = 8
@@ -116,6 +116,82 @@
         preferred_element_type=jnp.float32,
     )
     return (grad_qkv, grad_proj, grad_normed)
+
+
+WEIGHT_AXES = ("dp", "ty")
+
+
+def gather_weights(shards, layouts):
+    flat = [w.astype(jnp.bfloat16).reshape(1, -1) for w in shards]
+    sizes = [f.shape[1] for f in flat]
+    ny = lax.axis_size("ty")
+    nd = lax.axis_size("dp")
+    whole = lax.all_gather(jnp.concatenate(flat, axis=1), WEIGHT_AXES, axis=0, tiled=True)
+    out = []
+    offset = 0
+    for w, size, (dp_dim, ty_dim) in zip(shards, sizes, layouts):
+        part = whole[:, offset : offset + size].reshape((nd, ny) + w.shape)
+        offset += size
+        order = []
+        for dim in range(w.ndim):
+            if dim == dp_dim:
+                order.append(0)
+            if dim == ty_dim:
+                order.append(1)
+            order.append(dim + 2)
+        shape = list(w.shape)
+        shape[dp_dim] *= nd
+        shape[ty_dim] *= ny
+        out.append(jnp.transpose(part, order).reshape(shape))
+    return out
+
+
+def scatter_grads(grads, layouts, shard_shapes):
+    ny = lax.axis_size("ty")
+    nd = lax.axis_size("dp")
+    flat = []
+    for g, (dp_dim, ty_dim), shard in zip(grads, layouts, shard_shapes):
+        split = []
+        for dim in range(g.ndim):
+            if dim == dp_dim:
+                split.extend([nd, shard[dim]])
+            elif dim == ty_dim:
+                split.extend([ny, shard[dim]])
+            else:
+                split.append(shard[dim])
+        parts = g.reshape(split)
+        pos = 0
+        ty_pos = dp_pos = None
+        rest = []
+        for dim in range(g.ndim):
+            if dim == dp_dim:
+                dp_pos = pos
+                rest.append(pos + 1)
+                pos += 2
+            elif dim == ty_dim:
+                ty_pos = pos
+                rest.append(pos + 1)
+                pos += 2
+            else:
+                rest.append(pos)
+                pos += 1
+        flat.append(jnp.transpose(parts, [dp_pos, ty_pos] + rest).reshape(ny * nd, -1))
+    sizes = [f.shape[1] for f in flat]
+    stacked = jnp.concatenate(flat, axis=1)
+    width = stacked.shape[1]
+    lane = 768 if width % 768 == 0 else width
+    summed = lax.psum_scatter(
+        stacked.reshape(ny * nd * (width // lane), lane),
+        WEIGHT_AXES,
+        scatter_dimension=0,
+        tiled=True,
+    ).reshape(-1)
+    out = []
+    offset = 0
+    for size, shard in zip(sizes, shard_shapes):
+        out.append(summed[offset : offset + size].reshape(shard))
+        offset += size
+    return out
 
 
 def per_device(
@@ -129,31 +205,26 @@
     up_weight,
     down_weight,
 ):
-    gathered = (
-        lax.all_gather(qkv_time.astype(jnp.bfloat16), "dp", axis=0, tiled=True),
-        lax.all_gather(qkv_space.astype(jnp.bfloat16), "dp", axis=0, tiled=True),
-        lax.all_gather(up_weight.astype(jnp.bfloat16), "dp", axis=0, tiled=True),
-        lax.all_gather(proj_time.astype(jnp.bfloat16), "dp", axis=1, tiled=True),
-        lax.all_gather(proj_space.astype(jnp.bfloat16), "dp", axis=1, tiled=True),
-        lax.all_gather(down_weight.astype(jnp.bfloat16), "dp", axis=1, tiled=True),
-    )
-    time_qkv, space_qkv, up_full, time_proj, space_proj, down_full = gathered
+    qkv_layout = (0, 2)
+    proj_layout = (1, 0)
+    up_layout = (0, 1)
+    down_layout = (1, 0)
+    time_qkv, time_proj = gather_weights((qkv_time, proj_time), (qkv_layout, proj_layout))
+    space_qkv, space_proj, up_full, down_full = gather_weights(
+        (qkv_space, proj_space, up_weight, down_weight),
+        (qkv_layout, proj_layout, up_layout, down_layout),
+    )
 
     def spread_rows(values):
-        return lax.all_gather(values, "tensor", axis=0, tiled=True)
+        return lax.all_gather(values, "core", axis=0, tiled=True)
 
     def sum_rows(values):
         return lax.psum_scatter(
-            values.astype(jnp.bfloat16), "tensor", scatter_dimension=0, tiled=True
+            values.astype(jnp.bfloat16), "core", scatter_dimension=0, tiled=True
         ).astype(jnp.float32)
 
-    def spread_grads(values):
-        return lax.all_gather(values, "tensor", axis=0, tiled=True)
-
-    def sum_grads(values):
-        return lax.psum_scatter(
-            values.astype(jnp.bfloat16), "tensor", scatter_dimension=0, tiled=True
-        ).astype(jnp.float32)
+    spread_grads = spread_rows
+    sum_grads = sum_rows
 
     inputs = tokens.astype(jnp.float32)
     normed_time = spread_rows(normalize(inputs, norm_gains[0]).astype(jnp.bfloat16))
@@ -172,15 +243,7 @@
     output = (
         after_space + sum_rows(jnp.dot(hidden, down_full, preferred_element_type=jnp.float32))
     ).astype(jnp.bfloat16)
-    gathered = (
-        lax.all_gather(qkv_time.astype(jnp.bfloat16), "dp", axis=0, tiled=True),
-        lax.all_gather(qkv_space.astype(jnp.bfloat16), "dp", axis=0, tiled=True),
-        lax.all_gather(up_weight.astype(jnp.bfloat16), "dp", axis=0, tiled=True),
-        lax.all_gather(proj_time.astype(jnp.bfloat16), "dp", axis=1, tiled=True),
-        lax.all_gather(proj_space.astype(jnp.bfloat16), "dp", axis=1, tiled=True),
-        lax.all_gather(down_weight.astype(jnp.bfloat16), "dp", axis=1, tiled=True),
-    )
-    time_qkv, space_qkv, up_full, time_proj, space_proj, down_full = gathered
+
     grad_after = cotangent.astype(jnp.float32)
     down_rows = spread_grads(grad_after.astype(jnp.bfloat16))
     grad_down = jnp.dot(hidden.T, down_rows, preferred_element_type=jnp.float32)
@@ -188,6 +251,9 @@
     _, gelu_back = jax.vjp(partial(jax.nn.gelu, approximate=False), hidden_pre)
     grad_pre = gelu_back(grad_hidden)[0].astype(jnp.bfloat16)
     grad_up = jnp.dot(normed_mlp.T, grad_pre, preferred_element_type=jnp.float32)
+    grad_up, grad_down = scatter_grads(
+        (grad_up, grad_down), (up_layout, down_layout), (up_weight.shape, down_weight.shape)
+    )
     _, norm_back = jax.vjp(normalize, after_space, norm_gains[2])
     back_rows, gain_mlp = norm_back(
         sum_grads(jnp.dot(grad_pre, up_full.T, preferred_element_type=jnp.float32))
@@ -205,25 +271,26 @@
         space_rows,
         False,
     )
+    grad_qkv_space, grad_proj_space = scatter_grads(
+        (grad_qkv_space, grad_proj_space),
+        (qkv_layout, proj_layout),
+        (qkv_space.shape, proj_space.shape),
+    )
     back_rows, gain_space = norm_back(sum_grads(grad_normed))
     grad_after = grad_after + back_rows
     time_rows = spread_grads(grad_after.astype(jnp.bfloat16))
     grad_qkv_time, grad_proj_time, grad_normed = attend_backward(
         normed_time, time_qkv, time_proj, grouped_time, summary_time, merged_time, time_rows, True
     )
+    grad_qkv_time, grad_proj_time = scatter_grads(
+        (grad_qkv_time, grad_proj_time),
+        (qkv_layout, proj_layout),
+        (qkv_time.shape, proj_time.shape),
+    )
     _, norm_back = jax.vjp(normalize, inputs, norm_gains[0])
     back_rows, gain_time = norm_back(sum_grads(grad_normed))
     grad_tokens = grad_after + back_rows
-    shared = (
-        lax.psum_scatter(grad_qkv_time, "dp", scatter_dimension=0, tiled=True),
-        lax.psum_scatter(grad_qkv_space, "dp", scatter_dimension=0, tiled=True),
-        lax.psum_scatter(grad_up, "dp", scatter_dimension=0, tiled=True),
-        lax.psum_scatter(grad_proj_time, "dp", scatter_dimension=1, tiled=True),
-        lax.psum_scatter(grad_proj_space, "dp", scatter_dimension=1, tiled=True),
-        lax.psum_scatter(grad_down, "dp", scatter_dimension=1, tiled=True),
-    )
-    grad_qkv_time, grad_qkv_space, grad_up, grad_proj_time, grad_proj_space, grad_down = shared
-    grad_gains = lax.psum(jnp.stack([gain_time, gain_space, gain_mlp]), ("dp", "tensor"))
+    grad_gains = lax.psum(jnp.stack([gain_time, gain_space, gain_mlp]), ("dp", "ty", "core"))
     return (
         output,
         grad_tokens,
@@ -238,30 +305,25 @@
 
 
 def solution(mesh):
-    return jax.shard_map(
-        per_device,
-        mesh=mesh,
-        in_specs=(
-            P(("dp", "tensor"), None),
-            P(("dp", "tensor"), None),
-            P(),
-            P("dp", None, "tensor"),
-            P("tensor", "dp"),
-            P("dp", None, "tensor"),
-            P("tensor", "dp"),
-            P("dp", "tensor"),
-            P("tensor", "dp"),
-        ),
-        out_specs=(
-            P(("dp", "tensor"), None),
-            P(("dp", "tensor"), None),
-            P(),
-            P("dp", None, "tensor"),
-            P("tensor", "dp"),
-            P("dp", None, "tensor"),
-            P("tensor", "dp"),
-            P("dp", "tensor"),
-            P("tensor", "dp"),
-        ),
-        check_vma=False,
-    )
+    def run(*args):
+        rows_here = args[0].shape[0] // mesh.size
+        cores = FRAMES * PATCH // rows_here
+        tensor = mesh.shape["tensor"]
+        assert tensor % cores == 0
+        devices = mesh.devices.reshape(mesh.shape["dp"], tensor // cores, cores)
+        chips = Mesh(devices, ("dp", "ty", "core"))
+        rows = P(("dp", "ty", "core"), None)
+        qkv = P("dp", None, ("ty", "core"))
+        proj = P(("ty", "core"), "dp")
+        up = P("dp", ("ty", "core"))
+        down = P(("ty", "core"), "dp")
+        mapped = jax.shard_map(
+            per_device,
+            mesh=chips,
+            in_specs=(rows, rows, P(), qkv, proj, qkv, proj, up, down),
+            out_specs=(rows, rows, P(), qkv, proj, qkv, proj, up, down),
+            check_vma=False,
+        )
+        return mapped(*args)
+
+    return run

time: 1290 us -> 1250 us (0.969)
  local copies, waits for them, and re-layouts: 136 us -> 336 us
  blocking collectives: 180 us -> 41 us
  waiting for transfers between devices: 673 us -> 571 us
  matrix products: 204 us -> 185 us
  other arithmetic: 69.9 us -> 87.1 us
    reduce_scatter x10 -> x9, waiting for transfers between devices: 495 us -> 317 us  [the longest x3 286 us: scatter_grads(): lax.psum_scatter(stacked.reshape(ny * nd * (width // lane), lane), WEIGHT...]
    all_gather x4 -> x0, blocking collectives: 139 us -> none  [the longest x1 39 us: per_device(): lax.all_gather(qkv_time.astype(jnp.bfloat16), 'dp', axis=0, tiled=True)]
    reshape x1 -> x32, local copies, waits for them, and re-layouts: 5.25 us -> 102 us  [the longest x8 26.3 us: gather_weights(): part = whole[:, offset:offset + size].reshape((nd, ny) + w.shape)]
    all_gather x8, waiting for transfers between devices: 177 us -> 254 us  [the longest x2 241 us: gather_weights(): lax.all_gather(jnp.concatenate(flat, axis=1), WEIGHT_AXES, axis=0, tiled=...]
    unnamed x126 -> x131, local copies, waits for them, and re-layouts: 12.8 us -> 57.3 us
    transpose x2 -> x10, local copies, waits for them, and re-layouts: 17.5 us -> 51.5 us  [the longest x5 21.2 us: scatter_grads(): jnp.transpose(parts, [dp_pos, ty_pos] + rest).reshape(ny * nd, -1)]
    dot_general x1, matrix products: 28.6 us -> 11 us  [per_device(): jnp.dot(down_rows, down_full.T, preferred_element_type=jnp.float32)]
    dot_general x0 -> x4, local copies, waits for them, and re-layouts: none -> 17.1 us  [the longest x2 8.75 us: attend_backward(): jnp.dot(normed.T, grad_mixed, preferred_element_type=jnp.float32)]
  transfers between devices with their start and end apart: 20 -> 17, of which waited for: 15 -> 10; matrix products, arithmetic and copies ran while one was open for 14% -> 31% of each run, Pallas kernels for 0% -> 0%
where the time goes in v1:
time: 1250 us; the launch traced here: 1240 us
  waiting for transfers between devices  571 us (46%)
  local copies, waits for them, and re-layouts  336 us (27%)
  matrix products  185 us (15%)
  other arithmetic  87.1 us (7%)
  blocking collectives  41 us (3%)
  between operations  15.2 us (1%)
    reduce_scatter x3, waiting for transfers between devices, scatter_grads(): lax.psum_scatter(stacked.reshape(ny * nd * (width // lane), lane), WEIGHT...  286 us
    all_gather x2, waiting for transfers between devices, gather_weights(): lax.all_gather(jnp.concatenate(flat, axis=1), WEIGHT_AXES, axis=0, tiled=...  241 us
    unnamed x131, local copies, waits for them, and re-layouts  57.3 us
    psum x1, blocking collectives, per_device(): lax.psum(jnp.stack([gain_time, gain_space, gain_mlp]), ('dp', 'ty', 'core'))  41 us
    reduce_scatter x6, waiting for transfers between devices, sum_rows(): lax.psum_scatter(values.astype(jnp.bfloat16), 'core', scatter_dimension=0...  31.2 us
    dot_general x1, matrix products, per_device(): jnp.dot(normed_mlp, up_full, preferred_element_type=jnp.float32)  27.4 us
    another operation x3, local copies, waits for them, and re-layouts, to_groups(): shaped = values.reshape((clip_count, FRAMES, PATCH) + trailing)  26.5 us
    reshape x8, local copies, waits for them, and re-layouts, gather_weights(): part = whole[:, offset:offset + size].reshape((nd, ny) + w.shape)  26.3 us
  transfers between devices with their start and end apart: 17, of which 10 were waited for; matrix products, arithmetic and copies ran while one was open for 31% of the time, Pallas kernels for 0%

profile of v1, /device:TPU:0, one launch (start us, length us, event | category | flops | bytes accessed | tf_op | source)
XLA Modules:
  0.0 1236.9 jit_solution(403839025935211907)
XLA Ops:
  16.8 77.2 %all-gather.23.cloned.1.call-done = bf16[16,1,73728]{2,1,0:T(2,128)(2,1)} async-done(((bf16[1,1,73728]{2,1,0:T(2,128)(2,1)}), bf16[16,1,73728]{2,1,0:T(2,128)(2,1)}) %all-gather.23.cloned.1.call-update) | async-done | bytes 2359312 | tf_op jit(solution)/shard_map/all_gather | solution.py:129
  128.8 11.8 reshape.366
  140.7 11.3 copy.157
  176.5 10.1 maximum_bitcast_fusion.1
  190.8 164.0 %all-gather.25.cloned.1.call-done = bf16[16,1,221184]{2,1,0:T(2,128)(2,1)} async-done(((bf16[1,1,221184]{2,1,0:T(2,128)(2,1)}), bf16[16,1,221184]{2,1,0:T(2,128)(2,1)}) %all-gather.25.cloned.1.call-update) | async-done | bytes 7077904 | tf_op jit(solution)/shard_map/all_gather | solution.py:129
  354.8 13.5 %copy.158 = bf16[16,1,221184]{2,0,1:T(8,128)(2,1)S(1)} copy(bf16[16,1,221184]{2,1,0:T(2,128)(2,1)} %all-gather.25.cloned.1.call-done) | data formatting | bytes 14155776
  400.7 12.0 reshape.367
  453.1 8.4 reduce-scatter.12.cloned.1.call-done
  486.7 27.4 %multiply_convert_fusion.1 = (bf16[1568,1536]{1,0:T(8,128)(2,1)}, f32[1568,1536]{1,0:T(8,128)}, f32[1568,1536]{1,0:T(8,128)}) fusion(bf16[1568,768]{1,0:T(8,128)(2,1)} %all-gather.15.cloned.1.call-done, bf16[768,1536]{1,0:T(8,128)(2,1)} %bitcast.315), kind=kOutput, calls=%fused_computation.16 | convolution fusion | flops 3855925248 | bytes 28852224 | tf_op jit(solution)/shard_map/dot_general | solution.py:241
  514.1 11.0 fusion.6
  547.1 10.6 reduce-scatter.14.cloned.1.call-done
  564.3 12.4 %all-gather.19.cloned.1.call-done = bf16[1568,768]{1,0:T(8,128)(2,1)} async-done(((bf16[784,768]{1,0:T(8,128)(2,1)}), bf16[1568,768]{1,0:T(8,128)(2,1)}) %all-gather.19.cloned.1.call-update) | async-done | bytes 2408464 | tf_op jit(solution)/shard_map/all_gather | solution.py:219
  599.7 11.5 multiply_convert_fusion
  623.6 9.0 convert_element_type.184
  645.2 10.6 fusion.86
  662.6 8.5 fusion.85
  752.7 10.4 reshape.352
  819.6 12.0 copy.110
  831.6 8.9 reshape_reshape.40
  878.1 16.1 %reduce-scatter.24.cloned.1.call-done = f32[96,768]{1,0:T(8,128)} async-done(((f32[1536,768]{1,0:T(8,128)}), f32[96,768]{1,0:T(8,128)}) %reduce-scatter.24.cloned.1.call-update) | async-done | bytes 294928 | tf_op jit(solution)/shard_map/reduce_scatter | solution.py:183
  897.8 172.6 %reduce-scatter.26.cloned.1.call-done = f32[192,768]{1,0:T(8,128)} async-done(((f32[3072,768]{1,0:T(8,128)}), f32[192,768]{1,0:T(8,128)}) %reduce-scatter.26.cloned.1.call-update) | async-done | bytes 589840 | tf_op jit(solution)/shard_map/reduce_scatter | solution.py:183
  1073.3 8.5 reduce-scatter.20.cloned.1.call-done
  1085.4 41.0 %psum.7 = f32[3,768]{1,0:T(4,128)} all-reduce(f32[3,768]{1,0:T(4,128)S(1)} %pad_maximum_fusion.3), channel_id=1, replica_groups=mesh['dp'=8,'ty'=2,'core'=2] {'dp','ty','core'}, use_global_device_ids=true, to_apply=%region_27.0 | all-reduce | flops 2304 | bytes 18432 | tf_op jit(solution)/shard_map/psum | solution.py:293
  1129.8 96.8 %reduce-scatter.22.cloned.1.call-done = f32[96,768]{1,0:T(8,128)} async-done(((f32[1536,768]{1,0:T(8,128)}), f32[96,768]{1,0:T(8,128)}) %reduce-scatter.22.cloned.1.call-update) | async-done | bytes 294928 | tf_op jit(solution)/shard_map/reduce_scatter | solution.py:183
  (319 shorter events, 446.0 us)
Async XLA Ops:
  7.2 86.7 %all-gather.23.cloned.1.call-start = ((), (), s32[]{:S(2)}) async-start(), calls=%async_computation.24 | async-start | bytes 5013504 | tf_op jit(solution)/shard_map/all_gather | solution.py:129
  10.8 110.5 %all-gather.11.cloned.1.call-start = ((), (), s32[]{:S(2)}) async-start(), calls=%async_computation.9 | async-start | bytes 3612672 | tf_op jit(solution)/shard_map/all_gather | solution.py:219
  11.7 177.4 %copy-start.43 = (f32[768]{0:T(1024)}, f32[768]{0:T(1024)S(1)}, u32[]{:S(2)}) copy-start(f32[768]{0:T(1024)S(1)} %get-tuple-element.35) | copy-start | bytes 9220
  14.1 172.6 %reduce-scatter.10.cloned.1.call-start = ((), (), s32[]{:S(2)}) async-start(), calls=%async_computation.10 | async-start | bytes 3612672 | tf_op jit(solution)/shard_map/reduce_scatter | solution.py:222
  175.5 179.2 %all-gather.25.cloned.1.call-start = ((), (), s32[]{:S(2)}) async-start(), calls=%async_computation.25 | async-start | bytes 15040512 | tf_op jit(solution)/shard_map/all_gather | solution.py:129
  186.6 206.8 %all-gather.13.cloned.1.call-start = ((), (), s32[]{:S(2)}) async-start(), calls=%async_computation.11 | async-start | bytes 3612672 | tf_op jit(solution)/shard_map/all_gather | solution.py:219
  190.7 270.8 %reduce-scatter.12.cloned.1.call-start = ((), (), s32[]{:S(2)}) async-start(), calls=%async_computation.12 | async-start | bytes 3612672 | tf_op jit(solution)/shard_map/reduce_scatter | solution.py:222
  377.7 71.1 %copy-start.31 = (bf16[384,768]{1,0:T(8,128)(2,1)}, bf16[384,768]{1,0:T(8,128)(2,1)S(1)}, u32[]{:S(2)}) copy-start(bf16[384,768]{1,0:T(8,128)(2,1)S(1)} %reshape.329) | copy-start | bytes 1769476
  453.0 33.6 %all-gather.15.cloned.1.call-start = ((), (), s32[]{:S(2)}) async-start(), calls=%async_computation.13 | async-start | bytes 3612672 | tf_op jit(solution)/shard_map/all_gather | solution.py:219
  466.1 48.0 %all-gather.17.cloned.1.call-start = ((), (), s32[]{:S(2)}) async-start(), calls=%async_computation.15 | async-start | bytes 3612672 | tf_op jit(solution)/shard_map/all_gather | solution.py:219
  466.9 77.2 %reduce-scatter.16.cloned.1.call-start = ((), (), s32[]{:S(2)}) async-start(), calls=%async_computation.16 | async-start | bytes 3612672 | tf_op jit(solution)/shard_map/reduce_scatter | solution.py:222
  532.4 25.2 %reduce-scatter.14.cloned.1.call-start = ((), (), s32[]{:S(2)}) async-start(), calls=%async_computation.14 | async-start | bytes 3612672 | tf_op jit(solution)/shard_map/reduce_scatter | solution.py:222
  540.2 36.5 %all-gather.19.cloned.1.call-start = ((), (), s32[]{:S(2)}) async-start(), calls=%async_computation.17 | async-start | bytes 3612672 | tf_op jit(solution)/shard_map/all_gather | solution.py:219
  562.8 13.9 %copy-start.32 = (bf16[384,768]{1,0:T(8,128)(2,1)S(1)}, bf16[384,768]{1,0:T(8,128)(2,1)}, u32[]{:S(2)}) copy-start(bf16[384,768]{1,0:T(8,128)(2,1)} %copy-done.31) | copy-start | bytes 1769476
  564.2 165.2 %reduce-scatter.18.cloned.1.call-start = ((), (), s32[]{:S(2)}) async-start(), calls=%async_computation.18 | async-start | bytes 3612672 | tf_op jit(solution)/shard_map/reduce_scatter | solution.py:222
  639.5 129.7 %all-gather.21.cloned.1.call-start = ((), (), s32[]{:S(2)}) async-start(), calls=%async_computation.19 | async-start | bytes 3612672 | tf_op jit(solution)/shard_map/all_gather | solution.py:219
  736.4 157.9 %reduce-scatter.24.cloned.1.call-start = ((), (), s32[]{:S(2)}) async-start(), calls=%async_computation.22 | async-start | bytes 5013504 | tf_op jit(solution)/shard_map/reduce_scatter | solution.py:183
  745.5 325.0 %reduce-scatter.26.cloned.1.call-start = ((), (), s32[]{:S(2)}) async-start(), calls=%async_computation.23 | async-start | bytes 10027008 | tf_op jit(solution)/shard_map/reduce_scatter | solution.py:183
  763.2 318.7 %reduce-scatter.20.cloned.1.call-start = ((), (), s32[]{:S(2)}) async-start(), calls=%async_computation.20 | async-start | bytes 3612672 | tf_op jit(solution)/shard_map/reduce_scatter | solution.py:222
  868.6 358.0 %reduce-scatter.22.cloned.1.call-start = ((), (), s32[]{:S(2)}) async-start(), calls=%async_computation.21 | async-start | bytes 5013504 | tf_op jit(solution)/shard_map/reduce_scatter | solution.py:183
  877.4 204.4 %copy-start.38 = (f32[784]{0:T(1024)S(1)}, f32[784]{0:T(1024)}, u32[]{:S(2)}) copy-start(f32[784]{0:T(1024)} %copy-done.37) | copy-start | bytes 9412
  877.4 204.4 %copy-start.42 = (f32[768]{0:T(1024)S(1)}, f32[768]{0:T(1024)}, u32[]{:S(2)}) copy-start(f32[768]{0:T(1024)} %copy-done.41) | copy-start | bytes 9220
  897.8 186.1 %copy-start.51 = (f32[784]{0:T(1024)S(1)}, f32[784]{0:T(1024)}, u32[]{:S(2)}) copy-start(f32[784]{0:T(1024)} %copy-done.50) | copy-start | bytes 9412
  897.8 186.1 %copy-start.47 = (f32[784]{0:T(1024)S(1)}, f32[784]{0:T(1024)}, u32[]{:S(2)}) copy-start(f32[784]{0:T(1024)} %copy-done.46) | copy-start | bytes 9412
  (52 other events, 195.9 us)
Sparse Core Ops, SparseCore 0:
  11.4 82.5 all-gather.22
  96.0 9.6 all-gather.10
  175.7 8.8 reduce-scatter.9
  187.2 167.5 all-gather.24
  356.7 9.2 all-gather.12
  453.1 8.3 reduce-scatter.11
  466.3 12.3 all-gather.14
  480.2 12.1 all-gather.16
  532.5 11.4 reduce-scatter.15
  546.2 11.4 reduce-scatter.13
  564.4 12.3 all-gather.18
  639.6 11.3 reduce-scatter.17
  736.5 12.1 all-gather.20
  753.8 140.4 reduce-scatter.23
  899.8 170.6 reduce-scatter.25
  1072.6 9.2 reduce-scatter.19
  1086.9 139.6 reduce-scatter.21

commit v2 on v1

--- a/solution.py
+++ b/solution.py
@@ -175,7 +175,9 @@
             else:
                 rest.append(pos)
                 pos += 1
-        flat.append(jnp.transpose(parts, [dp_pos, ty_pos] + rest).reshape(ny * nd, -1))
+        flat.append(
+            jnp.transpose(parts, [dp_pos, ty_pos] + rest).reshape(ny * nd, -1).astype(jnp.bfloat16)
+        )
     sizes = [f.shape[1] for f in flat]
     stacked = jnp.concatenate(flat, axis=1)
     width = stacked.shape[1]
@@ -189,7 +191,7 @@
     out = []
     offset = 0
     for size, shard in zip(sizes, shard_shapes):
-        out.append(summed[offset : offset + size].reshape(shard))
+        out.append(summed[offset : offset + size].reshape(shard).astype(jnp.float32))
         offset += size
     return out
 
@@ -210,18 +212,18 @@
     up_layout = (0, 1)
     down_layout = (1, 0)
     time_qkv, time_proj = gather_weights((qkv_time, proj_time), (qkv_layout, proj_layout))
-    space_qkv, space_proj, up_full, down_full = gather_weights(
-        (qkv_space, proj_space, up_weight, down_weight),
-        (qkv_layout, proj_layout, up_layout, down_layout),
-    )
+    space_qkv, space_proj = gather_weights((qkv_space, proj_space), (qkv_layout, proj_layout))
+    up_full, down_full = gather_weights((up_weight, down_weight), (up_layout, down_layout))
+
+    def swap(values):
+        return lax.ppermute(values, "core", perm=[(0, 1), (1, 0)])
 
     def spread_rows(values):
-        return lax.all_gather(values, "core", axis=0, tiled=True)
+        return jnp.concatenate([values, swap(values)], axis=0)
 
     def sum_rows(values):
-        return lax.psum_scatter(
-            values.astype(jnp.bfloat16), "core", scatter_dimension=0, tiled=True
-        ).astype(jnp.float32)
+        half = values.shape[0] // 2
+        return values[:half] + swap(values[half:].astype(jnp.bfloat16)).astype(jnp.float32)
 
     spread_grads = spread_rows
     sum_grads = sum_rows

time: 1250 us -> 964 us (0.77)
  waiting for transfers between devices: 571 us -> 322 us
  local copies, waits for them, and re-layouts: 336 us -> 296 us
  other arithmetic: 87.1 us -> 105 us
    all_gather x2 -> x3, waiting for transfers between devices: 241 us -> 94.7 us  [gather_weights(): lax.all_gather(jnp.concatenate(flat, axis=1), WEIGHT_AXES, axis=0, tiled=...]
    reduce_scatter x3, waiting for transfers between devices: 286 us -> 225 us  [scatter_grads(): lax.psum_scatter(stacked.reshape(ny * nd * (width // lane), lane), WEIGHT...]
    reshape x13 -> x0, local copies, waits for them, and re-layouts: 44.1 us -> none  [the longest x5 25.6 us: scatter_grads(): jnp.transpose(parts, [dp_pos, ty_pos] + rest).reshape(ny * nd, -1)]
    convert_element_type x0 -> x19, local copies, waits for them, and re-layouts: none -> 41.3 us  [the longest x14 39.2 us: scatter_grads(): jnp.transpose(parts, [dp_pos, ty_pos] + rest).reshape(ny * nd, -1)]
    reduce_scatter x6 -> x0, waiting for transfers between devices: 31.2 us -> none  [sum_rows(): lax.psum_scatter(values.astype(jnp.bfloat16), 'core', scatter_dimension=0...]
    transpose x5 -> x0, local copies, waits for them, and re-layouts: 21.2 us -> none  [scatter_grads(): jnp.transpose(parts, [dp_pos, ty_pos] + rest).reshape(ny * nd, -1)]
    unnamed x131 -> x189, local copies, waits for them, and re-layouts: 57.3 us -> 58.6 us
  transfers between devices with their start and end apart: 17 -> 18, of which waited for: 10 -> 6; matrix products, arithmetic and copies ran while one was open for 31% -> 43% of each run, Pallas kernels for 0% -> 0%
where the time goes in v2:
time: 964 us; the launch traced here: 954 us
  waiting for transfers between devices  322 us (33%)
  local copies, waits for them, and re-layouts  296 us (31%)
  matrix products  173 us (18%)
  other arithmetic  105 us (11%)
  blocking collectives  38.9 us (4%)
  between operations  15.7 us (2%)
    reduce_scatter x3, waiting for transfers between devices, scatter_grads(): lax.psum_scatter(stacked.reshape(ny * nd * (width // lane), lane), WEIGHT...  225 us
    all_gather x3, waiting for transfers between devices, gather_weights(): lax.all_gather(jnp.concatenate(flat, axis=1), WEIGHT_AXES, axis=0, tiled=...  94.7 us
    unnamed x189, local copies, waits for them, and re-layouts  58.6 us
    convert_element_type x14, local copies, waits for them, and re-layouts, scatter_grads(): jnp.transpose(parts, [dp_pos, ty_pos] + rest).reshape(ny * nd, -1)  39.2 us
    psum x1, blocking collectives, per_device(): lax.psum(jnp.stack([gain_time, gain_space, gain_mlp]), ('dp', 'ty', 'core'))  38.9 us
    dot_general x1, matrix products, per_device(): jnp.dot(normed_mlp, up_full, preferred_element_type=jnp.float32)  27 us
    another operation x3, local copies, waits for them, and re-layouts, to_groups(): shaped = values.reshape((clip_count, FRAMES, PATCH) + trailing)  23.7 us
    reshape x8, local copies, waits for them, and re-layouts, gather_weights(): part = whole[:, offset:offset + size].reshape((nd, ny) + w.shape)  22.2 us
  transfers between devices with their start and end apart: 18, of which 6 were waited for; matrix products, arithmetic and copies ran while one was open for 43% of the time, Pallas kernels for 0%

profile of v2, /device:TPU:0, one launch (start us, length us, event | category | flops | bytes accessed | tf_op | source)
XLA Modules:
  0.0 953.9 jit_solution(14014961861470111191)
XLA Ops:
  18.0 75.9 %all-gather.7.cloned.1.call-done = bf16[16,1,73728]{2,1,0:T(2,128)(2,1)} async-done(((bf16[1,1,73728]{2,1,0:T(2,128)(2,1)}), bf16[16,1,73728]{2,1,0:T(2,128)(2,1)}) %all-gather.7.cloned.1.call-update) | async-done | bytes 2359312 | tf_op jit(solution)/shard_map/all_gather | solution.py:129
  115.8 7.5 convolution_convert_fusion.1
  123.3 11.9 %reshape.352 = bf16[1,8,196,3,6,64]{5,4,3,2,1,0:T(8,128)(2,1)} reshape(bf16[1568,1152]{1,0:T(8,128)(2,1)} %convolution_convert_fusion.1) | data formatting | bytes 7225344 | tf_op jit(solution)/shard_map/reshape;reshape | solution.py:27
  135.2 8.4 copy.158
  204.2 7.4 convolution_convert_fusion
  211.6 11.8 %reshape.353 = bf16[8,196,3,6,64]{4,3,2,1,0:T(8,128)(2,1)} reshape(bf16[1568,1152]{1,0:T(8,128)(2,1)} %convolution_convert_fusion) | data formatting | bytes 7225344 | tf_op jit(solution)/shard_map/reshape;reshape | solution.py:30
  283.4 15.7 %all-gather.11.cloned.1.call-done = bf16[16,1,147456]{2,1,0:T(2,128)(2,1)} async-done(((bf16[1,1,147456]{2,1,0:T(2,128)(2,1)}), bf16[16,1,147456]{2,1,0:T(2,128)(2,1)}) %all-gather.11.cloned.1.call-update) | async-done | bytes 4718608 | tf_op jit(solution)/shard_map/all_gather | solution.py:129
  299.1 9.8 %copy.159 = bf16[16,1,147456]{2,0,1:T(8,128)(2,1)S(1)} copy(bf16[16,1,147456]{2,1,0:T(2,128)(2,1)} %all-gather.11.cloned.1.call-done) | data formatting | bytes 9437184
  326.1 27.0 %multiply_convert_fusion.1 = (bf16[1568,1536]{1,0:T(8,128)(2,1)S(1)}, f32[1568,1536]{1,0:T(8,128)}, f32[1568,1536]{1,0:T(8,128)}) fusion(bf16[768,1536]{1,0:T(8,128)(2,1)S(1)} %bitcast.299, bf16[784,768]{1,0:T(8,128)(2,1)} %collective-permute-done.4, bf16[784,768]{1,0:T(8,128)(2,1)} %multiply_convert_fusion.5), kind=kOutput, calls=%fused_computation.8 | convolution fusion | flops 3860742144 | bytes 28852224 | tf_op jit(solution)/shard_map/dot_general | solution.py:243
  353.0 12.2 %add_convert_fusion = bf16[1568,1536]{1,0:T(8,128)(2,1)S(1)} fusion(f32[1568,1536]{1,0:T(8,128)} %get-tuple-element.43, bf16[1568,768]{1,0:T(8,128)(2,1)S(1)} %copy-done.51, bf16[1536,768]{0,1:T(8,128)(2,1)S(1)} %bitcast.297, f32[1568,1536]{1,0:T(8,128)} %get-tuple-element.60), kind=kOutput, calls=%fused_computation.7 | convolution fusion | flops 3733094400 | bytes 28852224 | tf_op jit(solution)/shard_map/dot_general | solution.py:252
  399.0 7.7 convolution_convert_fusion.3
  414.7 8.3 convolution_convert_fusion.2
  448.9 7.0 fusion.39
  455.9 7.4 multiply_reduce_fusion
  463.2 11.5 %multiply_convert_fusion = bf16[8,6,196,196]{2,3,1,0:T(8,128)(2,1)} fusion(f32[8,6,196,196]{2,3,1,0:T(8,128)} %get-tuple-element.62, f32[8,6,196,196]{2,3,1,0:T(8,128)} %copy-done, f32[8,6,196]{2,1,0:T(8,128)S(1)} %get-tuple-element.61, f32[8,6,196]{2,1,0:T(8,128)S(1)} %log_add_fusion.1), kind=kLoop, calls=%fused_computation.1 | loop fusion | flops 9219840 | bytes 18514944 | tf_op jit(solution)/shard_map/convert_element_type | solution.py:99
  504.0 9.0 convert_element_type.261
  513.0 7.8 fusion.89
  549.9 9.6 %pad_maximum_fusion = bf16[16,147456]{1,0:T(8,128)(2,1)} fusion(bf16[16,73728]{1,0:T(8,128)(2,1)S(1)} %copy-done.22, bf16[16,73728]{1,0:T(8,128)(2,1)S(1)} %bitcast.282), kind=kLoop, calls=%fused_computation.41 | loop fusion | flops 9437184 | bytes 9437184 | tf_op jit(solution)/shard_map/concatenate | solution.py:182
  584.3 7.3 multiply_reduce_fusion.2
  618.1 12.0 %copy.110 = bf16[1,8,196,3,6,64]{2,1,5,4,3,0:T(8,128)(2,1)} copy(bf16[1,8,196,3,6,64]{5,1,4,2,3,0:T(8,128)(2,1)} %maximum_bitcast_fusion) | data formatting | bytes 7225344 | tf_op jit(solution)/shard_map/transpose | solution.py:37
  630.1 9.0 reshape_reshape.40
  666.5 38.9 %psum.7 = f32[3,768]{1,0:T(4,128)} all-reduce(f32[3,768]{1,0:T(4,128)S(1)} %pad_maximum_fusion.14), channel_id=1, replica_groups=mesh['dp'=8,'ty'=2,'core'=2] {'dp','ty','core'}, use_global_device_ids=true, to_apply=%region_21.0 | all-reduce | flops 2304 | bytes 18432 | tf_op jit(solution)/shard_map/psum | solution.py:295
  715.5 95.1 %reduce-scatter.8.cloned.1.call-done = bf16[192,768]{1,0:T(8,128)(2,1)} async-done(((bf16[3072,768]{1,0:T(8,128)(2,1)}), bf16[192,768]{1,0:T(8,128)(2,1)}) %reduce-scatter.8.cloned.1.call-update) | async-done | bytes 294928 | tf_op jit(solution)/shard_map/reduce_scatter | solution.py:185
  813.5 130.0 %reduce-scatter.4.cloned.1.call-done = bf16[96,768]{1,0:T(8,128)(2,1)} async-done(((bf16[1536,768]{1,0:T(8,128)(2,1)}), bf16[96,768]{1,0:T(8,128)(2,1)}) %reduce-scatter.4.cloned.1.call-update) | async-done | bytes 147472 | tf_op jit(solution)/shard_map/reduce_scatter | solution.py:185
  (383 shorter events, 390.1 us)
Async XLA Ops:
  7.2 86.7 %all-gather.7.cloned.1.call-start = ((), (), s32[]{:S(2)}) async-start(), calls=%async_computation.6 | async-start | bytes 5013504 | tf_op jit(solution)/shard_map/all_gather | solution.py:129
  10.8 165.0 %all-gather.9.cloned.1.call-start = ((), (), s32[]{:S(2)}) async-start(), calls=%async_computation.7 | async-start | bytes 5013504 | tf_op jit(solution)/shard_map/all_gather | solution.py:129
  12.2 158.6 %copy-start.71 = (f32[768]{0:T(1024)}, f32[768]{0:T(1024)S(1)}, u32[]{:S(2)}) copy-start(f32[768]{0:T(1024)S(1)} %get-tuple-element.35) | copy-start | bytes 9220
  13.7 102.1 %collective-permute-start = (bf16[784,768]{1,0:T(8,128)(2,1)}, bf16[784,768]{1,0:T(8,128)(2,1)}, u32[]{:S(2)}, u32[]{:S(2)}) collective-permute-start(bf16[784,768]{1,0:T(8,128)(2,1)} %fusion.21), channel_id=1, source_target_pairs={{0,1},{1,0},{2,3},{3,2},{4,5},{5,4},{6,7},{7,6},{8,9},{9,8},{10,11... | collective-permute-start | bytes 3612680 | tf_op jit(solution)/shard_map/ppermute | solution.py:219
  15.8 283.3 %all-gather.11.cloned.1.call-start = ((), (), s32[]{:S(2)}) async-start(), calls=%async_computation.8 | async-start | bytes 10027008 | tf_op jit(solution)/shard_map/all_gather | solution.py:129
  162.3 5.2 collective-permute-start.1
  167.4 544.6 %reduce-scatter.6.cloned.1.call-start = ((), (), s32[]{:S(2)}) async-start(), calls=%async_computation.4 | async-start | bytes 2506752 | tf_op jit(solution)/shard_map/reduce_scatter | solution.py:185
  170.3 108.0 %copy-start.2 = (f32[784,768]{1,0:T(8,128)}, f32[784,768]{1,0:T(8,128)S(1)}, u32[]{:S(2)}) copy-start(f32[784,768]{1,0:T(8,128)S(1)} %get-tuple-element.47) | copy-start | bytes 7225348
  172.3 31.9 %collective-permute-start.2 = (bf16[784,768]{1,0:T(8,128)(2,1)}, bf16[784,768]{1,0:T(8,128)(2,1)}, u32[]{:S(2)}, u32[]{:S(2)}) collective-permute-start(bf16[784,768]{1,0:T(8,128)(2,1)} %multiply_convert_fusion.6), channel_id=1, source_target_pairs={{0,1},{1,0},{2,3},{3,2},{4,5},{5,4},{6,7},{7,6},{8,9},{9,8},{10,11... | collective-permute-start | bytes 3612680 | tf_op jit(solution)/shard_map/ppermute | solution.py:219
  172.3 103.7 %collective-permute-start.6 = (bf16[784,768]{1,0:T(8,128)(2,1)}, bf16[784,768]{1,0:T(8,128)(2,1)}, u32[]{:S(2)}, u32[]{:S(2)}) collective-permute-start(bf16[784,768]{1,0:T(8,128)(2,1)} %param.10), channel_id=1, source_target_pairs={{0,1},{1,0},{2,3},{3,2},{4,5},{5,4},{6,7},{7,6},{8,9},{9,8},{10,11... | collective-permute-start | bytes 3612680 | tf_op jit(solution)/shard_map/ppermute | solution.py:219
  188.5 71.3 %copy-start.44 = (bf16[384,768]{1,0:T(8,128)(2,1)}, bf16[384,768]{1,0:T(8,128)(2,1)S(1)}, u32[]{:S(2)}) copy-start(bf16[384,768]{1,0:T(8,128)(2,1)S(1)} %reshape.319) | copy-start | bytes 1769476
  265.9 12.5 %collective-permute-start.3 = (bf16[784,768]{1,0:T(8,128)(2,1)}, bf16[784,768]{1,0:T(8,128)(2,1)}, u32[]{:S(2)}, u32[]{:S(2)}) collective-permute-start(bf16[784,768]{1,0:T(8,128)(2,1)} %slice.245), channel_id=1, source_target_pairs={{0,1},{1,0},{2,3},{3,2},{4,5},{5,4},{6,7},{7,6},{8,9},{9,8},{10,11... | collective-permute-start | bytes 3612680 | tf_op jit(solution)/shard_map/ppermute | solution.py:219
  282.9 43.0 %collective-permute-start.4 = (bf16[784,768]{1,0:T(8,128)(2,1)}, bf16[784,768]{1,0:T(8,128)(2,1)}, u32[]{:S(2)}, u32[]{:S(2)}) collective-permute-start(bf16[784,768]{1,0:T(8,128)(2,1)} %multiply_convert_fusion.5), channel_id=1, source_target_pairs={{0,1},{1,0},{2,3},{3,2},{4,5},{5,4},{6,7},{7,6},{8,9},{9,8},{10,11... | collective-permute-start | bytes 3612680 | tf_op jit(solution)/shard_map/ppermute | solution.py:219
  326.1 27.0 %copy-start.51 = (bf16[1568,768]{1,0:T(8,128)(2,1)S(1)}, bf16[1568,768]{1,0:T(8,128)(2,1)}, u32[]{:S(2)}) copy-start(bf16[1568,768]{1,0:T(8,128)(2,1)} %constant_dynamic-update-slice_fusion) | copy-start | bytes 7225348
  353.0 17.7 %copy-start.80 = (bf16[1568,1536]{1,0:T(8,128)(2,1)}, bf16[1568,1536]{1,0:T(8,128)(2,1)S(1)}, u32[]{:S(2)}) copy-start(bf16[1568,1536]{1,0:T(8,128)(2,1)S(1)} %get-tuple-element.42) | copy-start | bytes 14450692
  370.7 15.6 %collective-permute-start.7 = (bf16[784,768]{1,0:T(8,128)(2,1)}, bf16[784,768]{1,0:T(8,128)(2,1)}, u32[]{:S(2)}, u32[]{:S(2)}) collective-permute-start(bf16[784,768]{1,0:T(8,128)(2,1)} %slice.243), channel_id=1, source_target_pairs={{0,1},{1,0},{2,3},{3,2},{4,5},{5,4},{6,7},{7,6},{8,9},{9,8},{10,11... | collective-permute-start | bytes 3612680 | tf_op jit(solution)/shard_map/ppermute | solution.py:219
  376.1 14.1 %collective-permute-start.5 = (bf16[784,768]{1,0:T(8,128)(2,1)}, bf16[784,768]{1,0:T(8,128)(2,1)}, u32[]{:S(2)}, u32[]{:S(2)}) collective-permute-start(bf16[784,768]{1,0:T(8,128)(2,1)} %slice.244), channel_id=1, source_target_pairs={{0,1},{1,0},{2,3},{3,2},{4,5},{5,4},{6,7},{7,6},{8,9},{9,8},{10,11... | collective-permute-start | bytes 3612680 | tf_op jit(solution)/shard_map/ppermute | solution.py:219
  398.4 40.2 %collective-permute-start.8 = (bf16[784,768]{1,0:T(8,128)(2,1)}, bf16[784,768]{1,0:T(8,128)(2,1)}, u32[]{:S(2)}, u32[]{:S(2)}) collective-permute-start(bf16[784,768]{1,0:T(8,128)(2,1)} %fusion.56), channel_id=1, source_target_pairs={{0,1},{1,0},{2,3},{3,2},{4,5},{5,4},{6,7},{7,6},{8,9},{9,8},{10,11... | collective-permute-start | bytes 3612680 | tf_op jit(solution)/shard_map/ppermute | solution.py:219
  534.7 5.3 collective-permute-start.9
  539.9 270.7 %reduce-scatter.8.cloned.1.call-start = ((), (), s32[]{:S(2)}) async-start(), calls=%async_computation.5 | async-start | bytes 5013504 | tf_op jit(solution)/shard_map/reduce_scatter | solution.py:185
  549.0 15.8 %collective-permute-start.10 = (bf16[784,768]{1,0:T(8,128)(2,1)S(1)}, bf16[784,768]{1,0:T(8,128)(2,1)}, u32[]{:S(2)}, u32[]{:S(2)}) collective-permute-start(bf16[784,768]{1,0:T(8,128)(2,1)S(1)} %fusion.75), channel_id=1, source_target_pairs={{0,1},{1,0},{2,3},{3,2},{4,5},{5,4},{6,7},{7,6},{8,9},{9,8},{10,11... | collective-permute-start | bytes 3612680 | tf_op jit(solution)/shard_map/ppermute | solution.py:219
  564.8 378.6 %reduce-scatter.4.cloned.1.call-start = ((), (), s32[]{:S(2)}) async-start(), calls=%async_computation.3 | async-start | bytes 2506752 | tf_op jit(solution)/shard_map/reduce_scatter | solution.py:185
  662.3 3.0 collective-permute-start.11
  662.9 42.6 %copy-start.74 = (f32[784]{0:T(1024)S(1)}, f32[784]{0:T(1024)}, u32[]{:S(2)}) copy-start(f32[784]{0:T(1024)} %copy-done.73) | copy-start | bytes 9412
  (81 other events, 362.6 us)
Sparse Core Ops, SparseCore 0:
  11.4 82.5 all-gather.6
  97.3 78.4 all-gather.8
  178.6 120.3 all-gather.10
  540.0 127.2 reduce-scatter.5
  672.4 138.2 reduce-scatter.7
  815.4 127.9 reduce-scatter.3

commit v3 on v2

--- a/solution.py
+++ b/solution.py
@@ -5,6 +5,7 @@
 import jax.numpy as jnp
 from jax import lax
 from jax.sharding import Mesh, PartitionSpec as P
+
 
 HD = 64
 FRAMES = 8
@@ -118,36 +119,37 @@
     return (grad_qkv, grad_proj, grad_normed)
 
 
-WEIGHT_AXES = ("dp", "ty")
+def swap_ty(values):
+    return lax.ppermute(values, "ty", perm=[(0, 1), (1, 0)])
 
 
 def gather_weights(shards, layouts):
+    assert lax.axis_size("ty") == 2
     flat = [w.astype(jnp.bfloat16).reshape(1, -1) for w in shards]
     sizes = [f.shape[1] for f in flat]
-    ny = lax.axis_size("ty")
     nd = lax.axis_size("dp")
-    whole = lax.all_gather(jnp.concatenate(flat, axis=1), WEIGHT_AXES, axis=0, tiled=True)
+    mine = lax.all_gather(jnp.concatenate(flat, axis=1), "dp", axis=0, tiled=True)
+    whole = jnp.stack([mine, swap_ty(mine)])
     out = []
     offset = 0
     for w, size, (dp_dim, ty_dim) in zip(shards, sizes, layouts):
-        part = whole[:, offset : offset + size].reshape((nd, ny) + w.shape)
+        part = whole[:, :, offset : offset + size].reshape((2, nd) + w.shape)
         offset += size
         order = []
         for dim in range(w.ndim):
             if dim == dp_dim:
+                order.append(1)
+            if dim == ty_dim:
                 order.append(0)
-            if dim == ty_dim:
-                order.append(1)
             order.append(dim + 2)
         shape = list(w.shape)
         shape[dp_dim] *= nd
-        shape[ty_dim] *= ny
+        shape[ty_dim] *= 2
         out.append(jnp.transpose(part, order).reshape(shape))
     return out
 
 
 def scatter_grads(grads, layouts, shard_shapes):
-    ny = lax.axis_size("ty")
     nd = lax.axis_size("dp")
     flat = []
     for g, (dp_dim, ty_dim), shard in zip(grads, layouts, shard_shapes):
@@ -156,7 +158,7 @@
             if dim == dp_dim:
                 split.extend([nd, shard[dim]])
             elif dim == ty_dim:
-                split.extend([ny, shard[dim]])
+                split.extend([2, shard[dim]])
             else:
                 split.append(shard[dim])
         parts = g.reshape(split)
@@ -175,18 +177,14 @@
             else:
                 rest.append(pos)
                 pos += 1
-        flat.append(
-            jnp.transpose(parts, [dp_pos, ty_pos] + rest).reshape(ny * nd, -1).astype(jnp.bfloat16)
-        )
-    sizes = [f.shape[1] for f in flat]
-    stacked = jnp.concatenate(flat, axis=1)
-    width = stacked.shape[1]
+        flat.append(jnp.transpose(parts, [ty_pos, dp_pos] + rest).reshape(2, nd, -1))
+    sizes = [f.shape[2] for f in flat]
+    stacked = jnp.concatenate(flat, axis=2)
+    own = stacked[0] + swap_ty(stacked[1].astype(jnp.bfloat16)).astype(jnp.float32)
+    width = own.shape[1]
     lane = 768 if width % 768 == 0 else width
     summed = lax.psum_scatter(
-        stacked.reshape(ny * nd * (width // lane), lane),
-        WEIGHT_AXES,
-        scatter_dimension=0,
-        tiled=True,
+        own.astype(jnp.bfloat16).reshape(-1, lane), "dp", scatter_dimension=0, tiled=True
     ).reshape(-1)
     out = []
     offset = 0

time: 964 us -> 896 us (0.929)
  waiting for transfers between devices: 322 us -> 212 us
  local copies, waits for them, and re-layouts: 296 us -> 326 us
    reduce_scatter x3, waiting for transfers between devices: 225 us -> 53.1 us  [scatter_grads(): lax.psum_scatter(own.astype(jnp.bfloat16).reshape(-1, lane), 'dp', scatte...]
    ppermute x0 -> x6, waiting for transfers between devices: none -> 66.8 us  [swap_ty(): return lax.ppermute(values, 'ty', perm=[(0, 1), (1, 0)])]
    reshape x11 -> x20, local copies, waits for them, and re-layouts: 33.3 us -> 79.4 us  [the longest x6 30.6 us: scatter_grads(): jnp.transpose(parts, [ty_pos, dp_pos] + rest).reshape(2, nd, -1)]
    convert_element_type x14 -> x3, local copies, waits for them, and re-layouts: 39.2 us -> 2.99 us  [scatter_grads(): stacked[1].astype(jnp.bfloat16)]
    transpose x0 -> x3, local copies, waits for them, and re-layouts: none -> 19.7 us  [scatter_grads(): jnp.transpose(parts, [ty_pos, dp_pos] + rest).reshape(2, nd, -1)]
    concatenate x3 -> x0, other arithmetic: 13 us -> none  [scatter_grads(): stacked = jnp.concatenate(flat, axis=1)]
    another operation x0 -> x5, other arithmetic: none -> 9.67 us  [gather_weights(): whole = jnp.stack([mine, swap_ty(mine)])]
    unnamed x189 -> x190, local copies, waits for them, and re-layouts: 58.6 us -> 56.8 us
  transfers between devices with their start and end apart: 18 -> 24, of which waited for: 6 -> 8; matrix products, arithmetic and copies ran while one was open for 43% -> 60% of each run, Pallas kernels for 0% -> 0%
where the time goes in v3:
time: 896 us; the launch traced here: 886 us
  local copies, waits for them, and re-layouts  326 us (36%)
  waiting for transfers between devices  212 us (24%)
  matrix products  179 us (20%)
  other arithmetic  102 us (11%)
  blocking collectives  40.2 us (4%)
  between operations  15.8 us (2%)
  starting transfers between devices  10.8 us (1%)
    all_gather x3, waiting for transfers between devices, gather_weights(): lax.all_gather(jnp.concatenate(flat, axis=1), 'dp', axis=0, tiled=True)  90.6 us
    ppermute x6, waiting for transfers between devices, swap_ty(): return lax.ppermute(values, 'ty', perm=[(0, 1), (1, 0)])  66.8 us
    unnamed x190, local copies, waits for them, and re-layouts  56.8 us
    reduce_scatter x3, waiting for transfers between devices, scatter_grads(): lax.psum_scatter(own.astype(jnp.bfloat16).reshape(-1, lane), 'dp', scatte...  53.1 us
    psum x1, blocking collectives, per_device(): lax.psum(jnp.stack([gain_time, gain_space, gain_mlp]), ('dp', 'ty', 'core'))  40.2 us
    reshape x6, local copies, waits for them, and re-layouts, scatter_grads(): jnp.transpose(parts, [ty_pos, dp_pos] + rest).reshape(2, nd, -1)  30.6 us
    dot_general x1, matrix products, per_device(): jnp.dot(normed_mlp, up_full, preferred_element_type=jnp.float32)  26.7 us
    another operation x3, local copies, waits for them, and re-layouts, to_groups(): shaped = values.reshape((clip_count, FRAMES, PATCH) + trailing)  23.7 us
  transfers between devices with their start and end apart: 24, of which 8 were waited for; matrix products, arithmetic and copies ran while one was open for 60% of the time, Pallas kernels for 0%

profile of v3, /device:TPU:0, one launch (start us, length us, event | category | flops | bytes accessed | tf_op | source)
XLA Modules:
  0.0 886.1 jit_solution(12133834910805040095)
XLA Ops:
  16.6 48.8 %all-gather.7.cloned.1.call-done = bf16[8,1,73728]{2,1,0:T(2,128)(2,1)} async-done(((bf16[1,1,73728]{2,1,0:T(2,128)(2,1)}), bf16[8,1,73728]{2,1,0:T(2,128)(2,1)}) %all-gather.7.cloned.1.call-update) | async-done | bytes 1179664 | tf_op jit(solution)/shard_map/all_gather | solution.py:131
  76.8 41.8 %all-gather.9.cloned.1.call-done = bf16[8,1,73728]{2,1,0:T(2,128)(2,1)} async-done(((bf16[1,1,73728]{2,1,0:T(2,128)(2,1)}), bf16[8,1,73728]{2,1,0:T(2,128)(2,1)}) %all-gather.9.cloned.1.call-update) | async-done | bytes 1179664 | tf_op jit(solution)/shard_map/all_gather | solution.py:131
  140.5 7.4 convolution_convert_fusion.1
  147.8 11.9 %reshape.374 = bf16[1,8,196,3,6,64]{5,4,3,2,1,0:T(8,128)(2,1)} reshape(bf16[1568,1152]{1,0:T(8,128)(2,1)} %convolution_convert_fusion.1) | data formatting | bytes 7225344 | tf_op jit(solution)/shard_map/reshape;reshape | solution.py:28
  159.8 8.4 copy.160
  218.0 7.3 convolution_convert_fusion
  225.3 11.7 %reshape.375 = bf16[8,196,3,6,64]{4,3,2,1,0:T(8,128)(2,1)} reshape(bf16[1568,1152]{1,0:T(8,128)(2,1)} %convolution_convert_fusion) | data formatting | bytes 7225344 | tf_op jit(solution)/shard_map/reshape;reshape | solution.py:31
  311.6 36.2 %collective-permute-done.7 = bf16[8,147456]{1,0:T(8,128)(2,1)} collective-permute-done((bf16[8,147456]{1,0:T(8,128)(2,1)}, bf16[8,147456]{1,0:T(8,128)(2,1)}, u32[]{:S(2)}, u32[]{:S(2)}) %collective-permute-start.7) | collective-permute-done | bytes 2359328 | tf_op jit(solution)/shard_map/ppermute | solution.py:123
  366.2 26.7 %multiply_convert_fusion.1 = (bf16[1568,1536]{1,0:T(8,128)(2,1)S(1)}, f32[1568,1536]{1,0:T(8,128)}, f32[1568,1536]{1,0:T(8,128)}) fusion(bf16[768,1536]{1,0:T(8,128)(2,1)S(1)} %bitcast.337, bf16[784,768]{1,0:T(8,128)(2,1)} %collective-permute-done.6, bf16[784,768]{1,0:T(8,128)(2,1)} %multiply_convert_fusion.5), kind=kOutput, calls=%fused_computation.8 | convolution fusion | flops 3860742144 | bytes 28852224 | tf_op jit(solution)/shard_map/dot_general | solution.py:241
  392.9 8.0 fusion.101
  415.9 7.9 copy.117
  430.6 12.8 %add_convert_fusion = bf16[1568,1536]{1,0:T(8,128)(2,1)S(1)} fusion(f32[1568,1536]{1,0:T(8,128)} %get-tuple-element.43, bf16[1568,768]{1,0:T(8,128)(2,1)} %constant_dynamic-update-slice_fusion, bf16[1536,768]{0,1:T(8,128)(2,1)} %bitcast.340, f32[1568,1536]{1,0:T(8,128)} %get-tuple-element.66), kind=kOutput, calls=%fused_computation.7 | convolution fusion | flops 3733094400 | bytes 28852224 | tf_op jit(solution)/shard_map/dot_general | solution.py:250
  449.0 7.9 fusion.63
  507.1 7.5 fusion.47
  514.6 7.4 multiply_reduce_fusion
  521.9 11.4 %multiply_convert_fusion = bf16[8,6,196,196]{2,3,1,0:T(8,128)(2,1)} fusion(f32[8,6,196,196]{2,3,1,0:T(8,128)} %get-tuple-element.68, f32[8,6,196,196]{2,3,1,0:T(8,128)} %copy-done, f32[8,6,196]{2,1,0:T(8,128)S(1)} %get-tuple-element.67, f32[8,6,196]{2,1,0:T(8,128)S(1)} %copy-done.43), kind=kLoop, calls=%fused_computation.1 | loop fusion | flops 9219840 | bytes 18514944 | tf_op jit(solution)/shard_map/convert_element_type | solution.py:100
  564.4 9.0 %convert_element_type.231 = bf16[1568,1152]{0,1:T(8,128)(2,1)} reshape(bf16[8,196,3,6,64]{1,0,4,3,2:T(8,128)(2,1)} %copy.103) | data formatting | bytes 7225344 | tf_op jit(solution)/shard_map/convert_element_type | solution.py:109
  573.4 8.3 fusion.99
  614.1 18.0 %collective-permute-done.16 = bf16[8,73728]{1,0:T(8,128)(2,1)S(1)} collective-permute-done((bf16[8,73728]{1,0:T(8,128)(2,1)S(1)}, bf16[8,73728]{1,0:T(8,128)(2,1)S(1)}, u32[]{:S(2)}, u32[]{:S(2)}) %collective-permute-start.16) | collective-permute-done | bytes 1179680 | tf_op jit(solution)/shard_map/ppermute | solution.py:123
  689.7 12.1 %copy.108 = bf16[1,8,196,3,6,64]{2,1,5,4,3,0:T(8,128)(2,1)} copy(bf16[1,8,196,3,6,64]{5,1,4,2,3,0:T(8,128)(2,1)} %maximum_bitcast_fusion) | data formatting | bytes 7225344 | tf_op jit(solution)/shard_map/transpose | solution.py:38
  701.7 9.0 %reshape_reshape.40 = bf16[1568,1152]{0,1:T(8,128)(2,1)} reshape(bf16[1,8,196,3,6,64]{2,1,5,4,3,0:T(8,128)(2,1)} %copy.108) | data formatting | bytes 7225344 | tf_op jit(solution)/shard_map/reshape;reshape | solution.py:110
  748.2 12.6 %collective-permute-done.15 = bf16[8,73728]{1,0:T(8,128)(2,1)} collective-permute-done((bf16[8,73728]{1,0:T(8,128)(2,1)}, bf16[8,73728]{1,0:T(8,128)(2,1)}, u32[]{:S(2)}, u32[]{:S(2)}) %collective-permute-start.15) | collective-permute-done | bytes 1179680 | tf_op jit(solution)/shard_map/ppermute | solution.py:123
  772.8 40.2 %psum.7 = f32[3,768]{1,0:T(4,128)} all-reduce(f32[3,768]{1,0:T(4,128)S(1)} %pad_maximum_fusion.14), channel_id=1, replica_groups=mesh['dp'=8,'ty'=2,'core'=2] {'dp','ty','core'}, use_global_device_ids=true, to_apply=%region_21.0 | all-reduce | flops 2304 | bytes 18432 | tf_op jit(solution)/shard_map/psum | solution.py:293
  822.5 53.1 %reduce-scatter.4.cloned.1.call-done = bf16[96,768]{1,0:T(8,128)(2,1)} async-done(((bf16[768,768]{1,0:T(8,128)(2,1)}), bf16[96,768]{1,0:T(8,128)(2,1)}) %reduce-scatter.4.cloned.1.call-update) | async-done | bytes 147472 | tf_op jit(solution)/shard_map/reduce_scatter | solution.py:186
  (404 shorter events, 444.9 us)
Async XLA Ops:
  7.2 58.3 %all-gather.7.cloned.1.call-start = ((), (), s32[]{:S(2)}) async-start(), calls=%async_computation.6 | async-start | bytes 2654208 | tf_op jit(solution)/shard_map/all_gather | solution.py:131
  10.8 107.8 %all-gather.9.cloned.1.call-start = ((), (), s32[]{:S(2)}) async-start(), calls=%async_computation.7 | async-start | bytes 2654208 | tf_op jit(solution)/shard_map/all_gather | solution.py:131
  13.7 126.8 %collective-permute-start = (bf16[784,768]{1,0:T(8,128)(2,1)}, bf16[784,768]{1,0:T(8,128)(2,1)}, u32[]{:S(2)}, u32[]{:S(2)}) collective-permute-start(bf16[784,768]{1,0:T(8,128)(2,1)} %fusion.23), channel_id=1, source_target_pairs={{0,1},{1,0},{2,3},{3,2},{4,5},{5,4},{6,7},{7,6},{8,9},{9,8},{10,11... | collective-permute-start | bytes 3612680 | tf_op jit(solution)/shard_map/ppermute | solution.py:217
  14.2 280.2 %collective-permute-start.9 = (bf16[784,768]{1,0:T(8,128)(2,1)}, bf16[784,768]{1,0:T(8,128)(2,1)}, u32[]{:S(2)}, u32[]{:S(2)}) collective-permute-start(bf16[784,768]{1,0:T(8,128)(2,1)} %param.10), channel_id=1, source_target_pairs={{0,1},{1,0},{2,3},{3,2},{4,5},{5,4},{6,7},{7,6},{8,9},{9,8},{10,11... | collective-permute-start | bytes 3612680 | tf_op jit(solution)/shard_map/ppermute | solution.py:217
  15.8 271.5 %all-gather.11.cloned.1.call-start = ((), (), s32[]{:S(2)}) async-start(), calls=%async_computation.8 | async-start | bytes 5308416 | tf_op jit(solution)/shard_map/all_gather | solution.py:131
  68.4 55.6 %collective-permute-start.1 = (bf16[8,73728]{1,0:T(8,128)(2,1)S(1)}, bf16[8,73728]{1,0:T(8,128)(2,1)S(1)}, u32[]{:S(2)}, u32[]{:S(2)}) collective-permute-start(bf16[8,73728]{1,0:T(8,128)(2,1)S(1)} %bitcast.312), channel_id=1, source_target_pairs={{0,2},{2,0},{1,3},{3,1},{4,6},{6,4},{5,7},{7,5},{8,10},{10,8},{9,1... | collective-permute-start | bytes 3538952 | tf_op jit(solution)/shard_map/ppermute | solution.py:123
  74.2 692.3 %reduce-scatter.6.cloned.1.call-start = ((), (), s32[]{:S(2)}) async-start(), calls=%async_computation.4 | async-start | bytes 1327104 | tf_op jit(solution)/shard_map/reduce_scatter | solution.py:186
  122.6 64.6 %collective-permute-start.4 = (bf16[8,73728]{1,0:T(8,128)(2,1)}, bf16[8,73728]{1,0:T(8,128)(2,1)}, u32[]{:S(2)}, u32[]{:S(2)}) collective-permute-start(bf16[8,73728]{1,0:T(8,128)(2,1)} %bitcast.292), channel_id=1, source_target_pairs={{0,2},{2,0},{1,3},{3,1},{4,6},{6,4},{5,7},{7,5},{8,10},{10,8},{9,1... | collective-permute-start | bytes 3538952 | tf_op jit(solution)/shard_map/ppermute | solution.py:123
  187.1 3.0 collective-permute-start.2
  192.5 25.5 %collective-permute-start.3 = (bf16[784,768]{1,0:T(8,128)(2,1)}, bf16[784,768]{1,0:T(8,128)(2,1)}, u32[]{:S(2)}, u32[]{:S(2)}) collective-permute-start(bf16[784,768]{1,0:T(8,128)(2,1)} %multiply_convert_fusion.6), channel_id=1, source_target_pairs={{0,1},{1,0},{2,3},{3,2},{4,5},{5,4},{6,7},{7,6},{8,9},{9,8},{10,11... | collective-permute-start | bytes 3612680 | tf_op jit(solution)/shard_map/ppermute | solution.py:217
  279.5 26.7 %collective-permute-start.5 = (bf16[784,768]{1,0:T(8,128)(2,1)}, bf16[784,768]{1,0:T(8,128)(2,1)}, u32[]{:S(2)}, u32[]{:S(2)}) collective-permute-start(bf16[784,768]{1,0:T(8,128)(2,1)} %slice.320), channel_id=1, source_target_pairs={{0,1},{1,0},{2,3},{3,2},{4,5},{5,4},{6,7},{7,6},{8,9},{9,8},{10,11... | collective-permute-start | bytes 3612680 | tf_op jit(solution)/shard_map/ppermute | solution.py:217
  293.9 53.9 %collective-permute-start.7 = (bf16[8,147456]{1,0:T(8,128)(2,1)}, bf16[8,147456]{1,0:T(8,128)(2,1)}, u32[]{:S(2)}, u32[]{:S(2)}) collective-permute-start(bf16[8,147456]{1,0:T(8,128)(2,1)} %bitcast.289), channel_id=1, source_target_pairs={{0,2},{2,0},{1,3},{3,1},{4,6},{6,4},{5,7},{7,5},{8,10},{10,8},{9,1... | collective-permute-start | bytes 7077896 | tf_op jit(solution)/shard_map/ppermute | solution.py:123
  311.4 54.6 %collective-permute-start.6 = (bf16[784,768]{1,0:T(8,128)(2,1)}, bf16[784,768]{1,0:T(8,128)(2,1)}, u32[]{:S(2)}, u32[]{:S(2)}) collective-permute-start(bf16[784,768]{1,0:T(8,128)(2,1)} %multiply_convert_fusion.5), channel_id=1, source_target_pairs={{0,1},{1,0},{2,3},{3,2},{4,5},{5,4},{6,7},{7,6},{8,9},{9,8},{10,11... | collective-permute-start | bytes 3612680 | tf_op jit(solution)/shard_map/ppermute | solution.py:217
  415.9 67.7 %collective-permute-start.8 = (bf16[784,768]{1,0:T(8,128)(2,1)}, bf16[784,768]{1,0:T(8,128)(2,1)}, u32[]{:S(2)}, u32[]{:S(2)}) collective-permute-start(bf16[784,768]{1,0:T(8,128)(2,1)} %slice.319), channel_id=1, source_target_pairs={{0,1},{1,0},{2,3},{3,2},{4,5},{5,4},{6,7},{7,6},{8,9},{9,8},{10,11... | collective-permute-start | bytes 3612680 | tf_op jit(solution)/shard_map/ppermute | solution.py:217
  474.8 3.9 collective-permute-start.10
  490.5 3.8 collective-permute-start.11
  493.5 241.3 %collective-permute-start.17 = (bf16[8,147456]{1,0:T(8,128)(2,1)}, bf16[8,147456]{1,0:T(8,128)(2,1)}, u32[]{:S(2)}, u32[]{:S(2)}) collective-permute-start(bf16[8,147456]{1,0:T(8,128)(2,1)} %fusion.38), channel_id=1, source_target_pairs={{0,2},{2,0},{1,3},{3,1},{4,6},{6,4},{5,7},{7,5},{8,10},{10,8},{9,1... | collective-permute-start | bytes 7077896 | tf_op jit(solution)/shard_map/ppermute | solution.py:123
  603.3 3.0 collective-permute-start.12
  604.0 28.1 %collective-permute-start.16 = (bf16[8,73728]{1,0:T(8,128)(2,1)S(1)}, bf16[8,73728]{1,0:T(8,128)(2,1)S(1)}, u32[]{:S(2)}, u32[]{:S(2)}) collective-permute-start(bf16[8,73728]{1,0:T(8,128)(2,1)S(1)} %fusion.72), channel_id=1, source_target_pairs={{0,2},{2,0},{1,3},{3,1},{4,6},{6,4},{5,7},{7,5},{8,10},{10,8},{9,1... | collective-permute-start | bytes 3538952 | tf_op jit(solution)/shard_map/ppermute | solution.py:123
  613.7 20.2 %collective-permute-start.13 = (bf16[784,768]{1,0:T(8,128)(2,1)}, bf16[784,768]{1,0:T(8,128)(2,1)}, u32[]{:S(2)}, u32[]{:S(2)}) collective-permute-start(bf16[784,768]{1,0:T(8,128)(2,1)} %fusion.86), channel_id=1, source_target_pairs={{0,1},{1,0},{2,3},{3,2},{4,5},{5,4},{6,7},{7,6},{8,9},{9,8},{10,11... | collective-permute-start | bytes 3612680 | tf_op jit(solution)/shard_map/ppermute | solution.py:217
  633.9 185.7 %reduce-scatter.8.cloned.1.call-start = ((), (), s32[]{:S(2)}) async-start(), calls=%async_computation.5 | async-start | bytes 2654208 | tf_op jit(solution)/shard_map/reduce_scatter | solution.py:186
  733.5 27.3 %collective-permute-start.15 = (bf16[8,73728]{1,0:T(8,128)(2,1)}, bf16[8,73728]{1,0:T(8,128)(2,1)}, u32[]{:S(2)}, u32[]{:S(2)}) collective-permute-start(bf16[8,73728]{1,0:T(8,128)(2,1)} %fusion.71), channel_id=1, source_target_pairs={{0,2},{2,0},{1,3},{3,1},{4,6},{6,4},{5,7},{7,5},{8,10},{10,8},{9,1... | collective-permute-start | bytes 3538952 | tf_op jit(solution)/shard_map/ppermute | solution.py:123
  740.6 134.9 %reduce-scatter.4.cloned.1.call-start = ((), (), s32[]{:S(2)}) async-start(), calls=%async_computation.3 | async-start | bytes 1327104 | tf_op jit(solution)/shard_map/reduce_scatter | solution.py:186
  748.2 21.7 %collective-permute-start.14 = (bf16[784,768]{1,0:T(8,128)(2,1)}, bf16[784,768]{1,0:T(8,128)(2,1)S(1)}, u32[]{:S(2)}, u32[]{:S(2)}) collective-permute-start(bf16[784,768]{1,0:T(8,128)(2,1)} %slice.316), channel_id=1, source_target_pairs={{0,1},{1,0},{2,3},{3,2},{4,5},{5,4},{6,7},{7,6},{8,9},{9,8},{10,11... | collective-permute-start | bytes 3612680 | tf_op jit(solution)/shard_map/ppermute | solution.py:217
  (87 other events, 1242.5 us)
Sparse Core Ops, SparseCore 0:
  10.9 54.5 all-gather.6
  68.2 50.3 all-gather.8
  120.8 77.8 all-gather.10
  634.0 63.1 reduce-scatter.5
  740.7 67.7 reduce-scatter.7
  811.7 63.7 reduce-scatter.3

commit v4 on v2

--- a/solution.py
+++ b/solution.py
@@ -5,6 +5,7 @@
 import jax.numpy as jnp
 from jax import lax
 from jax.sharding import Mesh, PartitionSpec as P
+
 
 HD = 64
 FRAMES = 8
@@ -149,6 +150,7 @@
 def scatter_grads(grads, layouts, shard_shapes):
     ny = lax.axis_size("ty")
     nd = lax.axis_size("dp")
+    assert ny == 2
     flat = []
     for g, (dp_dim, ty_dim), shard in zip(grads, layouts, shard_shapes):
         split = []
@@ -176,24 +178,35 @@
                 rest.append(pos)
                 pos += 1
         flat.append(
-            jnp.transpose(parts, [dp_pos, ty_pos] + rest).reshape(ny * nd, -1).astype(jnp.bfloat16)
+            jnp.transpose(parts, [dp_pos, ty_pos] + rest)
+            .reshape(nd, ny, -1)
+            .astype(jnp.bfloat16)
         )
-    sizes = [f.shape[1] for f in flat]
-    stacked = jnp.concatenate(flat, axis=1)
-    width = stacked.shape[1]
+    sizes = [f.shape[2] for f in flat]
+    stacked = jnp.concatenate(flat, axis=2)
+    width = stacked.shape[2]
     lane = 768 if width % 768 == 0 else width
-    summed = lax.psum_scatter(
-        stacked.reshape(ny * nd * (width // lane), lane),
-        WEIGHT_AXES,
-        scatter_dimension=0,
-        tiled=True,
-    ).reshape(-1)
+    blocks = lax.psum_scatter(
+        stacked.reshape(-1, lane), "dp", scatter_dimension=0, tiled=True
+    ).reshape(ny, width)
+    return blocks, sizes, shard_shapes
+
+
+def finish_grads(blocks, sizes, shard_shapes):
+    here = lax.axis_index("ty")
+    own = lax.dynamic_index_in_dim(blocks, here, axis=0, keepdims=False)
+    other = lax.dynamic_index_in_dim(blocks, 1 - here, axis=0, keepdims=False)
+    summed = own.astype(jnp.float32) + swap_ty(other).astype(jnp.float32)
     out = []
     offset = 0
     for size, shard in zip(sizes, shard_shapes):
-        out.append(summed[offset : offset + size].reshape(shard).astype(jnp.float32))
+        out.append(summed[offset : offset + size].reshape(shard))
         offset += size
     return out
+
+
+def swap_ty(values):
+    return lax.ppermute(values, "ty", perm=[(0, 1), (1, 0)])
 
 
 def per_device(
@@ -253,9 +266,10 @@
     _, gelu_back = jax.vjp(partial(jax.nn.gelu, approximate=False), hidden_pre)
     grad_pre = gelu_back(grad_hidden)[0].astype(jnp.bfloat16)
     grad_up = jnp.dot(normed_mlp.T, grad_pre, preferred_element_type=jnp.float32)
-    grad_up, grad_down = scatter_grads(
+    mlp_blocks = scatter_grads(
         (grad_up, grad_down), (up_layout, down_layout), (up_weight.shape, down_weight.shape)
     )
+    grad_up, grad_down = finish_grads(*mlp_blocks)
     _, norm_back = jax.vjp(normalize, after_space, norm_gains[2])
     back_rows, gain_mlp = norm_back(
         sum_grads(jnp.dot(grad_pre, up_full.T, preferred_element_type=jnp.float32))
@@ -273,21 +287,24 @@
         space_rows,
         False,
     )
-    grad_qkv_space, grad_proj_space = scatter_grads(
+    space_blocks = scatter_grads(
         (grad_qkv_space, grad_proj_space),
         (qkv_layout, proj_layout),
         (qkv_space.shape, proj_space.shape),
     )
+    grad_qkv_space, grad_proj_space = finish_grads(*space_blocks)
     back_rows, gain_space = norm_back(sum_grads(grad_normed))
     grad_after = grad_after + back_rows
     time_rows = spread_grads(grad_after.astype(jnp.bfloat16))
     grad_qkv_time, grad_proj_time, grad_normed = attend_backward(
         normed_time, time_qkv, time_proj, grouped_time, summary_time, merged_time, time_rows, True
     )
-    grad_qkv_time, grad_proj_time = scatter_grads(
-        (grad_qkv_time, grad_proj_time),
-        (qkv_layout, proj_layout),
-        (qkv_time.shape, proj_time.shape),
+    grad_qkv_time, grad_proj_time = finish_grads(
+        *scatter_grads(
+            (grad_qkv_time, grad_proj_time),
+            (qkv_layout, proj_layout),
+            (qkv_time.shape, proj_time.shape),
+        )
     )
     _, norm_back = jax.vjp(normalize, inputs, norm_gains[0])
     back_rows, gain_time = norm_back(sum_grads(grad_normed))

time: 964 us -> 850 us (0.88)
  waiting for transfers between devices: 322 us -> 178 us
  local copies, waits for them, and re-layouts: 296 us -> 321 us
    reduce_scatter x3, waiting for transfers between devices: 225 us -> 75 us  [scatter_grads(): lax.psum_scatter(stacked.reshape(-1, lane), 'dp', scatter_dimension=0, ti...]
    concatenate x0 -> x3, local copies, waits for them, and re-layouts: none -> 9.68 us  [scatter_grads(): stacked = jnp.concatenate(flat, axis=2)]
    unnamed x189 -> x184, local copies, waits for them, and re-layouts: 58.6 us -> 63.6 us
    convert_element_type x19 -> x12, local copies, waits for them, and re-layouts: 41.3 us -> 42.6 us  [scatter_grads(): flat.append(jnp.transpose(parts, [dp_pos, ty_pos] + rest).reshape(nd, ny,...]
  transfers between devices with their start and end apart: 18 -> 21, of which waited for: 6 -> 6; matrix products, arithmetic and copies ran while one was open for 43% -> 52% of each run, Pallas kernels for 0% -> 0%
where the time goes in v4:
time: 850 us; the launch traced here: 840 us
  local copies, waits for them, and re-layouts  321 us (38%)
  waiting for transfers between devices  178 us (21%)
  matrix products  173 us (20%)
  other arithmetic  102 us (12%)
  blocking collectives  39.6 us (5%)
  between operations  16 us (2%)
  starting transfers between devices  9.59 us (1%)
    all_gather x3, waiting for transfers between devices, gather_weights(): lax.all_gather(jnp.concatenate(flat, axis=1), WEIGHT_AXES, axis=0, tiled=...  94.8 us
    reduce_scatter x3, waiting for transfers between devices, scatter_grads(): lax.psum_scatter(stacked.reshape(-1, lane), 'dp', scatter_dimension=0, ti...  75 us
    unnamed x184, local copies, waits for them, and re-layouts  63.6 us
    convert_element_type x12, local copies, waits for them, and re-layouts, scatter_grads(): flat.append(jnp.transpose(parts, [dp_pos, ty_pos] + rest).reshape(nd, ny,...  42.6 us
    psum x1, blocking collectives, per_device(): lax.psum(jnp.stack([gain_time, gain_space, gain_mlp]), ('dp', 'ty', 'core'))  39.6 us
    dot_general x1, matrix products, per_device(): jnp.dot(normed_mlp, up_full, preferred_element_type=jnp.float32)  27 us
    another operation x3, local copies, waits for them, and re-layouts, to_groups(): shaped = values.reshape((clip_count, FRAMES, PATCH) + trailing)  23.7 us
    reshape x8, local copies, waits for them, and re-layouts, gather_weights(): part = whole[:, offset:offset + size].reshape((nd, ny) + w.shape)  22.2 us
  transfers between devices with their start and end apart: 21, of which 6 were waited for; matrix products, arithmetic and copies ran while one was open for 52% of the time, Pallas kernels for 0%

profile of v4, /device:TPU:0, one launch (start us, length us, event | category | flops | bytes accessed | tf_op | source)
XLA Modules:
  0.0 839.6 jit_solution(9303885954838887489)
XLA Ops:
  18.0 75.9 %all-gather.7.cloned.1.call-done = bf16[16,1,73728]{2,1,0:T(2,128)(2,1)} async-done(((bf16[1,1,73728]{2,1,0:T(2,128)(2,1)}), bf16[16,1,73728]{2,1,0:T(2,128)(2,1)}) %all-gather.7.cloned.1.call-update) | async-done | bytes 2359312 | tf_op jit(solution)/shard_map/all_gather | solution.py:130
  115.7 7.5 convolution_convert_fusion.1
  123.3 11.9 %reshape.391 = bf16[1,8,196,3,6,64]{5,4,3,2,1,0:T(8,128)(2,1)} reshape(bf16[1568,1152]{1,0:T(8,128)(2,1)} %convolution_convert_fusion.1) | data formatting | bytes 7225344 | tf_op jit(solution)/shard_map/reshape;reshape | solution.py:28
  135.2 8.4 %copy.204 = bf16[1,8,196,3,6,64]{5,1,4,2,3,0:T(8,128)(2,1)S(1)} copy(bf16[1,8,196,3,6,64]{5,4,3,2,1,0:T(8,128)(2,1)} %reshape.391) | data formatting | bytes 7225344 | tf_op jit(solution)/shard_map/reshape;reshape | solution.py:28
  204.2 7.4 convolution_convert_fusion
  211.6 11.8 %reshape.392 = bf16[8,196,3,6,64]{4,3,2,1,0:T(8,128)(2,1)} reshape(bf16[1568,1152]{1,0:T(8,128)(2,1)} %convolution_convert_fusion) | data formatting | bytes 7225344 | tf_op jit(solution)/shard_map/reshape;reshape | solution.py:31
  283.2 15.8 %all-gather.11.cloned.1.call-done = bf16[16,1,147456]{2,1,0:T(2,128)(2,1)} async-done(((bf16[1,1,147456]{2,1,0:T(2,128)(2,1)}), bf16[16,1,147456]{2,1,0:T(2,128)(2,1)}) %all-gather.11.cloned.1.call-update) | async-done | bytes 4718608 | tf_op jit(solution)/shard_map/all_gather | solution.py:130
  299.1 9.8 %copy.205 = bf16[16,1,147456]{2,0,1:T(8,128)(2,1)S(1)} copy(bf16[16,1,147456]{2,1,0:T(2,128)(2,1)} %all-gather.11.cloned.1.call-done) | data formatting | bytes 9437184
  326.1 27.0 %multiply_convert_fusion.1 = (bf16[1568,1536]{1,0:T(8,128)(2,1)S(1)}, f32[1568,1536]{1,0:T(8,128)}, f32[1568,1536]{1,0:T(8,128)}) fusion(bf16[768,1536]{1,0:T(8,128)(2,1)S(1)} %bitcast.310, bf16[784,768]{1,0:T(8,128)(2,1)} %collective-permute-done.4, bf16[784,768]{1,0:T(8,128)(2,1)} %multiply_convert_fusion.5), kind=kOutput, calls=%fused_computation.8 | convolution fusion | flops 3860742144 | bytes 28852224 | tf_op jit(solution)/shard_map/dot_general | solution.py:256
  353.1 12.2 %add_convert_fusion = bf16[1568,1536]{1,0:T(8,128)(2,1)S(1)} fusion(f32[1568,1536]{1,0:T(8,128)} %get-tuple-element.52, bf16[1568,768]{1,0:T(8,128)(2,1)S(1)} %copy-done.49, bf16[1536,768]{0,1:T(8,128)(2,1)S(1)} %bitcast.308, f32[1568,1536]{1,0:T(8,128)} %get-tuple-element.75), kind=kOutput, calls=%fused_computation.7 | convolution fusion | flops 3733094400 | bytes 28852224 | tf_op jit(solution)/shard_map/dot_general | solution.py:265
  399.0 7.7 convolution_convert_fusion.3
  414.4 8.3 convolution_convert_fusion.2
  448.6 7.0 fusion.39
  455.6 7.4 multiply_reduce_fusion
  463.0 11.5 %multiply_convert_fusion = bf16[8,6,196,196]{2,3,1,0:T(8,128)(2,1)} fusion(f32[8,6,196,196]{2,3,1,0:T(8,128)} %get-tuple-element.77, f32[8,6,196,196]{2,3,1,0:T(8,128)} %copy-done, f32[8,6,196]{2,1,0:T(8,128)S(1)} %get-tuple-element.76, f32[8,6,196]{2,1,0:T(8,128)S(1)} %log_add_fusion.1), kind=kLoop, calls=%fused_computation.1 | loop fusion | flops 9219840 | bytes 18514944 | tf_op jit(solution)/shard_map/convert_element_type | solution.py:100
  496.4 9.0 %convert_element_type.255 = bf16[1568,1152]{0,1:T(8,128)(2,1)} reshape(bf16[8,196,3,6,64]{1,0,4,3,2:T(8,128)(2,1)} %copy.151) | data formatting | bytes 7225344 | tf_op jit(solution)/shard_map/convert_element_type | solution.py:109
  519.8 7.0 convert_bitcast_fusion.2
  572.9 7.3 multiply_reduce_fusion.2
  607.2 12.0 %copy.156 = bf16[1,8,196,3,6,64]{2,1,5,4,3,0:T(8,128)(2,1)} copy(bf16[1,8,196,3,6,64]{5,1,4,2,3,0:T(8,128)(2,1)} %maximum_bitcast_fusion) | data formatting | bytes 7225344 | tf_op jit(solution)/shard_map/transpose | solution.py:38
  619.2 9.0 %reshape_reshape.40 = bf16[1568,1152]{0,1:T(8,128)(2,1)} reshape(bf16[1,8,196,3,6,64]{2,1,5,4,3,0:T(8,128)(2,1)} %copy.156) | data formatting | bytes 7225344 | tf_op jit(solution)/shard_map/reshape;reshape | solution.py:110
  628.2 6.7 convert_bitcast_fusion.3
  660.3 8.0 reshape.372
  694.5 39.6 %psum.7 = f32[3,768]{1,0:T(4,128)} all-reduce(f32[3,768]{1,0:T(4,128)S(1)} %pad_maximum_fusion.14), channel_id=1, replica_groups=mesh['dp'=8,'ty'=2,'core'=2] {'dp','ty','core'}, use_global_device_ids=true, to_apply=%region_21.22 | all-reduce | flops 2304 | bytes 18432 | tf_op jit(solution)/shard_map/psum | solution.py:312
  740.8 75.0 %reduce-scatter.8.cloned.1.call-done = bf16[384,768]{1,0:T(8,128)(2,1)} async-done(((bf16[3072,768]{1,0:T(8,128)(2,1)}), bf16[384,768]{1,0:T(8,128)(2,1)}) %reduce-scatter.8.cloned.1.call-update) | async-done | bytes 589840 | tf_op jit(solution)/shard_map/reduce_scatter | solution.py:189
  (395 shorter events, 420.4 us)
Async XLA Ops:
  7.2 86.7 %all-gather.7.cloned.1.call-start = ((), (), s32[]{:S(2)}) async-start(), calls=%async_computation.6 | async-start | bytes 5013504 | tf_op jit(solution)/shard_map/all_gather | solution.py:130
  10.8 165.0 %all-gather.9.cloned.1.call-start = ((), (), s32[]{:S(2)}) async-start(), calls=%async_computation.7 | async-start | bytes 5013504 | tf_op jit(solution)/shard_map/all_gather | solution.py:130
  12.2 158.6 %copy-start.69 = (f32[768]{0:T(1024)}, f32[768]{0:T(1024)S(1)}, u32[]{:S(2)}) copy-start(f32[768]{0:T(1024)S(1)} %get-tuple-element.44) | copy-start | bytes 9220
  13.7 102.1 %collective-permute-start = (bf16[784,768]{1,0:T(8,128)(2,1)}, bf16[784,768]{1,0:T(8,128)(2,1)}, u32[]{:S(2)}, u32[]{:S(2)}) collective-permute-start(bf16[784,768]{1,0:T(8,128)(2,1)} %fusion.21), channel_id=1, source_target_pairs={{0,1},{1,0},{2,3},{3,2},{4,5},{5,4},{6,7},{7,6},{8,9},{9,8},{10,11... | collective-permute-start | bytes 3612680 | tf_op jit(solution)/shard_map/ppermute | solution.py:232
  15.8 283.3 %all-gather.11.cloned.1.call-start = ((), (), s32[]{:S(2)}) async-start(), calls=%async_computation.8 | async-start | bytes 10027008 | tf_op jit(solution)/shard_map/all_gather | solution.py:130
  162.3 5.2 collective-permute-start.1
  167.4 523.4 %reduce-scatter.6.cloned.1.call-start = ((), (), s32[]{:S(2)}) async-start(), calls=%async_computation.4 | async-start | bytes 2654208 | tf_op jit(solution)/shard_map/reduce_scatter | solution.py:189
  170.3 107.9 %copy-start.2 = (f32[784,768]{1,0:T(8,128)}, f32[784,768]{1,0:T(8,128)S(1)}, u32[]{:S(2)}) copy-start(f32[784,768]{1,0:T(8,128)S(1)} %get-tuple-element.56) | copy-start | bytes 7225348
  172.2 31.9 %collective-permute-start.2 = (bf16[784,768]{1,0:T(8,128)(2,1)}, bf16[784,768]{1,0:T(8,128)(2,1)}, u32[]{:S(2)}, u32[]{:S(2)}) collective-permute-start(bf16[784,768]{1,0:T(8,128)(2,1)} %multiply_convert_fusion.6), channel_id=1, source_target_pairs={{0,1},{1,0},{2,3},{3,2},{4,5},{5,4},{6,7},{7,6},{8,9},{9,8},{10,11... | collective-permute-start | bytes 3612680 | tf_op jit(solution)/shard_map/ppermute | solution.py:232
  172.3 103.6 %collective-permute-start.6 = (bf16[784,768]{1,0:T(8,128)(2,1)}, bf16[784,768]{1,0:T(8,128)(2,1)}, u32[]{:S(2)}, u32[]{:S(2)}) collective-permute-start(bf16[784,768]{1,0:T(8,128)(2,1)} %param.10), channel_id=1, source_target_pairs={{0,1},{1,0},{2,3},{3,2},{4,5},{5,4},{6,7},{7,6},{8,9},{9,8},{10,11... | collective-permute-start | bytes 3612680 | tf_op jit(solution)/shard_map/ppermute | solution.py:232
  188.5 71.2 %copy-start.42 = (bf16[384,768]{1,0:T(8,128)(2,1)}, bf16[384,768]{1,0:T(8,128)(2,1)S(1)}, u32[]{:S(2)}) copy-start(bf16[384,768]{1,0:T(8,128)(2,1)S(1)} %reshape.357) | copy-start | bytes 1769476
  265.7 12.5 %collective-permute-start.3 = (bf16[784,768]{1,0:T(8,128)(2,1)}, bf16[784,768]{1,0:T(8,128)(2,1)}, u32[]{:S(2)}, u32[]{:S(2)}) collective-permute-start(bf16[784,768]{1,0:T(8,128)(2,1)} %slice.299), channel_id=1, source_target_pairs={{0,1},{1,0},{2,3},{3,2},{4,5},{5,4},{6,7},{7,6},{8,9},{9,8},{10,11... | collective-permute-start | bytes 3612680 | tf_op jit(solution)/shard_map/ppermute | solution.py:232
  282.7 43.3 %collective-permute-start.4 = (bf16[784,768]{1,0:T(8,128)(2,1)}, bf16[784,768]{1,0:T(8,128)(2,1)}, u32[]{:S(2)}, u32[]{:S(2)}) collective-permute-start(bf16[784,768]{1,0:T(8,128)(2,1)} %multiply_convert_fusion.5), channel_id=1, source_target_pairs={{0,1},{1,0},{2,3},{3,2},{4,5},{5,4},{6,7},{7,6},{8,9},{9,8},{10,11... | collective-permute-start | bytes 3612680 | tf_op jit(solution)/shard_map/ppermute | solution.py:232
  370.7 15.7 %collective-permute-start.7 = (bf16[784,768]{1,0:T(8,128)(2,1)}, bf16[784,768]{1,0:T(8,128)(2,1)}, u32[]{:S(2)}, u32[]{:S(2)}) collective-permute-start(bf16[784,768]{1,0:T(8,128)(2,1)} %slice.297), channel_id=1, source_target_pairs={{0,1},{1,0},{2,3},{3,2},{4,5},{5,4},{6,7},{7,6},{8,9},{9,8},{10,11... | collective-permute-start | bytes 3612680 | tf_op jit(solution)/shard_map/ppermute | solution.py:232
  376.1 14.1 %collective-permute-start.5 = (bf16[784,768]{1,0:T(8,128)(2,1)}, bf16[784,768]{1,0:T(8,128)(2,1)}, u32[]{:S(2)}, u32[]{:S(2)}) collective-permute-start(bf16[784,768]{1,0:T(8,128)(2,1)} %slice.298), channel_id=1, source_target_pairs={{0,1},{1,0},{2,3},{3,2},{4,5},{5,4},{6,7},{7,6},{8,9},{9,8},{10,11... | collective-permute-start | bytes 3612680 | tf_op jit(solution)/shard_map/ppermute | solution.py:232
  398.5 39.8 %collective-permute-start.8 = (bf16[784,768]{1,0:T(8,128)(2,1)}, bf16[784,768]{1,0:T(8,128)(2,1)}, u32[]{:S(2)}, u32[]{:S(2)}) collective-permute-start(bf16[784,768]{1,0:T(8,128)(2,1)} %fusion.56), channel_id=1, source_target_pairs={{0,1},{1,0},{2,3},{3,2},{4,5},{5,4},{6,7},{7,6},{8,9},{9,8},{10,11... | collective-permute-start | bytes 3612680 | tf_op jit(solution)/shard_map/ppermute | solution.py:232
  514.5 21.7 %collective-permute-start.9 = (bf16[784,768]{1,0:T(8,128)(2,1)}, bf16[784,768]{1,0:T(8,128)(2,1)}, u32[]{:S(2)}, u32[]{:S(2)}) collective-permute-start(bf16[784,768]{1,0:T(8,128)(2,1)} %slice.296), channel_id=1, source_target_pairs={{0,1},{1,0},{2,3},{3,2},{4,5},{5,4},{6,7},{7,6},{8,9},{9,8},{10,11... | collective-permute-start | bytes 3612680 | tf_op jit(solution)/shard_map/ppermute | solution.py:232
  546.2 7.0 collective-permute-start.10
  552.8 181.3 %reduce-scatter.4.cloned.1.call-start = ((), (), s32[]{:S(2)}) async-start(), calls=%async_computation.3 | async-start | bytes 2654208 | tf_op jit(solution)/shard_map/reduce_scatter | solution.py:189
  649.0 166.8 %reduce-scatter.8.cloned.1.call-start = ((), (), s32[]{:S(2)}) async-start(), calls=%async_computation.5 | async-start | bytes 5308416 | tf_op jit(solution)/shard_map/reduce_scatter | solution.py:189
  678.8 3.2 collective-permute-start.11
  693.0 46.0 %collective-permute-start.13 = (bf16[73728]{0:T(1024)(128)(2,1)S(1)}, bf16[73728]{0:T(1024)(128)(2,1)S(1)}, u32[]{:S(2)}, u32[]{:S(2)}) collective-permute-start(bf16[73728]{0:T(1024)(128)(2,1)S(1)} %get-tuple-element.67), channel_id=1, source_target_pairs={{0,2},{2,0},{1,3},{3,1},{4,6},{6,4},{5,7},{7,5},{8,10},{10,8},{9,1... | collective-permute-start | bytes 442376 | tf_op jit(solution)/shard_map/ppermute | solution.py:209
  736.2 87.2 %collective-permute-start.12 = (bf16[73728]{0:T(1024)(128)(2,1)S(1)}, bf16[73728]{0:T(1024)(128)(2,1)S(1)}, u32[]{:S(2)}, u32[]{:S(2)}) collective-permute-start(bf16[73728]{0:T(1024)(128)(2,1)S(1)} %get-tuple-element.69), channel_id=1, source_target_pairs={{0,2},{2,0},{1,3},{3,1},{4,6},{6,4},{5,7},{7,5},{8,10},{10,8},{9,1... | collective-permute-start | bytes 442376 | tf_op jit(solution)/shard_map/ppermute | solution.py:209
  821.9 8.5 %collective-permute-start.14 = (bf16[147456]{0:T(1024)(128)(2,1)S(1)}, bf16[147456]{0:T(1024)(128)(2,1)S(1)}, u32[]{:S(2)}, u32[]{:S(2)}) collective-permute-start(bf16[147456]{0:T(1024)(128)(2,1)S(1)} %get-tuple-element.65), channel_id=1, source_target_pairs={{0,2},{2,0},{1,3},{3,1},{4,6},{6,4},{5,7},{7,5},{8,10},{10,8},{9,1... | collective-permute-start | bytes 884744 | tf_op jit(solution)/shard_map/ppermute | solution.py:209
  (82 other events, 402.2 us)
Sparse Core Ops, SparseCore 0:
  11.4 82.5 all-gather.6
  97.3 78.4 all-gather.8
  178.6 120.3 all-gather.10
  552.9 68.0 reduce-scatter.5
  649.1 68.1 reduce-scatter.3
  720.8 94.9 reduce-scatter.7

commit v5 on v4

--- a/solution.py
+++ b/solution.py
@@ -123,11 +123,12 @@
 
 
 def gather_weights(shards, layouts):
-    flat = [w.astype(jnp.bfloat16).reshape(1, -1) for w in shards]
-    sizes = [f.shape[1] for f in flat]
+    lane = 768
+    flat = [w.astype(jnp.bfloat16).reshape(-1, lane) for w in shards]
+    sizes = [f.shape[0] for f in flat]
     ny = lax.axis_size("ty")
     nd = lax.axis_size("dp")
-    whole = lax.all_gather(jnp.concatenate(flat, axis=1), WEIGHT_AXES, axis=0, tiled=True)
+    whole = lax.all_gather(jnp.concatenate(flat, axis=0), WEIGHT_AXES, axis=0, tiled=False)
     out = []
     offset = 0
     for w, size, (dp_dim, ty_dim) in zip(shards, sizes, layouts):
@@ -179,16 +180,15 @@
                 pos += 1
         flat.append(
             jnp.transpose(parts, [dp_pos, ty_pos] + rest)
-            .reshape(nd, ny, -1)
+            .reshape(nd, ny, -1, 768)
             .astype(jnp.bfloat16)
         )
     sizes = [f.shape[2] for f in flat]
     stacked = jnp.concatenate(flat, axis=2)
-    width = stacked.shape[2]
-    lane = 768 if width % 768 == 0 else width
+    rows = stacked.shape[2]
     blocks = lax.psum_scatter(
-        stacked.reshape(-1, lane), "dp", scatter_dimension=0, tiled=True
-    ).reshape(ny, width)
+        stacked.reshape(-1, 768), "dp", scatter_dimension=0, tiled=True
+    ).reshape(ny, rows, 768)
     return blocks, sizes, shard_shapes
 
 

time: 850 us -> 694 us (0.82)
  waiting for transfers between devices: 178 us -> 89.8 us
  local copies, waits for them, and re-layouts: 321 us -> 280 us
  other arithmetic: 102 us -> 78 us
    reduce_scatter x3, waiting for transfers between devices: 75 us -> 21.5 us  [scatter_grads(): lax.psum_scatter(stacked.reshape(-1, 768), 'dp', scatter_dimension=0, til...]
    all_gather x3, waiting for transfers between devices: 94.8 us -> 61.1 us  [gather_weights(): lax.all_gather(jnp.concatenate(flat, axis=0), WEIGHT_AXES, axis=0, tiled=...]
    unnamed x184 -> x155, local copies, waits for them, and re-layouts: 63.6 us -> 37.4 us
    reshape x11 -> x10, local copies, waits for them, and re-layouts: 20.7 us -> 2.84 us  [the longest x5 2.12 us: finish_grads(): out.append(summed[offset:offset + size].reshape(shard))]
    another operation x2, local copies, waits for them, and re-layouts: 5.97 us -> 15.9 us  [attend_forward(): from_groups(attended.astype(jnp.bfloat16), temporal)]
    concatenate x3 -> x0, local copies, waits for them, and re-layouts: 9.68 us -> none  [scatter_grads(): stacked = jnp.concatenate(flat, axis=2)]
    reshape x8 -> x6, local copies, waits for them, and re-layouts: 22.2 us -> 24.2 us  [gather_weights(): part = whole[:, offset:offset + size].reshape((nd, ny) + w.shape)]
  transfers between devices with their start and end apart: 21 -> 21, of which waited for: 6 -> 6; matrix products, arithmetic and copies ran while one was open for 52% -> 55% of each run, Pallas kernels for 0% -> 0%
where the time goes in v5:
time: 694 us; the launch traced here: 683 us
  local copies, waits for them, and re-layouts  280 us (40%)
  matrix products  171 us (25%)
  waiting for transfers between devices  89.8 us (13%)
  other arithmetic  78 us (11%)
  blocking collectives  40.4 us (6%)
  between operations  15.8 us (2%)
  starting transfers between devices  8.35 us (1%)
    all_gather x3, waiting for transfers between devices, gather_weights(): lax.all_gather(jnp.concatenate(flat, axis=0), WEIGHT_AXES, axis=0, tiled=...  61.1 us
    psum x1, blocking collectives, per_device(): lax.psum(jnp.stack([gain_time, gain_space, gain_mlp]), ('dp', 'ty', 'core'))  40.4 us
    unnamed x155, local copies, waits for them, and re-layouts  37.4 us
    convert_element_type x12, local copies, waits for them, and re-layouts, scatter_grads(): flat.append(jnp.transpose(parts, [dp_pos, ty_pos] + rest).reshape(nd, ny,...  37 us
    dot_general x1, matrix products, per_device(): jnp.dot(normed_mlp, up_full, preferred_element_type=jnp.float32)  26.9 us
    reshape x6, local copies, waits for them, and re-layouts, gather_weights(): part = whole[:, offset:offset + size].reshape((nd, ny) + w.shape)  24.2 us
    another operation x3, local copies, waits for them, and re-layouts, to_groups(): shaped = values.reshape((clip_count, FRAMES, PATCH) + trailing)  23.7 us
    reduce_scatter x3, waiting for transfers between devices, scatter_grads(): lax.psum_scatter(stacked.reshape(-1, 768), 'dp', scatter_dimension=0, til...  21.5 us
  transfers between devices with their start and end apart: 21, of which 6 were waited for; matrix products, arithmetic and copies ran while one was open for 55% of the time, Pallas kernels for 0%

profile of v5, /device:TPU:0, one launch (start us, length us, event | category | flops | bytes accessed | tf_op | source)
XLA Modules:
  0.0 683.0 jit_solution(8466374500680111258)
XLA Ops:
  15.3 61.1 %all-gather.7.cloned.1.call-done = bf16[1536,768]{1,0:T(8,128)(2,1)} async-done(((bf16[96,768]{1,0:T(8,128)(2,1)}), bf16[1536,768]{1,0:T(8,128)(2,1)}) %all-gather.7.cloned.1.call-update) | async-done | bytes 2359312 | tf_op jit(solution)/shard_map/all_gather | solution.py:131
  97.0 7.5 %convolution_convert_fusion.1 = bf16[1568,1152]{1,0:T(8,128)(2,1)} fusion(bf16[768,1152]{0,1:T(8,128)(2,1)S(1)} %reshape_reshape.32, bf16[784,768]{1,0:T(8,128)(2,1)} %collective-permute-done, bf16[784,768]{1,0:T(8,128)(2,1)} %fusion.21), kind=kOutput, calls=%fused_computation.26 | convolution fusion | flops 2781155328 | bytes 7790592 | tf_op jit(solution)/shard_map/dot_general | solution.py:45
  104.5 11.9 %reshape.348 = bf16[1,8,196,3,6,64]{5,4,3,2,1,0:T(8,128)(2,1)} reshape(bf16[1568,1152]{1,0:T(8,128)(2,1)} %convolution_convert_fusion.1) | data formatting | bytes 7225344 | tf_op jit(solution)/shard_map/reshape;reshape | solution.py:28
  116.4 8.4 %copy.152 = bf16[1,8,196,3,6,64]{5,1,4,2,3,0:T(8,128)(2,1)S(1)} copy(bf16[1,8,196,3,6,64]{5,4,3,2,1,0:T(8,128)(2,1)} %reshape.348) | data formatting | bytes 7225344 | tf_op jit(solution)/shard_map/reshape;reshape | solution.py:28
  137.6 11.6 %reshape_reshape.34 = bf16[1568,384]{0,1:T(8,128)(2,1)S(1)} reshape(bf16[1,8,196,6,64]{2,1,4,3,0:T(8,128)(2,1)S(1)} %copy.85) | data formatting | bytes 2408448 | tf_op jit(solution)/shard_map/reshape;reshape | solution.py:66
  171.7 7.6 %reshape.311 = bf16[8,2,96,3,192]{4,3,2,1,0:T(4,128)(2,1)} reshape(bf16[16,72,768]{2,1,0:T(8,128)(2,1)} %slice.154) | data formatting | bytes 3538944 | tf_op jit(solution)/shard_map/reshape | solution.py:135
  189.1 7.3 %convolution_convert_fusion = bf16[1568,1152]{1,0:T(8,128)(2,1)} fusion(bf16[768,1152]{0,1:T(8,128)(2,1)} %reshape_reshape.35, bf16[784,768]{1,0:T(8,128)(2,1)} %collective-permute-done.2, bf16[784,768]{1,0:T(8,128)(2,1)} %multiply_convert_fusion.6), kind=kOutput, calls=%fused_computation.25 | convolution fusion | flops 2781155328 | bytes 7790592 | tf_op jit(solution)/shard_map/dot_general | solution.py:45
  196.4 11.7 %reshape.349 = bf16[8,196,3,6,64]{4,3,2,1,0:T(8,128)(2,1)} reshape(bf16[1568,1152]{1,0:T(8,128)(2,1)} %convolution_convert_fusion) | data formatting | bytes 7225344 | tf_op jit(solution)/shard_map/reshape;reshape | solution.py:31
  208.1 6.8 fusion.83
  275.9 26.9 %multiply_convert_fusion.1 = (bf16[1568,1536]{1,0:T(8,128)(2,1)}, f32[1568,1536]{1,0:T(8,128)}, f32[1568,1536]{1,0:T(8,128)}) fusion(bf16[768,1536]{1,0:T(8,128)(2,1)S(1)} %bitcast.300, bf16[784,768]{1,0:T(8,128)(2,1)} %collective-permute-done.4, bf16[784,768]{1,0:T(8,128)(2,1)} %multiply_convert_fusion.5), kind=kOutput, calls=%fused_computation.8 | convolution fusion | flops 3860742144 | bytes 28852224 | tf_op jit(solution)/shard_map/dot_general | solution.py:256
  302.8 11.1 %add_convert_fusion = bf16[1568,1536]{1,0:T(8,128)(2,1)S(1)} fusion(f32[1568,1536]{1,0:T(8,128)} %get-tuple-element.43, bf16[1568,768]{1,0:T(8,128)(2,1)} %constant_dynamic-update-slice_fusion, bf16[1536,768]{0,1:T(8,128)(2,1)S(1)} %bitcast.298, f32[1568,1536]{1,0:T(8,128)} %get-tuple-element.60), kind=kOutput, calls=%fused_computation.7 | convolution fusion | flops 3733094400 | bytes 28852224 | tf_op jit(solution)/shard_map/dot_general | solution.py:265
  346.2 7.0 %fusion.39 = bf16[8,196,1,6,64]{1,4,3,0,2:T(8,128)(2,1)} fusion(bf16[8,196,6,64]{1,3,2,0:T(8,128)(2,1)S(1)} %copy.100, f32[8,6,196,196]{2,3,1,0:T(8,128)} %copy-done, f32[8,6,196]{2,1,0:T(8,128)S(1)} %log_add_fusion.1), kind=kOutput, calls=%fused_computation.116 | convolution fusion | flops 241559808 | bytes 9821952 | tf_op jit(solution)/shard_map/bhlm,blhe->bmhe/dot_general | solution.py:88
  353.2 7.4 %multiply_reduce_fusion = (f32[8,6,196]{2,1,0:T(8,128)S(1)}, f32[8,6,196,196]{2,3,1,0:T(8,128)}) fusion(f32[8,6,196,196]{2,3,1,0:T(8,128)} %copy-done, f32[8,6,196]{2,1,0:T(8,128)S(1)} %log_add_fusion.1, bf16[8,196,6,64]{1,3,2,0:T(8,128)(2,1)S(1)} %copy.100, bf16[8,196,1,6,64]{1,4,3,0,2:T(8,128)(2,1)S(1)} %copy-done.34), kind=kOutput, calls=%fused_computation.2 | convolution fusion | flops 243394368 | bytes 17235456 | tf_op jit(solution)/shard_map/blhe,bmhe->bhlm/dot_general | solution.py:94
  360.7 11.5 %multiply_convert_fusion = bf16[8,6,196,196]{2,3,1,0:T(8,128)(2,1)} fusion(f32[8,6,196,196]{2,3,1,0:T(8,128)} %get-tuple-element.62, f32[8,6,196,196]{2,3,1,0:T(8,128)} %copy-done, f32[8,6,196]{2,1,0:T(8,128)S(1)} %get-tuple-element.61, f32[8,6,196]{2,1,0:T(8,128)S(1)} %log_add_fusion.1), kind=kLoop, calls=%fused_computation.1 | loop fusion | flops 9219840 | bytes 18514944 | tf_op jit(solution)/shard_map/convert_element_type | solution.py:100
  400.6 9.0 %convert_element_type.252 = bf16[1568,1152]{0,1:T(8,128)(2,1)} reshape(bf16[8,196,3,6,64]{1,0,4,3,2:T(8,128)(2,1)} %copy.105) | data formatting | bytes 7225344 | tf_op jit(solution)/shard_map/convert_element_type | solution.py:109
  409.6 6.8 convert_bitcast_fusion.2
  425.6 9.0 %convolution_convert_fusion.3 = bf16[768,1536]{1,0:T(8,128)(2,1)} fusion(bf16[1568,1536]{1,0:T(8,128)(2,1)} %copy-done.69, bf16[784,768]{1,0:T(8,128)(2,1)} %collective-permute-done.4, bf16[784,768]{1,0:T(8,128)(2,1)} %multiply_convert_fusion.5), kind=kOutput, calls=%fused_computation.55 | convolution fusion | flops 3705372672 | bytes 9584640 | tf_op jit(solution)/shard_map/dot_general | solution.py:268
  441.8 9.1 %convolution_convert_fusion.2 = bf16[1536,768]{1,0:T(8,128)(2,1)} fusion(bf16[1568,1536]{1,0:T(8,128)(2,1)} %get-tuple-element.42, bf16[1568,768]{1,0:T(8,128)(2,1)} %constant_dynamic-update-slice_fusion), kind=kOutput, calls=%fused_computation.54 | convolution fusion | flops 3700555776 | bytes 9584640 | tf_op jit(solution)/shard_map/dot_general | solution.py:264
  520.6 6.8 multiply_reduce_fusion.2
  541.0 12.1 %copy.110 = bf16[1,8,196,3,6,64]{2,1,5,4,3,0:T(8,128)(2,1)} copy(bf16[1,8,196,3,6,64]{5,1,4,2,3,0:T(8,128)(2,1)} %maximum_bitcast_fusion) | data formatting | bytes 7225344 | tf_op jit(solution)/shard_map/transpose | solution.py:38
  553.1 9.0 %reshape_reshape.40 = bf16[1568,1152]{0,1:T(8,128)(2,1)} reshape(bf16[1,8,196,3,6,64]{2,1,5,4,3,0:T(8,128)(2,1)} %copy.110) | data formatting | bytes 7225344 | tf_op jit(solution)/shard_map/reshape;reshape | solution.py:110
  562.1 6.8 convert_bitcast_fusion.3
  593.5 40.4 %psum.7 = f32[3,768]{1,0:T(4,128)} all-reduce(f32[3,768]{1,0:T(4,128)S(1)} %pad_maximum_fusion.17), channel_id=1, replica_groups=mesh['dp'=8,'ty'=2,'core'=2] {'dp','ty','core'}, use_global_device_ids=true, to_apply=%region_21.22 | all-reduce | flops 2304 | bytes 18432 | tf_op jit(solution)/shard_map/psum | solution.py:312
  644.3 21.4 %reduce-scatter.4.cloned.1.call-done = bf16[192,768]{1,0:T(8,128)(2,1)} async-done(((bf16[1536,768]{1,0:T(8,128)(2,1)}), bf16[192,768]{1,0:T(8,128)(2,1)}) %reduce-scatter.4.cloned.1.call-update) | async-done | bytes 294928 | tf_op jit(solution)/shard_map/reduce_scatter | solution.py:189
  (354 shorter events, 338.9 us)
Async XLA Ops:
  7.2 69.2 %all-gather.7.cloned.1.call-start = ((), (), s32[]{:S(2)}) async-start(), calls=%async_computation.6 | async-start | bytes 2506752 | tf_op jit(solution)/shard_map/all_gather | solution.py:131
  10.3 151.5 %all-gather.9.cloned.1.call-start = ((), (), s32[]{:S(2)}) async-start(), calls=%async_computation.7 | async-start | bytes 2506752 | tf_op jit(solution)/shard_map/all_gather | solution.py:131
  11.2 148.1 %copy-start.62 = (f32[768]{0:T(1024)}, f32[768]{0:T(1024)S(1)}, u32[]{:S(2)}) copy-start(f32[768]{0:T(1024)S(1)} %get-tuple-element.35) | copy-start | bytes 9220
  13.6 83.4 %collective-permute-start = (bf16[784,768]{1,0:T(8,128)(2,1)}, bf16[784,768]{1,0:T(8,128)(2,1)}, u32[]{:S(2)}, u32[]{:S(2)}) collective-permute-start(bf16[784,768]{1,0:T(8,128)(2,1)} %fusion.21), channel_id=1, source_target_pairs={{0,1},{1,0},{2,3},{3,2},{4,5},{5,4},{6,7},{7,6},{8,9},{9,8},{10,11... | collective-permute-start | bytes 3612680 | tf_op jit(solution)/shard_map/ppermute | solution.py:232
  15.2 240.6 %all-gather.11.cloned.1.call-start = ((), (), s32[]{:S(2)}) async-start(), calls=%async_computation.8 | async-start | bytes 5013504 | tf_op jit(solution)/shard_map/all_gather | solution.py:131
  152.9 3.1 collective-permute-start.1
  155.0 484.5 %reduce-scatter.6.cloned.1.call-start = ((), (), s32[]{:S(2)}) async-start(), calls=%async_computation.4 | async-start | bytes 2654208 | tf_op jit(solution)/shard_map/reduce_scatter | solution.py:189
  158.9 92.1 %copy-start.2 = (f32[784,768]{1,0:T(8,128)}, f32[784,768]{1,0:T(8,128)S(1)}, u32[]{:S(2)}) copy-start(f32[784,768]{1,0:T(8,128)S(1)} %get-tuple-element.47) | copy-start | bytes 7225348
  161.6 27.4 %collective-permute-start.2 = (bf16[784,768]{1,0:T(8,128)(2,1)}, bf16[784,768]{1,0:T(8,128)(2,1)}, u32[]{:S(2)}, u32[]{:S(2)}) collective-permute-start(bf16[784,768]{1,0:T(8,128)(2,1)} %multiply_convert_fusion.6), channel_id=1, source_target_pairs={{0,1},{1,0},{2,3},{3,2},{4,5},{5,4},{6,7},{7,6},{8,9},{9,8},{10,11... | collective-permute-start | bytes 3612680 | tf_op jit(solution)/shard_map/ppermute | solution.py:232
  171.7 73.3 %copy-start.41 = (bf16[384,768]{1,0:T(8,128)(2,1)}, bf16[384,768]{1,0:T(8,128)(2,1)S(1)}, u32[]{:S(2)}) copy-start(bf16[384,768]{1,0:T(8,128)(2,1)S(1)} %reshape.313) | copy-start | bytes 1769476
  248.0 2.9 collective-permute-start.3
  248.4 6.3 collective-permute-start.6
  253.2 22.5 %collective-permute-start.4 = (bf16[784,768]{1,0:T(8,128)(2,1)}, bf16[784,768]{1,0:T(8,128)(2,1)}, u32[]{:S(2)}, u32[]{:S(2)}) collective-permute-start(bf16[784,768]{1,0:T(8,128)(2,1)} %multiply_convert_fusion.5), channel_id=1, source_target_pairs={{0,1},{1,0},{2,3},{3,2},{4,5},{5,4},{6,7},{7,6},{8,9},{9,8},{10,11... | collective-permute-start | bytes 3612680 | tf_op jit(solution)/shard_map/ppermute | solution.py:232
  318.0 5.0 collective-permute-start.7
  322.6 3.2 collective-permute-start.5
  329.9 6.2 collective-permute-start.8
  425.5 217.7 %reduce-scatter.8.cloned.1.call-start = ((), (), s32[]{:S(2)}) async-start(), calls=%async_computation.5 | async-start | bytes 5308416 | tf_op jit(solution)/shard_map/reduce_scatter | solution.py:189
  474.5 3.8 collective-permute-start.9
  478.0 187.8 %reduce-scatter.4.cloned.1.call-start = ((), (), s32[]{:S(2)}) async-start(), calls=%async_computation.3 | async-start | bytes 2654208 | tf_op jit(solution)/shard_map/reduce_scatter | solution.py:189
  487.8 8.3 %collective-permute-start.10 = (bf16[784,768]{1,0:T(8,128)(2,1)}, bf16[784,768]{1,0:T(8,128)(2,1)}, u32[]{:S(2)}, u32[]{:S(2)}) collective-permute-start(bf16[784,768]{1,0:T(8,128)(2,1)} %fusion.75), channel_id=1, source_target_pairs={{0,1},{1,0},{2,3},{3,2},{4,5},{5,4},{6,7},{7,6},{8,9},{9,8},{10,11... | collective-permute-start | bytes 3612680 | tf_op jit(solution)/shard_map/ppermute | solution.py:232
  587.4 3.1 collective-permute-start.11
  640.4 27.9 %collective-permute-start.13 = (bf16[96,768]{1,0:T(8,128)(2,1)S(1)}, bf16[96,768]{1,0:T(8,128)(2,1)S(1)}, u32[]{:S(2)}, u32[]{:S(2)}) collective-permute-start(bf16[96,768]{1,0:T(8,128)(2,1)S(1)} %dynamic-slice_bitcast_fusion.1), channel_id=1, source_target_pairs={{0,2},{2,0},{1,3},{3,1},{4,6},{6,4},{5,7},{7,5},{8,10},{10,8},{9,1... | collective-permute-start | bytes 442376 | tf_op jit(solution)/shard_map/ppermute | solution.py:209
  644.2 29.6 %collective-permute-start.14 = (bf16[192,768]{1,0:T(8,128)(2,1)S(1)}, bf16[192,768]{1,0:T(8,128)(2,1)S(1)}, u32[]{:S(2)}, u32[]{:S(2)}) collective-permute-start(bf16[192,768]{1,0:T(8,128)(2,1)S(1)} %dynamic-slice_bitcast_fusion), channel_id=1, source_target_pairs={{0,2},{2,0},{1,3},{3,1},{4,6},{6,4},{5,7},{7,5},{8,10},{10,8},{9,1... | collective-permute-start | bytes 884744 | tf_op jit(solution)/shard_map/ppermute | solution.py:209
  666.8 5.2 collective-permute-start.12
  (70 other events, 387.2 us)
Sparse Core Ops, SparseCore 0:
  11.4 64.9 all-gather.6
  79.8 60.6 all-gather.8
  155.1 78.1 all-gather.10
  425.7 68.3 reduce-scatter.5
  497.6 94.8 reduce-scatter.7
  595.8 69.9 reduce-scatter.3

commit v6 on v5

--- a/solution.py
+++ b/solution.py
@@ -119,33 +119,38 @@
     return (grad_qkv, grad_proj, grad_normed)
 
 
-WEIGHT_AXES = ("dp", "ty")
-
-
-def gather_weights(shards, layouts):
-    lane = 768
-    flat = [w.astype(jnp.bfloat16).reshape(-1, lane) for w in shards]
-    sizes = [f.shape[0] for f in flat]
-    ny = lax.axis_size("ty")
-    nd = lax.axis_size("dp")
-    whole = lax.all_gather(jnp.concatenate(flat, axis=0), WEIGHT_AXES, axis=0, tiled=False)
-    out = []
-    offset = 0
-    for w, size, (dp_dim, ty_dim) in zip(shards, sizes, layouts):
-        part = whole[:, offset : offset + size].reshape((nd, ny) + w.shape)
-        offset += size
-        order = []
-        for dim in range(w.ndim):
-            if dim == dp_dim:
-                order.append(0)
-            if dim == ty_dim:
-                order.append(1)
-            order.append(dim + 2)
-        shape = list(w.shape)
-        shape[dp_dim] *= nd
-        shape[ty_dim] *= ny
-        out.append(jnp.transpose(part, order).reshape(shape))
-    return out
+def gather_attention(qkv_shard, proj_shard):
+    rows, parts, width = qkv_shard.shape
+    mine = jnp.concatenate(
+        [qkv_shard.astype(jnp.bfloat16).reshape(rows, parts * width), proj_shard.astype(jnp.bfloat16).T],
+        axis=1,
+    )
+    other = swap_ty(mine)
+    split = parts * width
+    qkv_local = jnp.stack(
+        [mine[:, :split].reshape(rows, parts, width), other[:, :split].reshape(rows, parts, width)],
+        axis=2,
+    ).reshape(rows, 2 * split)
+    proj_local = jnp.concatenate([mine[:, split:], other[:, split:]], axis=1)
+    full = lax.all_gather(
+        jnp.concatenate([qkv_local, proj_local], axis=1), "dp", axis=0, tiled=True
+    )
+    w_qkv = full[:, : 2 * split].reshape(full.shape[0], parts, 2 * width)
+    w_proj = full[:, 2 * split :].T
+    return w_qkv, w_proj
+
+
+def gather_mlp(up_shard, down_shard):
+    width = up_shard.shape[1]
+    mine = jnp.concatenate(
+        [up_shard.astype(jnp.bfloat16), down_shard.astype(jnp.bfloat16).T], axis=1
+    )
+    other = swap_ty(mine)
+    local = jnp.concatenate(
+        [mine[:, :width], other[:, :width], mine[:, width:], other[:, width:]], axis=1
+    )
+    full = lax.all_gather(local, "dp", axis=0, tiled=True)
+    return full[:, : 2 * width], full[:, 2 * width :].T
 
 
 def scatter_grads(grads, layouts, shard_shapes):
@@ -193,10 +198,7 @@
 
 
 def finish_grads(blocks, sizes, shard_shapes):
-    here = lax.axis_index("ty")
-    own = lax.dynamic_index_in_dim(blocks, here, axis=0, keepdims=False)
-    other = lax.dynamic_index_in_dim(blocks, 1 - here, axis=0, keepdims=False)
-    summed = own.astype(jnp.float32) + swap_ty(other).astype(jnp.float32)
+    summed = blocks[0].astype(jnp.float32) + swap_ty(blocks[1]).astype(jnp.float32)
     out = []
     offset = 0
     for size, shard in zip(sizes, shard_shapes):
@@ -224,9 +226,9 @@
     proj_layout = (1, 0)
     up_layout = (0, 1)
     down_layout = (1, 0)
-    time_qkv, time_proj = gather_weights((qkv_time, proj_time), (qkv_layout, proj_layout))
-    space_qkv, space_proj = gather_weights((qkv_space, proj_space), (qkv_layout, proj_layout))
-    up_full, down_full = gather_weights((up_weight, down_weight), (up_layout, down_layout))
+    time_qkv, time_proj = gather_attention(qkv_time, proj_time)
+    space_qkv, space_proj = gather_attention(qkv_space, proj_space)
+    up_full, down_full = gather_mlp(up_weight, down_weight)
 
     def swap(values):
         return lax.ppermute(values, "core", perm=[(0, 1), (1, 0)])

time: 694 us -> 629 us (0.906)
  local copies, waits for them, and re-layouts: 280 us -> 200 us
  waiting for transfers between devices: 89.8 us -> 106 us
  other arithmetic: 78 us -> 70.5 us
    reshape x13 -> x2, local copies, waits for them, and re-layouts: 28.3 us -> 0.47 us  [gather_attention(): qkv_local = jnp.stack([mine[:, :split].reshape(rows, parts, width), other...]
    ppermute x3 -> x6, waiting for transfers between devices: 0.94 us -> 19.9 us  [swap_ty(): return lax.ppermute(values, 'ty', perm=[(0, 1), (1, 0)])]
    transpose x5 -> x2, local copies, waits for them, and re-layouts: 14.9 us -> 0.19 us  [gather_attention(): proj_shard.astype(jnp.bfloat16)]
    another operation x2, local copies, waits for them, and re-layouts: 15.9 us -> 6.11 us  [attend_forward(): from_groups(attended.astype(jnp.bfloat16), temporal)]
    slice x5 -> x10, local copies, waits for them, and re-layouts: 12.7 us -> 3.14 us  [the longest x3 2.9 us: finish_grads(): blocks[1]]
    ppermute x3 -> x6, starting transfers between devices: 4.44 us -> 12.3 us  [swap_ty(): return lax.ppermute(values, 'ty', perm=[(0, 1), (1, 0)])]
    unnamed x155 -> x163, local copies, waits for them, and re-layouts: 37.4 us -> 30.3 us
    convert_element_type x2 -> x1, local copies, waits for them, and re-layouts: 14.4 us -> 9.03 us  [attend_backward(): jnp.stack([grad_query, grad_key, grad_value], axis=2).astype(jnp.bfloat16)]
  transfers between devices with their start and end apart: 21 -> 24, of which waited for: 6 -> 10; matrix products, arithmetic and copies ran while one was open for 55% -> 47% of each run, Pallas kernels for 0% -> 0%
where the time goes in v6:
time: 629 us; the launch traced here: 622 us
  local copies, waits for them, and re-layouts  200 us (32%)
  matrix products  175 us (28%)
  waiting for transfers between devices  106 us (17%)
  other arithmetic  70.5 us (11%)
  blocking collectives  39.6 us (6%)
  between operations  15.8 us (3%)
  starting transfers between devices  15.1 us (2%)
    all_gather x2, waiting for transfers between devices, gather_attention(): lax.all_gather(jnp.concatenate([qkv_local, proj_local], axis=1), 'dp', ax...  42.7 us
    psum x1, blocking collectives, per_device(): lax.psum(jnp.stack([gain_time, gain_space, gain_mlp]), ('dp', 'ty', 'core'))  39.6 us
    convert_element_type x12, local copies, waits for them, and re-layouts, scatter_grads(): flat.append(jnp.transpose(parts, [dp_pos, ty_pos] + rest).reshape(nd, ny,...  37 us
    unnamed x163, local copies, waits for them, and re-layouts  30.3 us
    dot_general x1, matrix products, per_device(): jnp.dot(normed_mlp, up_full, preferred_element_type=jnp.float32)  30.1 us
    reduce_scatter x3, waiting for transfers between devices, scatter_grads(): lax.psum_scatter(stacked.reshape(-1, 768), 'dp', scatter_dimension=0, til...  24.5 us
    another operation x3, local copies, waits for them, and re-layouts, to_groups(): shaped = values.reshape((clip_count, FRAMES, PATCH) + trailing)  23.7 us
    ppermute x6, waiting for transfers between devices, swap_ty(): return lax.ppermute(values, 'ty', perm=[(0, 1), (1, 0)])  19.9 us
  transfers between devices with their start and end apart: 24, of which 10 were waited for; matrix products, arithmetic and copies ran while one was open for 47% of the time, Pallas kernels for 0%

profile of v6, /device:TPU:0, one launch (start us, length us, event | category | flops | bytes accessed | tf_op | source)
XLA Modules:
  0.0 621.7 jit_solution(102015834934951486)
XLA Ops:
  29.6 42.7 %all-gather.4.cloned.1.call-done = bf16[768,1536]{1,0:T(8,128)(2,1)} async-done(((bf16[96,1536]{1,0:T(8,128)(2,1)}), bf16[768,1536]{1,0:T(8,128)(2,1)}) %all-gather.4.cloned.1.call-update) | async-done | bytes 2359312 | tf_op jit(solution)/shard_map/all_gather | solution.py:135
  72.3 7.1 %convolution_convert_fusion.1 = bf16[1568,1152]{1,0:T(8,128)(2,1)} fusion(bf16[768,1536]{1,0:T(8,128)(2,1)} %all-gather.4.cloned.1.call-done, bf16[784,768]{1,0:T(8,128)(2,1)} %collective-permute-done, bf16[784,768]{1,0:T(8,128)(2,1)S(1)} %fusion.21), kind=kOutput, calls=%fused_computation.25 | convolution fusion | flops 2781155328 | bytes 7790592 | tf_op jit(solution)/shard_map/dot_general | solution.py:45
  79.4 12.0 %reshape.288 = bf16[1,8,196,3,6,64]{5,4,3,2,1,0:T(8,128)(2,1)} reshape(bf16[1568,1152]{1,0:T(8,128)(2,1)} %convolution_convert_fusion.1) | data formatting | bytes 7225344 | tf_op jit(solution)/shard_map/reshape;reshape | solution.py:28
  91.4 8.4 %copy.111 = bf16[1,8,196,3,6,64]{5,1,4,2,3,0:T(8,128)(2,1)S(1)} copy(bf16[1,8,196,3,6,64]{5,4,3,2,1,0:T(8,128)(2,1)} %reshape.288) | data formatting | bytes 7225344 | tf_op jit(solution)/shard_map/reshape;reshape | solution.py:28
  124.6 7.8 %collective-permute-done.7 = bf16[96,1536]{1,0:T(8,128)(2,1)S(1)} collective-permute-done((bf16[96,1536]{1,0:T(8,128)(2,1)S(1)}, bf16[96,1536]{1,0:T(8,128)(2,1)S(1)}, u32[]{:S(2)}, u32[]{:S(2)}) %collective-permute-start.7) | collective-permute-done | bytes 294944 | tf_op jit(solution)/shard_map/ppermute | solution.py:211
  133.5 7.3 %convolution_convert_fusion = bf16[1568,1152]{1,0:T(8,128)(2,1)} fusion(bf16[768,1536]{1,0:T(8,128)(2,1)} %all-gather.6.cloned.1.call-done, bf16[784,768]{1,0:T(8,128)(2,1)} %collective-permute-done.3, bf16[784,768]{1,0:T(8,128)(2,1)} %multiply_convert_fusion.8), kind=kOutput, calls=%fused_computation.24 | convolution fusion | flops 2781155328 | bytes 7790592 | tf_op jit(solution)/shard_map/dot_general | solution.py:45
  140.8 12.2 %reshape.289 = bf16[8,196,3,6,64]{4,3,2,1,0:T(8,128)(2,1)} reshape(bf16[1568,1152]{1,0:T(8,128)(2,1)} %convolution_convert_fusion) | data formatting | bytes 7225344 | tf_op jit(solution)/shard_map/reshape;reshape | solution.py:31
  153.0 6.8 %fusion.110 = (bf16[8,196,1,6,64]{4,3,2,1,0:T(8,128)(2,1)}, bf16[8,196,1,6,64]{4,3,2,1,0:T(8,128)(2,1)}, bf16[8,196,1,6,64]{4,3,2,1,0:T(8,128)(2,1)}) fusion(bf16[8,196,3,6,64]{4,3,2,1,0:T(8,128)(2,1)} %reshape.289), kind=kLoop, calls=%fused_computation.209 | loop fusion | bytes 7225344 | tf_op jit(solution)/shard_map/slice | solution.py:64
  199.9 11.8 %all-gather.8.cloned.1.call-done = bf16[768,3072]{1,0:T(8,128)(2,1)} async-done(((bf16[96,3072]{1,0:T(8,128)(2,1)}), bf16[768,3072]{1,0:T(8,128)(2,1)}) %all-gather.8.cloned.1.call-update) | async-done | bytes 4718608 | tf_op jit(solution)/shard_map/all_gather | solution.py:152
  211.7 30.1 %multiply_convert_fusion.1 = (bf16[1568,1536]{1,0:T(8,128)(2,1)}, f32[1568,1536]{1,0:T(8,128)}, f32[1568,1536]{1,0:T(8,128)}) fusion(bf16[768,3072]{1,0:T(8,128)(2,1)} %all-gather.8.cloned.1.call-done, bf16[784,768]{1,0:T(8,128)(2,1)S(1)} %collective-permute-done.6, bf16[784,768]{1,0:T(8,128)(2,1)S(1)} %multiply_convert_fusion.7), kind=kOutput, calls=%fused_computation.8 | convolution fusion | flops 3860742144 | bytes 28852224 | tf_op jit(solution)/shard_map/dot_general | solution.py:258
  241.8 11.2 %add_convert_fusion = bf16[1568,1536]{1,0:T(8,128)(2,1)S(1)} fusion(f32[1568,1536]{1,0:T(8,128)} %get-tuple-element.34, bf16[1568,768]{1,0:T(8,128)(2,1)} %constant_dynamic-update-slice_fusion, f32[1568,1536]{1,0:T(8,128)} %get-tuple-element.51, bf16[768,3072]{1,0:T(8,128)(2,1)S(1)} %copy-done.70), kind=kOutput, calls=%fused_computation.7 | convolution fusion | flops 3733094400 | bytes 28852224 | tf_op jit(solution)/shard_map/dot_general | solution.py:267
  285.7 7.0 %fusion.69 = bf16[8,196,1,6,64]{1,4,3,0,2:T(8,128)(2,1)} fusion(bf16[8,196,6,64]{1,3,2,0:T(8,128)(2,1)S(1)} %copy.61, f32[8,6,196,196]{2,3,1,0:T(8,128)} %copy-done, f32[8,6,196]{2,1,0:T(8,128)S(1)} %log_add_fusion.1), kind=kOutput, calls=%fused_computation.144 | convolution fusion | flops 242161920 | bytes 9821952 | tf_op jit(solution)/shard_map/bhlm,blhe->bmhe/dot_general | solution.py:88
  292.6 7.4 %multiply_reduce_fusion = (f32[8,6,196]{2,1,0:T(8,128)S(1)}, f32[8,6,196,196]{2,3,1,0:T(8,128)}) fusion(f32[8,6,196,196]{2,3,1,0:T(8,128)} %copy-done, f32[8,6,196]{2,1,0:T(8,128)S(1)} %log_add_fusion.1, bf16[8,196,6,64]{1,3,2,0:T(8,128)(2,1)S(1)} %copy.61, bf16[8,196,1,6,64]{1,4,3,0,2:T(8,128)(2,1)S(1)} %copy-done.31), kind=kOutput, calls=%fused_computation.2 | convolution fusion | flops 243394368 | bytes 17235456 | tf_op jit(solution)/shard_map/blhe,bmhe->bhlm/dot_general | solution.py:94
  300.0 11.5 %multiply_convert_fusion = bf16[8,6,196,196]{2,3,1,0:T(8,128)(2,1)} fusion(f32[8,6,196,196]{2,3,1,0:T(8,128)} %get-tuple-element.53, f32[8,6,196,196]{2,3,1,0:T(8,128)} %copy-done, f32[8,6,196]{2,1,0:T(8,128)S(1)} %get-tuple-element.52, f32[8,6,196]{2,1,0:T(8,128)S(1)} %log_add_fusion.1), kind=kLoop, calls=%fused_computation.1 | loop fusion | flops 9219840 | bytes 18514944 | tf_op jit(solution)/shard_map/convert_element_type | solution.py:100
  340.0 9.0 %convert_element_type.233 = bf16[1568,1152]{0,1:T(8,128)(2,1)} reshape(bf16[8,196,3,6,64]{1,0,4,3,2:T(8,128)(2,1)} %copy.66) | data formatting | bytes 7225344 | tf_op jit(solution)/shard_map/convert_element_type | solution.py:109
  349.1 6.7 %convert_bitcast_fusion.2 = bf16[8,2,96,3,192]{4,2,1,3,0:T(8,128)(2,1)S(1)} fusion(bf16[8,96,1568,1,1]{2,1,4,3,0:T(8,128)(2,1)S(1)} %bitcast.237, bf16[3,2,192,1568,1]{3,2,1,0,4:T(8,128)(2,1)} %bitcast.235), kind=kOutput, calls=%fused_computation.112 | convolution fusion | flops 2775416832 | bytes 7790592 | tf_op jit(solution)/shard_map/dot_general | solution.py:111
  365.1 8.3 %convolution_convert_fusion.3 = bf16[768,1536]{1,0:T(8,128)(2,1)} fusion(bf16[1568,1536]{1,0:T(8,128)(2,1)} %copy-done.73, bf16[784,768]{1,0:T(8,128)(2,1)S(1)} %copy-done.72, bf16[784,768]{1,0:T(8,128)(2,1)S(1)} %copy-done.39), kind=kOutput, calls=%fused_computation.55 | convolution fusion | flops 3705372672 | bytes 9584640 | tf_op jit(solution)/shard_map/dot_general | solution.py:270
  380.2 9.1 %convolution_convert_fusion.2 = bf16[1536,768]{1,0:T(8,128)(2,1)} fusion(bf16[1568,1536]{1,0:T(8,128)(2,1)} %get-tuple-element.33, bf16[1568,768]{1,0:T(8,128)(2,1)} %constant_dynamic-update-slice_fusion), kind=kOutput, calls=%fused_computation.54 | convolution fusion | flops 3700555776 | bytes 9584640 | tf_op jit(solution)/shard_map/dot_general | solution.py:266
  459.4 6.8 %multiply_reduce_fusion.2 = (f32[196,6,8]{2,1,0:T(8,128)S(1)}, f32[196,6,8,8]{2,3,1,0:T(8,128)S(1)}) fusion(f32[196,6,8,8]{2,3,1,0:T(8,128)} %copy-done.1, f32[196,6,8]{2,1,0:T(8,128)} %log_add_fusion, bf16[196,8,6,64]{3,1,2,0:T(8,128)(2,1)S(1)} %copy.68, bf16[196,8,3,6,64]{4,1,3,0,2:T(8,128)(2,1)} %bitcast.224), kind=kOutput, calls=%fused_computation.36 | convolution fusion | flops 9925440 | bytes 9571072 | tf_op jit(solution)/shard_map/blhe,bmhe->bhlm/dot_general | solution.py:94
  479.7 12.1 %copy.71 = bf16[1,8,196,3,6,64]{2,1,5,4,3,0:T(8,128)(2,1)} copy(bf16[1,8,196,3,6,64]{5,1,4,2,3,0:T(8,128)(2,1)} %maximum_bitcast_fusion) | data formatting | bytes 7225344 | tf_op jit(solution)/shard_map/transpose | solution.py:38
  491.8 9.0 %reshape_reshape.30 = bf16[1568,1152]{0,1:T(8,128)(2,1)} reshape(bf16[1,8,196,3,6,64]{2,1,5,4,3,0:T(8,128)(2,1)} %copy.71) | data formatting | bytes 7225344 | tf_op jit(solution)/shard_map/reshape;reshape | solution.py:110
  500.7 6.8 %convert_bitcast_fusion.3 = bf16[8,2,96,3,192]{4,2,1,3,0:T(8,128)(2,1)S(1)} fusion(bf16[8,96,1568,1,1]{2,1,4,3,0:T(8,128)(2,1)S(1)} %bitcast.238, bf16[3,2,192,1568,1]{3,2,1,0,4:T(8,128)(2,1)} %bitcast.236), kind=kOutput, calls=%fused_computation.113 | convolution fusion | flops 2775416832 | bytes 7790592 | tf_op jit(solution)/shard_map/dot_general | solution.py:111
  536.8 39.6 %psum.7 = f32[3,768]{1,0:T(4,128)} all-reduce(f32[3,768]{1,0:T(4,128)S(1)} %pad_maximum_fusion.21), channel_id=1, replica_groups=mesh['dp'=8,'ty'=2,'core'=2] {'dp','ty','core'}, use_global_device_ids=true, to_apply=%region_21.0 | all-reduce | flops 2304 | bytes 18432 | tf_op jit(solution)/shard_map/psum | solution.py:314
  580.3 24.5 %reduce-scatter.4.cloned.1.call-done = bf16[192,768]{1,0:T(8,128)(2,1)} async-done(((bf16[1536,768]{1,0:T(8,128)(2,1)}), bf16[192,768]{1,0:T(8,128)(2,1)}) %reduce-scatter.4.cloned.1.call-update) | async-done | bytes 294928 | tf_op jit(solution)/shard_map/reduce_scatter | solution.py:194
  (356 shorter events, 290.8 us)
Async XLA Ops:
  7.2 65.1 %all-gather.4.cloned.1.call-start = ((), (), s32[]{:S(2)}) async-start(), calls=%async_computation.3 | async-start | bytes 2654208 | tf_op jit(solution)/shard_map/all_gather | solution.py:135
  9.4 8.0 %collective-permute-start.1 = (bf16[96,768]{0,1:T(8,128)(2,1)S(1)}, bf16[96,768]{0,1:T(8,128)(2,1)S(1)}, u32[]{:S(2)}, u32[]{:S(2)}) collective-permute-start(bf16[96,768]{0,1:T(8,128)(2,1)S(1)} %pad_maximum_fusion.19), channel_id=1, source_target_pairs={{0,2},{2,0},{1,3},{3,1},{4,6},{6,4},{5,7},{7,5},{8,10},{10,8},{9,1... | collective-permute-start | bytes 442376 | tf_op jit(solution)/shard_map/ppermute | solution.py:211
  18.9 114.6 %all-gather.6.cloned.1.call-start = ((), (), s32[]{:S(2)}) async-start(), calls=%async_computation.4 | async-start | bytes 2654208 | tf_op jit(solution)/shard_map/all_gather | solution.py:135
  20.4 9.2 %collective-permute-start = (bf16[784,768]{1,0:T(8,128)(2,1)S(1)}, bf16[784,768]{1,0:T(8,128)(2,1)}, u32[]{:S(2)}, u32[]{:S(2)}) collective-permute-start(bf16[784,768]{1,0:T(8,128)(2,1)S(1)} %fusion.21), channel_id=1, source_target_pairs={{0,1},{1,0},{2,3},{3,2},{4,5},{5,4},{6,7},{7,6},{8,9},{9,8},{10,11... | collective-permute-start | bytes 3612680 | tf_op jit(solution)/shard_map/ppermute | solution.py:234
  20.7 7.4 %collective-permute-start.4 = (bf16[96,768]{0,1:T(8,128)(2,1)S(1)}, bf16[96,768]{0,1:T(8,128)(2,1)S(1)}, u32[]{:S(2)}, u32[]{:S(2)}) collective-permute-start(bf16[96,768]{0,1:T(8,128)(2,1)S(1)} %pad_maximum_fusion.20), channel_id=1, source_target_pairs={{0,2},{2,0},{1,3},{3,1},{4,6},{6,4},{5,7},{7,5},{8,10},{10,8},{9,1... | collective-permute-start | bytes 442376 | tf_op jit(solution)/shard_map/ppermute | solution.py:211
  29.5 182.1 %all-gather.8.cloned.1.call-start = ((), (), s32[]{:S(2)}) async-start(), calls=%async_computation.5 | async-start | bytes 5308416 | tf_op jit(solution)/shard_map/all_gather | solution.py:152
  117.6 2.9 collective-permute-start.2
  123.0 10.5 %collective-permute-start.3 = (bf16[784,768]{1,0:T(8,128)(2,1)}, bf16[784,768]{1,0:T(8,128)(2,1)}, u32[]{:S(2)}, u32[]{:S(2)}) collective-permute-start(bf16[784,768]{1,0:T(8,128)(2,1)} %multiply_convert_fusion.8), channel_id=1, source_target_pairs={{0,1},{1,0},{2,3},{3,2},{4,5},{5,4},{6,7},{7,6},{8,9},{9,8},{10,11... | collective-permute-start | bytes 3612680 | tf_op jit(solution)/shard_map/ppermute | solution.py:234
  123.1 9.4 %collective-permute-start.7 = (bf16[96,1536]{1,0:T(8,128)(2,1)S(1)}, bf16[96,1536]{1,0:T(8,128)(2,1)S(1)}, u32[]{:S(2)}, u32[]{:S(2)}) collective-permute-start(bf16[96,1536]{1,0:T(8,128)(2,1)S(1)} %pad_maximum_fusion.18), channel_id=1, source_target_pairs={{0,2},{2,0},{1,3},{3,1},{4,6},{6,4},{5,7},{7,5},{8,10},{10,8},{9,1... | collective-permute-start | bytes 884744 | tf_op jit(solution)/shard_map/ppermute | solution.py:211
  133.4 396.1 %reduce-scatter.6.cloned.1.call-start = ((), (), s32[]{:S(2)}) async-start(), calls=%async_computation.7 | async-start | bytes 2654208 | tf_op jit(solution)/shard_map/reduce_scatter | solution.py:194
  192.6 2.9 collective-permute-start.5
  192.7 6.1 collective-permute-start.9
  197.4 14.3 %collective-permute-start.6 = (bf16[784,768]{1,0:T(8,128)(2,1)S(1)}, bf16[784,768]{1,0:T(8,128)(2,1)S(1)}, u32[]{:S(2)}, u32[]{:S(2)}) collective-permute-start(bf16[784,768]{1,0:T(8,128)(2,1)S(1)} %multiply_convert_fusion.7), channel_id=1, source_target_pairs={{0,1},{1,0},{2,3},{3,2},{4,5},{5,4},{6,7},{7,6},{8,9},{9,8},{10,11... | collective-permute-start | bytes 3612680 | tf_op jit(solution)/shard_map/ppermute | solution.py:234
  257.2 5.0 collective-permute-start.10
  261.7 3.2 collective-permute-start.8
  269.0 6.4 %collective-permute-start.11 = (bf16[784,768]{1,0:T(8,128)(2,1)}, bf16[784,768]{1,0:T(8,128)(2,1)}, u32[]{:S(2)}, u32[]{:S(2)}) collective-permute-start(bf16[784,768]{1,0:T(8,128)(2,1)} %fusion.68), channel_id=1, source_target_pairs={{0,1},{1,0},{2,3},{3,2},{4,5},{5,4},{6,7},{7,6},{8,9},{9,8},{10,11... | collective-permute-start | bytes 3612680 | tf_op jit(solution)/shard_map/ppermute | solution.py:234
  365.0 211.5 %reduce-scatter.8.cloned.1.call-start = ((), (), s32[]{:S(2)}) async-start(), calls=%async_computation.8 | async-start | bytes 5308416 | tf_op jit(solution)/shard_map/reduce_scatter | solution.py:194
  413.3 3.5 collective-permute-start.12
  416.8 187.9 %reduce-scatter.4.cloned.1.call-start = ((), (), s32[]{:S(2)}) async-start(), calls=%async_computation.6 | async-start | bytes 2654208 | tf_op jit(solution)/shard_map/reduce_scatter | solution.py:194
  426.6 8.1 %collective-permute-start.13 = (bf16[784,768]{1,0:T(8,128)(2,1)}, bf16[784,768]{1,0:T(8,128)(2,1)}, u32[]{:S(2)}, u32[]{:S(2)}) collective-permute-start(bf16[784,768]{1,0:T(8,128)(2,1)} %fusion.102), channel_id=1, source_target_pairs={{0,1},{1,0},{2,3},{3,2},{4,5},{5,4},{6,7},{7,6},{8,9},{9,8},{10,11... | collective-permute-start | bytes 3612680 | tf_op jit(solution)/shard_map/ppermute | solution.py:234
  522.8 2.9 collective-permute-start.14
  530.4 76.8 %collective-permute-start.16 = (bf16[96,768]{1,0:T(8,128)(2,1)S(1)}, bf16[96,768]{1,0:T(8,128)(2,1)S(1)}, u32[]{:S(2)}, u32[]{:S(2)}) collective-permute-start(bf16[96,768]{1,0:T(8,128)(2,1)S(1)} %slice.236), channel_id=1, source_target_pairs={{0,2},{2,0},{1,3},{3,1},{4,6},{6,4},{5,7},{7,5},{8,10},{10,8},{9,1... | collective-permute-start | bytes 442376 | tf_op jit(solution)/shard_map/ppermute | solution.py:211
  577.5 35.3 %collective-permute-start.17 = (bf16[192,768]{1,0:T(8,128)(2,1)S(1)}, bf16[192,768]{1,0:T(8,128)(2,1)S(1)}, u32[]{:S(2)}, u32[]{:S(2)}) collective-permute-start(bf16[192,768]{1,0:T(8,128)(2,1)S(1)} %slice.240), channel_id=1, source_target_pairs={{0,2},{2,0},{1,3},{3,1},{4,6},{6,4},{5,7},{7,5},{8,10},{10,8},{9,1... | collective-permute-start | bytes 884744 | tf_op jit(solution)/shard_map/ppermute | solution.py:211
  605.7 5.2 collective-permute-start.15
  (77 other events, 718.2 us)
Sparse Core Ops, SparseCore 0:
  19.0 53.2 all-gather.3
  75.1 50.3 all-gather.5
  133.5 78.0 all-gather.7
  365.2 67.9 reduce-scatter.5
  436.6 94.8 reduce-scatter.7
  534.9 69.7 reduce-scatter.3

commit v7 on v6

--- a/solution.py
+++ b/solution.py
@@ -72,7 +72,7 @@
 def attend_backward(normed, w_qkv, w_proj, grouped, summary, merged, grad_rows, temporal):
     factor = 1.0 / math.sqrt(HD)
     width_here = merged.shape[1]
-    grad_proj = jnp.dot(merged.T, grad_rows, preferred_element_type=jnp.float32)
+    grad_proj = jnp.dot(grad_rows.T, merged, preferred_element_type=jnp.float32)
     grad_merged = jnp.dot(grad_rows, w_proj.T, preferred_element_type=jnp.float32).astype(
         jnp.bfloat16
     )
@@ -153,58 +153,31 @@
     return full[:, : 2 * width], full[:, 2 * width :].T
 
 
-def scatter_grads(grads, layouts, shard_shapes):
-    ny = lax.axis_size("ty")
-    nd = lax.axis_size("dp")
-    assert ny == 2
-    flat = []
-    for g, (dp_dim, ty_dim), shard in zip(grads, layouts, shard_shapes):
-        split = []
-        for dim in range(g.ndim):
-            if dim == dp_dim:
-                split.extend([nd, shard[dim]])
-            elif dim == ty_dim:
-                split.extend([ny, shard[dim]])
-            else:
-                split.append(shard[dim])
-        parts = g.reshape(split)
-        pos = 0
-        ty_pos = dp_pos = None
-        rest = []
-        for dim in range(g.ndim):
-            if dim == dp_dim:
-                dp_pos = pos
-                rest.append(pos + 1)
-                pos += 2
-            elif dim == ty_dim:
-                ty_pos = pos
-                rest.append(pos + 1)
-                pos += 2
-            else:
-                rest.append(pos)
-                pos += 1
-        flat.append(
-            jnp.transpose(parts, [dp_pos, ty_pos] + rest)
-            .reshape(nd, ny, -1, 768)
-            .astype(jnp.bfloat16)
-        )
-    sizes = [f.shape[2] for f in flat]
-    stacked = jnp.concatenate(flat, axis=2)
-    rows = stacked.shape[2]
-    blocks = lax.psum_scatter(
-        stacked.reshape(-1, 768), "dp", scatter_dimension=0, tiled=True
-    ).reshape(ny, rows, 768)
-    return blocks, sizes, shard_shapes
-
-
-def finish_grads(blocks, sizes, shard_shapes):
-    summed = blocks[0].astype(jnp.float32) + swap_ty(blocks[1]).astype(jnp.float32)
-    out = []
-    offset = 0
-    for size, shard in zip(sizes, shard_shapes):
-        out.append(summed[offset : offset + size].reshape(shard))
-        offset += size
-    return out
+def scatter_rows(pieces):
+    flat = [p.reshape(p.shape[0], -1) for p in pieces]
+    return lax.psum_scatter(
+        jnp.concatenate(flat, axis=1).astype(jnp.bfloat16), "dp", scatter_dimension=0, tiled=True
+    )
+
+
+def finish_attention(local, qkv_shape, proj_shape):
+    rows, parts, width = qkv_shape
+    split = parts * 2 * width
+    qkv = local[:, :split].reshape(rows, parts, 2, width)
+    proj = local[:, split:]
+    half = proj.shape[1] // 2
+    mine = jnp.concatenate([qkv[:, :, 0].reshape(rows, -1), proj[:, :half]], axis=1)
+    other = jnp.concatenate([qkv[:, :, 1].reshape(rows, -1), proj[:, half:]], axis=1)
+    summed = mine.astype(jnp.float32) + swap_ty(other).astype(jnp.float32)
+    return summed[:, : parts * width].reshape(qkv_shape), summed[:, parts * width :].T.reshape(proj_shape)
+
+
+def finish_mlp(local, up_shape, down_shape):
+    width = up_shape[1]
+    mine = jnp.concatenate([local[:, :width], local[:, 2 * width : 3 * width]], axis=1)
+    other = jnp.concatenate([local[:, width : 2 * width], local[:, 3 * width :]], axis=1)
+    summed = mine.astype(jnp.float32) + swap_ty(other).astype(jnp.float32)
+    return summed[:, :width].reshape(up_shape), summed[:, width:].T.reshape(down_shape)
 
 
 def swap_ty(values):
@@ -222,10 +195,6 @@
     up_weight,
     down_weight,
 ):
-    qkv_layout = (0, 2)
-    proj_layout = (1, 0)
-    up_layout = (0, 1)
-    down_layout = (1, 0)
     time_qkv, time_proj = gather_attention(qkv_time, proj_time)
     space_qkv, space_proj = gather_attention(qkv_space, proj_space)
     up_full, down_full = gather_mlp(up_weight, down_weight)
@@ -263,15 +232,13 @@
 
     grad_after = cotangent.astype(jnp.float32)
     down_rows = spread_grads(grad_after.astype(jnp.bfloat16))
-    grad_down = jnp.dot(hidden.T, down_rows, preferred_element_type=jnp.float32)
+    grad_down = jnp.dot(down_rows.T, hidden, preferred_element_type=jnp.float32)
     grad_hidden = jnp.dot(down_rows, down_full.T, preferred_element_type=jnp.float32)
     _, gelu_back = jax.vjp(partial(jax.nn.gelu, approximate=False), hidden_pre)
     grad_pre = gelu_back(grad_hidden)[0].astype(jnp.bfloat16)
     grad_up = jnp.dot(normed_mlp.T, grad_pre, preferred_element_type=jnp.float32)
-    mlp_blocks = scatter_grads(
-        (grad_up, grad_down), (up_layout, down_layout), (up_weight.shape, down_weight.shape)
-    )
-    grad_up, grad_down = finish_grads(*mlp_blocks)
+    mlp_local = scatter_rows((grad_up, grad_down))
+    grad_up, grad_down = finish_mlp(mlp_local, up_weight.shape, down_weight.shape)
     _, norm_back = jax.vjp(normalize, after_space, norm_gains[2])
     back_rows, gain_mlp = norm_back(
         sum_grads(jnp.dot(grad_pre, up_full.T, preferred_element_type=jnp.float32))
@@ -289,24 +256,16 @@
         space_rows,
         False,
     )
-    space_blocks = scatter_grads(
-        (grad_qkv_space, grad_proj_space),
-        (qkv_layout, proj_layout),
-        (qkv_space.shape, proj_space.shape),
-    )
-    grad_qkv_space, grad_proj_space = finish_grads(*space_blocks)
+    space_local = scatter_rows((grad_qkv_space, grad_proj_space))
+    grad_qkv_space, grad_proj_space = finish_attention(space_local, qkv_space.shape, proj_space.shape)
     back_rows, gain_space = norm_back(sum_grads(grad_normed))
     grad_after = grad_after + back_rows
     time_rows = spread_grads(grad_after.astype(jnp.bfloat16))
     grad_qkv_time, grad_proj_time, grad_normed = attend_backward(
         normed_time, time_qkv, time_proj, grouped_time, summary_time, merged_time, time_rows, True
     )
-    grad_qkv_time, grad_proj_time = finish_grads(
-        *scatter_grads(
-            (grad_qkv_time, grad_proj_time),
-            (qkv_layout, proj_layout),
-            (qkv_time.shape, proj_time.shape),
-        )
+    grad_qkv_time, grad_proj_time = finish_attention(
+        scatter_rows((grad_qkv_time, grad_proj_time)), qkv_time.shape, proj_time.shape
     )
     _, norm_back = jax.vjp(normalize, inputs, norm_gains[0])
     back_rows, gain_time = norm_back(sum_grads(grad_normed))

time: 629 us -> 615 us (0.978)
  waiting for transfers between devices: 106 us -> 161 us
  local copies, waits for them, and re-layouts: 200 us -> 154 us
  other arithmetic: 70.5 us -> 52.4 us
    reduce_scatter x3, waiting for transfers between devices: 24.5 us -> 67.8 us  [scatter_rows(): lax.psum_scatter(jnp.concatenate(flat, axis=1).astype(jnp.bfloat16), 'dp'...]
    convert_element_type x12 -> x0, local copies, waits for them, and re-layouts: 37 us -> none  [scatter_grads(): flat.append(jnp.transpose(parts, [dp_pos, ty_pos] + rest).reshape(nd, ny,...]
    dot_general x4 -> x0, local copies, waits for them, and re-layouts: 16.1 us -> none  [the longest x2 8.13 us: attend_backward(): jnp.dot(normed.T, grad_mixed, preferred_element_type=jnp.float32)]
    dot_general x4 -> x0, other arithmetic: 6.83 us -> none  [the longest x2 3.59 us: attend_backward(): grad_proj = jnp.dot(merged.T, grad_rows, preferred_element_type=jnp.float32)]
    ppermute x12, waiting for transfers between devices: 6.86 us -> 13.4 us  [swap(): return lax.ppermute(values, 'core', perm=[(0, 1), (1, 0)])]
    unnamed x163 -> x144, local copies, waits for them, and re-layouts: 30.3 us -> 28.8 us
  transfers between devices with their start and end apart: 24 -> 24, of which waited for: 10 -> 15; matrix products, arithmetic and copies ran while one was open for 47% -> 39% of each run, Pallas kernels for 0% -> 0%
where the time goes in v7:
time: 615 us; the launch traced here: 608 us
  matrix products  171 us (28%)
  waiting for transfers between devices  161 us (26%)
  local copies, waits for them, and re-layouts  154 us (25%)
  other arithmetic  52.4 us (9%)
  blocking collectives  40.3 us (7%)
  between operations  15.7 us (3%)
  starting transfers between devices  13.7 us (2%)
    reduce_scatter x3, waiting for transfers between devices, scatter_rows(): lax.psum_scatter(jnp.concatenate(flat, axis=1).astype(jnp.bfloat16), 'dp'...  67.8 us
    all_gather x2, waiting for transfers between devices, gather_attention(): lax.all_gather(jnp.concatenate([qkv_local, proj_local], axis=1), 'dp', ax...  42.7 us
    psum x1, blocking collectives, per_device(): lax.psum(jnp.stack([gain_time, gain_space, gain_mlp]), ('dp', 'ty', 'core'))  40.3 us
    dot_general x1, matrix products, per_device(): jnp.dot(normed_mlp, up_full, preferred_element_type=jnp.float32)  29.7 us
    unnamed x144, local copies, waits for them, and re-layouts  28.8 us
    ppermute x6, waiting for transfers between devices, swap_ty(): return lax.ppermute(values, 'ty', perm=[(0, 1), (1, 0)])  25.4 us
    another operation x3, local copies, waits for them, and re-layouts, to_groups(): shaped = values.reshape((clip_count, FRAMES, PATCH) + trailing)  25.3 us
    another operation x3, local copies, waits for them, and re-layouts, to_groups(): return values.reshape((-1, PATCH) + trailing)  21.6 us
  transfers between devices with their start and end apart: 24, of which 15 were waited for; matrix products, arithmetic and copies ran while one was open for 39% of the time, Pallas kernels for 0%

profile of v7, /device:TPU:0, one launch (start us, length us, event | category | flops | bytes accessed | tf_op | source)
XLA Modules:
  0.0 607.6 jit_solution(6979683561146218103)
XLA Ops:
  29.6 42.7 %all-gather.4.cloned.1.call-done = bf16[768,1536]{1,0:T(8,128)(2,1)} async-done(((bf16[96,1536]{1,0:T(8,128)(2,1)}), bf16[768,1536]{1,0:T(8,128)(2,1)}) %all-gather.4.cloned.1.call-update) | async-done | bytes 2359312 | tf_op jit(solution)/shard_map/all_gather | solution.py:135
  72.3 7.1 %convolution_convert_fusion.1 = bf16[1568,1152]{1,0:T(8,128)(2,1)} fusion(bf16[768,1536]{1,0:T(8,128)(2,1)} %all-gather.4.cloned.1.call-done, bf16[784,768]{1,0:T(8,128)(2,1)} %collective-permute-done, bf16[784,768]{1,0:T(8,128)(2,1)S(1)} %fusion.21), kind=kOutput, calls=%fused_computation.25 | convolution fusion | flops 2781155328 | bytes 7790592 | tf_op jit(solution)/shard_map/dot_general | solution.py:45
  79.4 12.3 %reshape.225 = bf16[1,8,196,3,6,64]{5,4,3,2,1,0:T(8,128)(2,1)} reshape(bf16[1568,1152]{1,0:T(8,128)(2,1)} %convolution_convert_fusion.1) | data formatting | bytes 7225344 | tf_op jit(solution)/shard_map/reshape;reshape | solution.py:28
  91.7 8.4 %copy.105 = bf16[1,8,196,3,6,64]{5,1,4,2,3,0:T(8,128)(2,1)S(1)} copy(bf16[1,8,196,3,6,64]{5,4,3,2,1,0:T(8,128)(2,1)} %reshape.225) | data formatting | bytes 7225344 | tf_op jit(solution)/shard_map/reshape;reshape | solution.py:28
  125.1 7.8 %collective-permute-done.7 = bf16[96,1536]{1,0:T(8,128)(2,1)S(1)} collective-permute-done((bf16[96,1536]{1,0:T(8,128)(2,1)S(1)}, bf16[96,1536]{1,0:T(8,128)(2,1)S(1)}, u32[]{:S(2)}, u32[]{:S(2)}) %collective-permute-start.7) | collective-permute-done | bytes 294944 | tf_op jit(solution)/shard_map/ppermute | solution.py:184
  133.9 7.3 %convolution_convert_fusion = bf16[1568,1152]{1,0:T(8,128)(2,1)} fusion(bf16[768,1536]{1,0:T(8,128)(2,1)} %all-gather.6.cloned.1.call-done, bf16[784,768]{1,0:T(8,128)(2,1)} %collective-permute-done.3, bf16[784,768]{1,0:T(8,128)(2,1)} %multiply_convert_fusion.8), kind=kOutput, calls=%fused_computation.24 | convolution fusion | flops 2781155328 | bytes 7790592 | tf_op jit(solution)/shard_map/dot_general | solution.py:45
  141.2 12.0 %reshape.226 = bf16[8,196,3,6,64]{4,3,2,1,0:T(8,128)(2,1)} reshape(bf16[1568,1152]{1,0:T(8,128)(2,1)} %convolution_convert_fusion) | data formatting | bytes 7225344 | tf_op jit(solution)/shard_map/reshape;reshape | solution.py:31
  153.2 6.8 %fusion.112 = (bf16[8,196,1,6,64]{4,3,2,1,0:T(8,128)(2,1)}, bf16[8,196,1,6,64]{4,3,2,1,0:T(8,128)(2,1)}, bf16[8,196,1,6,64]{4,3,2,1,0:T(8,128)(2,1)}) fusion(bf16[8,196,3,6,64]{4,3,2,1,0:T(8,128)(2,1)} %reshape.226), kind=kLoop, calls=%fused_computation.214 | loop fusion | bytes 7225344 | tf_op jit(solution)/shard_map/slice | solution.py:64
  200.4 11.6 %all-gather.8.cloned.1.call-done = bf16[768,3072]{1,0:T(8,128)(2,1)} async-done(((bf16[96,3072]{1,0:T(8,128)(2,1)}), bf16[768,3072]{1,0:T(8,128)(2,1)}) %all-gather.8.cloned.1.call-update) | async-done | bytes 4718608 | tf_op jit(solution)/shard_map/all_gather | solution.py:152
  212.0 29.7 %multiply_convert_fusion.1 = (bf16[1568,1536]{1,0:T(8,128)(2,1)S(1)}, f32[1568,1536]{1,0:T(8,128)}, f32[1568,1536]{1,0:T(8,128)}) fusion(bf16[768,3072]{1,0:T(8,128)(2,1)} %all-gather.8.cloned.1.call-done, bf16[784,768]{1,0:T(8,128)(2,1)S(1)} %collective-permute-done.6, bf16[784,768]{1,0:T(8,128)(2,1)S(1)} %multiply_convert_fusion.7), kind=kOutput, calls=%fused_computation.8 | convolution fusion | flops 3860742144 | bytes 28852224 | tf_op jit(solution)/shard_map/dot_general | solution.py:227
  241.7 12.9 %add_convert_fusion = bf16[1568,1536]{1,0:T(8,128)(2,1)S(1)} fusion(f32[1568,1536]{1,0:T(8,128)} %get-tuple-element.34, bf16[1568,768]{1,0:T(8,128)(2,1)} %constant_dynamic-update-slice_fusion, f32[1568,1536]{1,0:T(8,128)} %get-tuple-element.63, bf16[768,3072]{1,0:T(8,128)(2,1)S(1)} %copy-done.60), kind=kOutput, calls=%fused_computation.7 | convolution fusion | flops 3733094400 | bytes 28852224 | tf_op jit(solution)/shard_map/dot_general | solution.py:236
  286.0 7.5 %fusion.67 = bf16[8,196,1,6,64]{1,4,3,0,2:T(8,128)(2,1)} fusion(bf16[8,196,6,64]{1,3,2,0:T(8,128)(2,1)} %copy.64, f32[8,6,196,196]{2,3,1,0:T(8,128)} %copy-done, f32[8,6,196]{2,1,0:T(8,128)S(1)} %log_add_fusion.1), kind=kOutput, calls=%fused_computation.141 | convolution fusion | flops 242161920 | bytes 9821952 | tf_op jit(solution)/shard_map/bhlm,blhe->bmhe/dot_general | solution.py:88
  293.5 7.4 %multiply_reduce_fusion = (f32[8,6,196]{2,1,0:T(8,128)S(1)}, f32[8,6,196,196]{2,3,1,0:T(8,128)}) fusion(f32[8,6,196,196]{2,3,1,0:T(8,128)} %copy-done, f32[8,6,196]{2,1,0:T(8,128)S(1)} %log_add_fusion.1, bf16[8,196,6,64]{1,3,2,0:T(8,128)(2,1)S(1)} %copy-done.17, bf16[8,196,1,6,64]{1,4,3,0,2:T(8,128)(2,1)S(1)} %copy-done.24), kind=kOutput, calls=%fused_computation.2 | convolution fusion | flops 243394368 | bytes 17235456 | tf_op jit(solution)/shard_map/blhe,bmhe->bhlm/dot_general | solution.py:94
  300.9 11.4 %multiply_convert_fusion = bf16[8,6,196,196]{2,3,1,0:T(8,128)(2,1)} fusion(f32[8,6,196,196]{2,3,1,0:T(8,128)} %get-tuple-element.65, f32[8,6,196,196]{2,3,1,0:T(8,128)} %copy-done, f32[8,6,196]{2,1,0:T(8,128)S(1)} %get-tuple-element.64, f32[8,6,196]{2,1,0:T(8,128)S(1)} %log_add_fusion.1), kind=kLoop, calls=%fused_computation.1 | loop fusion | flops 9219840 | bytes 18514944 | tf_op jit(solution)/shard_map/convert_element_type | solution.py:100
  325.1 9.0 %convert_element_type.179 = bf16[1568,1152]{0,1:T(8,128)(2,1)} reshape(bf16[8,196,3,6,64]{1,0,4,3,2:T(8,128)(2,1)} %copy.69) | data formatting | bytes 7225344 | tf_op jit(solution)/shard_map/convert_element_type | solution.py:109
  345.1 7.6 %convolution_convert_fusion.5 = bf16[768,1536]{1,0:T(8,128)(2,1)S(1)} fusion(bf16[1568,1536]{1,0:T(8,128)(2,1)} %copy-done.65, bf16[784,768]{1,0:T(8,128)(2,1)} %copy-done.61, bf16[784,768]{1,0:T(8,128)(2,1)} %copy-done.31), kind=kOutput, calls=%fused_computation.57 | convolution fusion | flops 3705372672 | bytes 9584640 | tf_op jit(solution)/shard_map/dot_general | solution.py:239
  352.6 7.6 %convolution_convert_fusion.4 = bf16[768,1536]{1,0:T(8,128)(2,1)S(1)} fusion(bf16[1568,768]{1,0:T(8,128)(2,1)} %constant_dynamic-update-slice_fusion, bf16[1568,1536]{1,0:T(8,128)(2,1)} %copy-done.64), kind=kOutput, calls=%fused_computation.56 | convolution fusion | flops 3700555776 | bytes 9584640 | tf_op jit(solution)/shard_map/dot_general | solution.py:235
  363.2 6.3 %fusion.58 = f32[1568,768]{1,0:T(8,128)S(1)} fusion(bf16[1568,1152]{0,1:T(8,128)(2,1)} %convert_element_type.179, bf16[768,1536]{1,0:T(8,128)(2,1)} %all-gather.6.cloned.1.call-done), kind=kOutput, calls=%fused_computation.132 | convolution fusion | flops 2774532096 | bytes 10420224 | tf_op jit(solution)/shard_map/dot_general | solution.py:114
  396.9 7.6 %multiply_reduce_fusion.2 = (f32[196,6,8]{2,1,0:T(8,128)S(1)}, f32[196,6,8,8]{2,3,1,0:T(8,128)S(1)}) fusion(f32[196,6,8,8]{2,3,1,0:T(8,128)} %copy-done.1, f32[196,6,8]{2,1,0:T(8,128)} %log_add_fusion, bf16[196,8,6,64]{3,1,2,0:T(8,128)(2,1)} %copy.71, bf16[196,8,3,6,64]{4,1,3,0,2:T(8,128)(2,1)} %bitcast.157), kind=kOutput, calls=%fused_computation.36 | convolution fusion | flops 9925440 | bytes 10775296 | tf_op jit(solution)/shard_map/blhe,bmhe->bhlm/dot_general | solution.py:94
  418.0 12.1 %copy.74 = bf16[1,8,196,3,6,64]{2,1,5,4,3,0:T(8,128)(2,1)} copy(bf16[1,8,196,3,6,64]{5,1,4,2,3,0:T(8,128)(2,1)} %maximum_bitcast_fusion) | data formatting | bytes 7225344 | tf_op jit(solution)/shard_map/transpose | solution.py:38
  430.1 9.0 %reshape_reshape.28 = bf16[1568,1152]{0,1:T(8,128)(2,1)} reshape(bf16[1,8,196,3,6,64]{2,1,5,4,3,0:T(8,128)(2,1)} %copy.74) | data formatting | bytes 7225344 | tf_op jit(solution)/shard_map/reshape;reshape | solution.py:110
  449.8 6.1 %fusion.61 = f32[1568,768]{1,0:T(8,128)S(1)} fusion(bf16[1568,1152]{0,1:T(8,128)(2,1)} %reshape_reshape.28, bf16[768,1536]{1,0:T(8,128)(2,1)} %all-gather.4.cloned.1.call-done), kind=kOutput, calls=%fused_computation.135 | convolution fusion | flops 2774532096 | bytes 10420224 | tf_op jit(solution)/shard_map/dot_general | solution.py:114
  472.3 40.3 %psum.7 = f32[3,768]{1,0:T(4,128)} all-reduce(f32[3,768]{1,0:T(4,128)S(1)} %pad_maximum_fusion.32), channel_id=1, replica_groups=mesh['dp'=8,'ty'=2,'core'=2] {'dp','ty','core'}, use_global_device_ids=true, to_apply=%region_21.0 | all-reduce | flops 2304 | bytes 18432 | tf_op jit(solution)/shard_map/psum | solution.py:273
  517.3 67.8 %reduce-scatter.4.cloned.1.call-done = bf16[96,1536]{1,0:T(8,128)(2,1)} async-done(((bf16[768,1536]{1,0:T(8,128)(2,1)}), bf16[96,1536]{1,0:T(8,128)(2,1)}) %reduce-scatter.4.cloned.1.call-update) | async-done | bytes 294928 | tf_op jit(solution)/shard_map/reduce_scatter | solution.py:158
  (329 shorter events, 233.7 us)
Async XLA Ops:
  7.2 65.1 %all-gather.4.cloned.1.call-start = ((), (), s32[]{:S(2)}) async-start(), calls=%async_computation.3 | async-start | bytes 2654208 | tf_op jit(solution)/shard_map/all_gather | solution.py:135
  9.4 8.0 %collective-permute-start.1 = (bf16[96,768]{0,1:T(8,128)(2,1)S(1)}, bf16[96,768]{0,1:T(8,128)(2,1)S(1)}, u32[]{:S(2)}, u32[]{:S(2)}) collective-permute-start(bf16[96,768]{0,1:T(8,128)(2,1)S(1)} %pad_maximum_fusion.28), channel_id=1, source_target_pairs={{0,2},{2,0},{1,3},{3,1},{4,6},{6,4},{5,7},{7,5},{8,10},{10,8},{9,1... | collective-permute-start | bytes 442376 | tf_op jit(solution)/shard_map/ppermute | solution.py:184
  18.9 115.0 %all-gather.6.cloned.1.call-start = ((), (), s32[]{:S(2)}) async-start(), calls=%async_computation.4 | async-start | bytes 2654208 | tf_op jit(solution)/shard_map/all_gather | solution.py:135
  20.4 9.2 %collective-permute-start = (bf16[784,768]{1,0:T(8,128)(2,1)S(1)}, bf16[784,768]{1,0:T(8,128)(2,1)}, u32[]{:S(2)}, u32[]{:S(2)}) collective-permute-start(bf16[784,768]{1,0:T(8,128)(2,1)S(1)} %fusion.21), channel_id=1, source_target_pairs={{0,1},{1,0},{2,3},{3,2},{4,5},{5,4},{6,7},{7,6},{8,9},{9,8},{10,11... | collective-permute-start | bytes 3612680 | tf_op jit(solution)/shard_map/ppermute | solution.py:203
  20.7 7.4 %collective-permute-start.4 = (bf16[96,768]{0,1:T(8,128)(2,1)S(1)}, bf16[96,768]{0,1:T(8,128)(2,1)S(1)}, u32[]{:S(2)}, u32[]{:S(2)}) collective-permute-start(bf16[96,768]{0,1:T(8,128)(2,1)S(1)} %pad_maximum_fusion.29), channel_id=1, source_target_pairs={{0,2},{2,0},{1,3},{3,1},{4,6},{6,4},{5,7},{7,5},{8,10},{10,8},{9,1... | collective-permute-start | bytes 442376 | tf_op jit(solution)/shard_map/ppermute | solution.py:184
  29.5 182.4 %all-gather.8.cloned.1.call-start = ((), (), s32[]{:S(2)}) async-start(), calls=%async_computation.5 | async-start | bytes 5308416 | tf_op jit(solution)/shard_map/all_gather | solution.py:152
  118.0 2.9 collective-permute-start.2
  123.3 10.5 %collective-permute-start.3 = (bf16[784,768]{1,0:T(8,128)(2,1)}, bf16[784,768]{1,0:T(8,128)(2,1)}, u32[]{:S(2)}, u32[]{:S(2)}) collective-permute-start(bf16[784,768]{1,0:T(8,128)(2,1)} %multiply_convert_fusion.8), channel_id=1, source_target_pairs={{0,1},{1,0},{2,3},{3,2},{4,5},{5,4},{6,7},{7,6},{8,9},{9,8},{10,11... | collective-permute-start | bytes 3612680 | tf_op jit(solution)/shard_map/ppermute | solution.py:203
  123.5 9.4 %collective-permute-start.7 = (bf16[96,1536]{1,0:T(8,128)(2,1)S(1)}, bf16[96,1536]{1,0:T(8,128)(2,1)S(1)}, u32[]{:S(2)}, u32[]{:S(2)}) collective-permute-start(bf16[96,1536]{1,0:T(8,128)(2,1)S(1)} %pad_maximum_fusion.26), channel_id=1, source_target_pairs={{0,2},{2,0},{1,3},{3,1},{4,6},{6,4},{5,7},{7,5},{8,10},{10,8},{9,1... | collective-permute-start | bytes 884744 | tf_op jit(solution)/shard_map/ppermute | solution.py:184
  133.8 329.0 %reduce-scatter.6.cloned.1.call-start = ((), (), s32[]{:S(2)}) async-start(), calls=%async_computation.7 | async-start | bytes 2654208 | tf_op jit(solution)/shard_map/reduce_scatter | solution.py:158
  193.0 2.9 collective-permute-start.5
  193.1 6.1 %collective-permute-start.9 = (bf16[784,768]{1,0:T(8,128)(2,1)S(1)}, bf16[784,768]{1,0:T(8,128)(2,1)S(1)}, u32[]{:S(2)}, u32[]{:S(2)}) collective-permute-start(bf16[784,768]{1,0:T(8,128)(2,1)S(1)} %copy-done.14), channel_id=1, source_target_pairs={{0,1},{1,0},{2,3},{3,2},{4,5},{5,4},{6,7},{7,6},{8,9},{9,8},{10,11... | collective-permute-start | bytes 3612680 | tf_op jit(solution)/shard_map/ppermute | solution.py:203
  197.8 14.2 %collective-permute-start.6 = (bf16[784,768]{1,0:T(8,128)(2,1)S(1)}, bf16[784,768]{1,0:T(8,128)(2,1)S(1)}, u32[]{:S(2)}, u32[]{:S(2)}) collective-permute-start(bf16[784,768]{1,0:T(8,128)(2,1)S(1)} %multiply_convert_fusion.7), channel_id=1, source_target_pairs={{0,1},{1,0},{2,3},{3,2},{4,5},{5,4},{6,7},{7,6},{8,9},{9,8},{10,11... | collective-permute-start | bytes 3612680 | tf_op jit(solution)/shard_map/ppermute | solution.py:203
  258.8 4.8 collective-permute-start.10
  263.0 3.1 collective-permute-start.8
  268.8 2.9 collective-permute-start.11
  345.0 171.2 %reduce-scatter.8.cloned.1.call-start = ((), (), s32[]{:S(2)}) async-start(), calls=%async_computation.8 | async-start | bytes 5308416 | tf_op jit(solution)/shard_map/reduce_scatter | solution.py:158
  362.9 222.2 %reduce-scatter.4.cloned.1.call-start = ((), (), s32[]{:S(2)}) async-start(), calls=%async_computation.6 | async-start | bytes 2654208 | tf_op jit(solution)/shard_map/reduce_scatter | solution.py:158
  369.7 2.9 collective-permute-start.12
  376.2 2.9 collective-permute-start.13
  456.0 3.0 collective-permute-start.14
  465.7 47.2 %collective-permute-start.16 = (bf16[96,768]{0,1:T(8,128)(2,1)S(1)}, bf16[96,768]{0,1:T(8,128)(2,1)S(1)}, u32[]{:S(2)}, u32[]{:S(2)}) collective-permute-start(bf16[96,768]{0,1:T(8,128)(2,1)S(1)} %pad_maximum_fusion.31), channel_id=1, source_target_pairs={{0,2},{2,0},{1,3},{3,1},{4,6},{6,4},{5,7},{7,5},{8,10},{10,8},{9,1... | collective-permute-start | bytes 442376 | tf_op jit(solution)/shard_map/ppermute | solution.py:184
  588.1 7.8 %collective-permute-start.15 = (bf16[96,768]{0,1:T(8,128)(2,1)S(1)}, bf16[96,768]{0,1:T(8,128)(2,1)S(1)}, u32[]{:S(2)}, u32[]{:S(2)}) collective-permute-start(bf16[96,768]{0,1:T(8,128)(2,1)S(1)} %pad_maximum_fusion.30), channel_id=1, source_target_pairs={{0,2},{2,0},{1,3},{3,1},{4,6},{6,4},{5,7},{7,5},{8,10},{10,8},{9,1... | collective-permute-start | bytes 442376 | tf_op jit(solution)/shard_map/ppermute | solution.py:184
  589.7 9.9 %collective-permute-start.17 = (bf16[96,1536]{1,0:T(8,128)(2,1)S(1)}, bf16[96,1536]{1,0:T(8,128)(2,1)S(1)}, u32[]{:S(2)}, u32[]{:S(2)}) collective-permute-start(bf16[96,1536]{1,0:T(8,128)(2,1)S(1)} %pad_maximum_fusion.27), channel_id=1, source_target_pairs={{0,2},{2,0},{1,3},{3,1},{4,6},{6,4},{5,7},{7,5},{8,10},{10,8},{9,1... | collective-permute-start | bytes 884744 | tf_op jit(solution)/shard_map/ppermute | solution.py:184
  (68 other events, 601.5 us)
Sparse Core Ops, SparseCore 0:
  19.0 53.2 all-gather.3
  75.1 50.3 all-gather.5
  133.9 78.0 all-gather.7
  345.1 68.0 reduce-scatter.5
  416.7 95.7 reduce-scatter.7
  515.9 69.2 reduce-scatter.3

commit v8 on v7

--- a/solution.py
+++ b/solution.py
@@ -119,13 +119,16 @@
     return (grad_qkv, grad_proj, grad_normed)
 
 
-def gather_attention(qkv_shard, proj_shard):
+def attention_shards(qkv_shard, proj_shard):
     rows, parts, width = qkv_shard.shape
-    mine = jnp.concatenate(
+    return jnp.concatenate(
         [qkv_shard.astype(jnp.bfloat16).reshape(rows, parts * width), proj_shard.astype(jnp.bfloat16).T],
         axis=1,
     )
-    other = swap_ty(mine)
+
+
+def gather_attention(mine, other, qkv_shape):
+    rows, parts, width = qkv_shape
     split = parts * width
     qkv_local = jnp.stack(
         [mine[:, :split].reshape(rows, parts, width), other[:, :split].reshape(rows, parts, width)],
@@ -140,12 +143,11 @@
     return w_qkv, w_proj
 
 
-def gather_mlp(up_shard, down_shard):
-    width = up_shard.shape[1]
-    mine = jnp.concatenate(
-        [up_shard.astype(jnp.bfloat16), down_shard.astype(jnp.bfloat16).T], axis=1
-    )
-    other = swap_ty(mine)
+def mlp_shards(up_shard, down_shard):
+    return jnp.concatenate([up_shard.astype(jnp.bfloat16), down_shard.astype(jnp.bfloat16).T], axis=1)
+
+
+def gather_mlp(mine, other, width):
     local = jnp.concatenate(
         [mine[:, :width], other[:, :width], mine[:, width:], other[:, width:]], axis=1
     )
@@ -195,9 +197,15 @@
     up_weight,
     down_weight,
 ):
-    time_qkv, time_proj = gather_attention(qkv_time, proj_time)
-    space_qkv, space_proj = gather_attention(qkv_space, proj_space)
-    up_full, down_full = gather_mlp(up_weight, down_weight)
+    time_mine = attention_shards(qkv_time, proj_time)
+    time_qkv, time_proj = gather_attention(time_mine, swap_ty(time_mine), qkv_time.shape)
+    later = jnp.concatenate(
+        [attention_shards(qkv_space, proj_space), mlp_shards(up_weight, down_weight)], axis=1
+    )
+    later_other = swap_ty(later)
+    cut = later.shape[1] - 2 * up_weight.shape[1]
+    space_qkv, space_proj = gather_attention(later[:, :cut], later_other[:, :cut], qkv_space.shape)
+    up_full, down_full = gather_mlp(later[:, cut:], later_other[:, cut:], up_weight.shape[1])
 
     def swap(values):
         return lax.ppermute(values, "core", perm=[(0, 1), (1, 0)])

time: 615 us -> 609 us (level)
  waiting for transfers between devices: 161 us -> 154 us
    all_gather x2, waiting for transfers between devices: 42.7 us -> 36.1 us  [gather_attention(): lax.all_gather(jnp.concatenate([qkv_local, proj_local], axis=1), 'dp', ax...]
    ppermute x6 -> x5, waiting for transfers between devices: 25.4 us -> 23 us  [swap_ty(): return lax.ppermute(values, 'ty', perm=[(0, 1), (1, 0)])]
    unnamed x144 -> x148, local copies, waits for them, and re-layouts: 28.8 us -> 28.2 us
  transfers between devices with their start and end apart: 24 -> 23, of which waited for: 15 -> 16; matrix products, arithmetic and copies ran while one was open for 39% -> 40% of each run, Pallas kernels for 0% -> 0%
where the time goes in v8:
time: 609 us; the launch traced here: 601 us
  matrix products  171 us (28%)
  local copies, waits for them, and re-layouts  154 us (25%)
  waiting for transfers between devices  154 us (25%)
  other arithmetic  53.3 us (9%)
  blocking collectives  41.3 us (7%)
  between operations  15.6 us (3%)
  starting transfers between devices  12.3 us (2%)
    reduce_scatter x3, waiting for transfers between devices, scatter_rows(): lax.psum_scatter(jnp.concatenate(flat, axis=1).astype(jnp.bfloat16), 'dp'...  66.6 us
    psum x1, blocking collectives, per_device(): lax.psum(jnp.stack([gain_time, gain_space, gain_mlp]), ('dp', 'ty', 'core'))  41.3 us
    all_gather x2, waiting for transfers between devices, gather_attention(): lax.all_gather(jnp.concatenate([qkv_local, proj_local], axis=1), 'dp', ax...  36.1 us
    dot_general x1, matrix products, per_device(): jnp.dot(normed_mlp, up_full, preferred_element_type=jnp.float32)  29.7 us
    unnamed x148, local copies, waits for them, and re-layouts  28.2 us
    another operation x3, local copies, waits for them, and re-layouts, to_groups(): shaped = values.reshape((clip_count, FRAMES, PATCH) + trailing)  25.3 us
    ppermute x5, waiting for transfers between devices, swap_ty(): return lax.ppermute(values, 'ty', perm=[(0, 1), (1, 0)])  23 us
    another operation x3, local copies, waits for them, and re-layouts, to_groups(): return values.reshape((-1, PATCH) + trailing)  21.6 us
  transfers between devices with their start and end apart: 23, of which 16 were waited for; matrix products, arithmetic and copies ran while one was open for 40% of the time, Pallas kernels for 0%

profile of v8, /device:TPU:0, one launch (start us, length us, event | category | flops | bytes accessed | tf_op | source)
XLA Modules:
  0.0 601.3 jit_solution(2730374673272744595)
XLA Ops:
  24.5 11.0 %collective-permute-done.4 = bf16[96,2304]{1,0:T(8,128)(2,1)S(1)} collective-permute-done((bf16[96,2304]{1,0:T(8,128)(2,1)}, bf16[96,2304]{1,0:T(8,128)(2,1)S(1)}, u32[]{:S(2)}, u32[]{:S(2)}) %collective-permute-start.4) | collective-permute-done | bytes 442400 | tf_op jit(solution)/shard_map/ppermute | solution.py:186
  37.2 35.1 %all-gather.4.cloned.1.call-done = bf16[768,1536]{1,0:T(8,128)(2,1)} async-done(((bf16[96,1536]{1,0:T(8,128)(2,1)}), bf16[768,1536]{1,0:T(8,128)(2,1)}) %all-gather.4.cloned.1.call-update) | async-done | bytes 2359312 | tf_op jit(solution)/shard_map/all_gather | solution.py:138
  72.3 7.1 %convolution_convert_fusion.1 = bf16[1568,1152]{1,0:T(8,128)(2,1)} fusion(bf16[768,1536]{1,0:T(8,128)(2,1)} %all-gather.4.cloned.1.call-done, bf16[784,768]{1,0:T(8,128)(2,1)} %collective-permute-done, bf16[784,768]{1,0:T(8,128)(2,1)S(1)} %fusion.21), kind=kOutput, calls=%fused_computation.25 | convolution fusion | flops 2781155328 | bytes 7790592 | tf_op jit(solution)/shard_map/dot_general | solution.py:45
  79.4 12.3 %reshape.225 = bf16[1,8,196,3,6,64]{5,4,3,2,1,0:T(8,128)(2,1)} reshape(bf16[1568,1152]{1,0:T(8,128)(2,1)} %convolution_convert_fusion.1) | data formatting | bytes 7225344 | tf_op jit(solution)/shard_map/reshape;reshape | solution.py:28
  91.7 8.4 %copy.152 = bf16[1,8,196,3,6,64]{5,1,4,2,3,0:T(8,128)(2,1)S(1)} copy(bf16[1,8,196,3,6,64]{5,4,3,2,1,0:T(8,128)(2,1)} %reshape.225) | data formatting | bytes 7225344 | tf_op jit(solution)/shard_map/reshape;reshape | solution.py:28
  126.5 7.3 %convolution_convert_fusion = bf16[1568,1152]{1,0:T(8,128)(2,1)} fusion(bf16[768,1536]{1,0:T(8,128)(2,1)} %all-gather.6.cloned.1.call-done, bf16[784,768]{1,0:T(8,128)(2,1)} %collective-permute-done.3, bf16[784,768]{1,0:T(8,128)(2,1)} %multiply_convert_fusion.8), kind=kOutput, calls=%fused_computation.24 | convolution fusion | flops 2781155328 | bytes 7790592 | tf_op jit(solution)/shard_map/dot_general | solution.py:45
  133.9 12.0 %reshape.226 = bf16[8,196,3,6,64]{4,3,2,1,0:T(8,128)(2,1)} reshape(bf16[1568,1152]{1,0:T(8,128)(2,1)} %convolution_convert_fusion) | data formatting | bytes 7225344 | tf_op jit(solution)/shard_map/reshape;reshape | solution.py:31
  145.8 6.8 %fusion.112 = (bf16[8,196,1,6,64]{4,3,2,1,0:T(8,128)(2,1)}, bf16[8,196,1,6,64]{4,3,2,1,0:T(8,128)(2,1)}, bf16[8,196,1,6,64]{4,3,2,1,0:T(8,128)(2,1)}) fusion(bf16[8,196,3,6,64]{4,3,2,1,0:T(8,128)(2,1)} %reshape.226), kind=kLoop, calls=%fused_computation.212 | loop fusion | bytes 7225344 | tf_op jit(solution)/shard_map/slice | solution.py:64
  193.1 13.0 %all-gather.8.cloned.1.call-done = bf16[768,3072]{1,0:T(8,128)(2,1)} async-done(((bf16[96,3072]{1,0:T(8,128)(2,1)}), bf16[768,3072]{1,0:T(8,128)(2,1)}) %all-gather.8.cloned.1.call-update) | async-done | bytes 4718608 | tf_op jit(solution)/shard_map/all_gather | solution.py:154
  206.1 29.7 %multiply_convert_fusion.1 = (bf16[1568,1536]{1,0:T(8,128)(2,1)S(1)}, f32[1568,1536]{1,0:T(8,128)}, f32[1568,1536]{1,0:T(8,128)}) fusion(bf16[768,3072]{1,0:T(8,128)(2,1)} %all-gather.8.cloned.1.call-done, bf16[784,768]{1,0:T(8,128)(2,1)S(1)} %collective-permute-done.6, bf16[784,768]{1,0:T(8,128)(2,1)S(1)} %multiply_convert_fusion.7), kind=kOutput, calls=%fused_computation.8 | convolution fusion | flops 3860742144 | bytes 28852224 | tf_op jit(solution)/shard_map/dot_general | solution.py:235
  235.8 12.9 %add_convert_fusion = bf16[1568,1536]{1,0:T(8,128)(2,1)S(1)} fusion(f32[1568,1536]{1,0:T(8,128)} %get-tuple-element.43, bf16[1568,768]{1,0:T(8,128)(2,1)} %constant_dynamic-update-slice_fusion, f32[1568,1536]{1,0:T(8,128)} %get-tuple-element.72, bf16[768,3072]{1,0:T(8,128)(2,1)S(1)} %copy-done.61), kind=kOutput, calls=%fused_computation.7 | convolution fusion | flops 3733094400 | bytes 28852224 | tf_op jit(solution)/shard_map/dot_general | solution.py:244
  280.1 7.5 %fusion.67 = bf16[8,196,1,6,64]{1,4,3,0,2:T(8,128)(2,1)} fusion(bf16[8,196,6,64]{1,3,2,0:T(8,128)(2,1)} %copy.110, f32[8,6,196,196]{2,3,1,0:T(8,128)} %copy-done, f32[8,6,196]{2,1,0:T(8,128)S(1)} %log_add_fusion.1), kind=kOutput, calls=%fused_computation.141 | convolution fusion | flops 242161920 | bytes 9821952 | tf_op jit(solution)/shard_map/bhlm,blhe->bmhe/dot_general | solution.py:88
  287.7 7.4 %multiply_reduce_fusion = (f32[8,6,196]{2,1,0:T(8,128)S(1)}, f32[8,6,196,196]{2,3,1,0:T(8,128)}) fusion(f32[8,6,196,196]{2,3,1,0:T(8,128)} %copy-done, f32[8,6,196]{2,1,0:T(8,128)S(1)} %log_add_fusion.1, bf16[8,196,6,64]{1,3,2,0:T(8,128)(2,1)S(1)} %copy-done.17, bf16[8,196,1,6,64]{1,4,3,0,2:T(8,128)(2,1)S(1)} %copy-done.24), kind=kOutput, calls=%fused_computation.2 | convolution fusion | flops 243394368 | bytes 17235456 | tf_op jit(solution)/shard_map/blhe,bmhe->bhlm/dot_general | solution.py:94
  295.1 11.4 %multiply_convert_fusion = bf16[8,6,196,196]{2,3,1,0:T(8,128)(2,1)} fusion(f32[8,6,196,196]{2,3,1,0:T(8,128)} %get-tuple-element.74, f32[8,6,196,196]{2,3,1,0:T(8,128)} %copy-done, f32[8,6,196]{2,1,0:T(8,128)S(1)} %get-tuple-element.73, f32[8,6,196]{2,1,0:T(8,128)S(1)} %log_add_fusion.1), kind=kLoop, calls=%fused_computation.1 | loop fusion | flops 9219840 | bytes 18514944 | tf_op jit(solution)/shard_map/convert_element_type | solution.py:100
  319.2 9.0 %convert_element_type.179 = bf16[1568,1152]{0,1:T(8,128)(2,1)} reshape(bf16[8,196,3,6,64]{1,0,4,3,2:T(8,128)(2,1)} %copy.115) | data formatting | bytes 7225344 | tf_op jit(solution)/shard_map/convert_element_type | solution.py:109
  339.2 7.6 %convolution_convert_fusion.5 = bf16[768,1536]{1,0:T(8,128)(2,1)S(1)} fusion(bf16[1568,1536]{1,0:T(8,128)(2,1)} %copy-done.66, bf16[784,768]{1,0:T(8,128)(2,1)} %copy-done.62, bf16[784,768]{1,0:T(8,128)(2,1)} %copy-done.31), kind=kOutput, calls=%fused_computation.57 | convolution fusion | flops 3705372672 | bytes 9584640 | tf_op jit(solution)/shard_map/dot_general | solution.py:247
  346.8 7.6 %convolution_convert_fusion.4 = bf16[768,1536]{1,0:T(8,128)(2,1)S(1)} fusion(bf16[1568,768]{1,0:T(8,128)(2,1)} %constant_dynamic-update-slice_fusion, bf16[1568,1536]{1,0:T(8,128)(2,1)} %copy-done.65), kind=kOutput, calls=%fused_computation.56 | convolution fusion | flops 3700555776 | bytes 9584640 | tf_op jit(solution)/shard_map/dot_general | solution.py:243
  357.4 6.2 %fusion.58 = f32[1568,768]{1,0:T(8,128)S(1)} fusion(bf16[1568,1152]{0,1:T(8,128)(2,1)} %convert_element_type.179, bf16[768,1536]{1,0:T(8,128)(2,1)} %all-gather.6.cloned.1.call-done), kind=kOutput, calls=%fused_computation.132 | convolution fusion | flops 2774532096 | bytes 10420224 | tf_op jit(solution)/shard_map/dot_general | solution.py:114
  390.9 7.5 %multiply_reduce_fusion.2 = (f32[196,6,8]{2,1,0:T(8,128)S(1)}, f32[196,6,8,8]{2,3,1,0:T(8,128)S(1)}) fusion(f32[196,6,8,8]{2,3,1,0:T(8,128)} %copy-done.1, f32[196,6,8]{2,1,0:T(8,128)} %log_add_fusion, bf16[196,8,6,64]{3,1,2,0:T(8,128)(2,1)} %copy.117, bf16[196,8,3,6,64]{4,1,3,0,2:T(8,128)(2,1)} %bitcast.158), kind=kOutput, calls=%fused_computation.36 | convolution fusion | flops 9925440 | bytes 10775296 | tf_op jit(solution)/shard_map/blhe,bmhe->bhlm/dot_general | solution.py:94
  412.0 12.1 %copy.120 = bf16[1,8,196,3,6,64]{2,1,5,4,3,0:T(8,128)(2,1)} copy(bf16[1,8,196,3,6,64]{5,1,4,2,3,0:T(8,128)(2,1)} %maximum_bitcast_fusion) | data formatting | bytes 7225344 | tf_op jit(solution)/shard_map/transpose | solution.py:38
  424.1 9.0 %reshape_reshape.28 = bf16[1568,1152]{0,1:T(8,128)(2,1)} reshape(bf16[1,8,196,3,6,64]{2,1,5,4,3,0:T(8,128)(2,1)} %copy.120) | data formatting | bytes 7225344 | tf_op jit(solution)/shard_map/reshape;reshape | solution.py:110
  443.8 6.1 %fusion.61 = f32[1568,768]{1,0:T(8,128)S(1)} fusion(bf16[1568,1152]{0,1:T(8,128)(2,1)} %reshape_reshape.28, bf16[768,1536]{1,0:T(8,128)(2,1)} %all-gather.4.cloned.1.call-done), kind=kOutput, calls=%fused_computation.135 | convolution fusion | flops 2774532096 | bytes 10420224 | tf_op jit(solution)/shard_map/dot_general | solution.py:114
  466.4 41.3 %psum.7 = f32[3,768]{1,0:T(4,128)} all-reduce(f32[3,768]{1,0:T(4,128)S(1)} %pad_maximum_fusion.30), channel_id=1, replica_groups=mesh['dp'=8,'ty'=2,'core'=2] {'dp','ty','core'}, use_global_device_ids=true, to_apply=%region_21.0 | all-reduce | flops 2304 | bytes 18432 | tf_op jit(solution)/shard_map/psum | solution.py:281
  512.4 66.6 %reduce-scatter.4.cloned.1.call-done = bf16[96,1536]{1,0:T(8,128)(2,1)} async-done(((bf16[768,1536]{1,0:T(8,128)(2,1)}), bf16[96,1536]{1,0:T(8,128)(2,1)}) %reduce-scatter.4.cloned.1.call-update) | async-done | bytes 294928 | tf_op jit(solution)/shard_map/reduce_scatter | solution.py:160
  (328 shorter events, 230.7 us)
Async XLA Ops:
  7.2 65.1 %all-gather.4.cloned.1.call-start = ((), (), s32[]{:S(2)}) async-start(), calls=%async_computation.3 | async-start | bytes 2654208 | tf_op jit(solution)/shard_map/all_gather | solution.py:138
  9.4 8.0 %collective-permute-start.1 = (bf16[96,768]{0,1:T(8,128)(2,1)S(1)}, bf16[96,768]{0,1:T(8,128)(2,1)S(1)}, u32[]{:S(2)}, u32[]{:S(2)}) collective-permute-start(bf16[96,768]{0,1:T(8,128)(2,1)S(1)} %pad_maximum_fusion.27), channel_id=1, source_target_pairs={{0,2},{2,0},{1,3},{3,1},{4,6},{6,4},{5,7},{7,5},{8,10},{10,8},{9,1... | collective-permute-start | bytes 442376 | tf_op jit(solution)/shard_map/ppermute | solution.py:186
  18.9 106.6 %all-gather.6.cloned.1.call-start = ((), (), s32[]{:S(2)}) async-start(), calls=%async_computation.4 | async-start | bytes 2654208 | tf_op jit(solution)/shard_map/all_gather | solution.py:138
  19.0 102.9 %copy-start.54 = (f32[768]{0:T(1024)}, f32[768]{0:T(1024)S(1)}, u32[]{:S(2)}) copy-start(f32[768]{0:T(1024)S(1)} %get-tuple-element.35) | copy-start | bytes 9220
  20.3 16.9 %collective-permute-start = (bf16[784,768]{1,0:T(8,128)(2,1)S(1)}, bf16[784,768]{1,0:T(8,128)(2,1)}, u32[]{:S(2)}, u32[]{:S(2)}) collective-permute-start(bf16[784,768]{1,0:T(8,128)(2,1)S(1)} %fusion.21), channel_id=1, source_target_pairs={{0,1},{1,0},{2,3},{3,2},{4,5},{5,4},{6,7},{7,6},{8,9},{9,8},{10,11... | collective-permute-start | bytes 3612680 | tf_op jit(solution)/shard_map/ppermute | solution.py:211
  22.7 12.8 %collective-permute-start.4 = (bf16[96,2304]{1,0:T(8,128)(2,1)}, bf16[96,2304]{1,0:T(8,128)(2,1)S(1)}, u32[]{:S(2)}, u32[]{:S(2)}) collective-permute-start(bf16[96,2304]{1,0:T(8,128)(2,1)} %concatenate.75), channel_id=1, source_target_pairs={{0,2},{2,0},{1,3},{3,1},{4,6},{6,4},{5,7},{7,5},{8,10},{10,8},{9,1... | collective-permute-start | bytes 1327112 | tf_op jit(solution)/shard_map/ppermute | solution.py:186
  37.1 169.0 %all-gather.8.cloned.1.call-start = ((), (), s32[]{:S(2)}) async-start(), calls=%async_computation.5 | async-start | bytes 5308416 | tf_op jit(solution)/shard_map/all_gather | solution.py:154
  118.0 2.9 collective-permute-start.2
  123.3 3.2 collective-permute-start.3
  124.4 332.4 %reduce-scatter.6.cloned.1.call-start = ((), (), s32[]{:S(2)}) async-start(), calls=%async_computation.7 | async-start | bytes 2654208 | tf_op jit(solution)/shard_map/reduce_scatter | solution.py:160
  185.8 2.9 collective-permute-start.5
  185.9 6.1 %collective-permute-start.8 = (bf16[784,768]{1,0:T(8,128)(2,1)S(1)}, bf16[784,768]{1,0:T(8,128)(2,1)S(1)}, u32[]{:S(2)}, u32[]{:S(2)}) collective-permute-start(bf16[784,768]{1,0:T(8,128)(2,1)S(1)} %copy-done.14), channel_id=1, source_target_pairs={{0,1},{1,0},{2,3},{3,2},{4,5},{5,4},{6,7},{7,6},{8,9},{9,8},{10,11... | collective-permute-start | bytes 3612680 | tf_op jit(solution)/shard_map/ppermute | solution.py:211
  190.6 15.5 %collective-permute-start.6 = (bf16[784,768]{1,0:T(8,128)(2,1)S(1)}, bf16[784,768]{1,0:T(8,128)(2,1)S(1)}, u32[]{:S(2)}, u32[]{:S(2)}) collective-permute-start(bf16[784,768]{1,0:T(8,128)(2,1)S(1)} %multiply_convert_fusion.7), channel_id=1, source_target_pairs={{0,1},{1,0},{2,3},{3,2},{4,5},{5,4},{6,7},{7,6},{8,9},{9,8},{10,11... | collective-permute-start | bytes 3612680 | tf_op jit(solution)/shard_map/ppermute | solution.py:211
  252.9 4.8 collective-permute-start.9
  257.2 3.1 collective-permute-start.7
  263.0 2.9 collective-permute-start.10
  339.1 172.1 %reduce-scatter.8.cloned.1.call-start = ((), (), s32[]{:S(2)}) async-start(), calls=%async_computation.8 | async-start | bytes 5308416 | tf_op jit(solution)/shard_map/reduce_scatter | solution.py:160
  357.1 221.9 %reduce-scatter.4.cloned.1.call-start = ((), (), s32[]{:S(2)}) async-start(), calls=%async_computation.6 | async-start | bytes 2654208 | tf_op jit(solution)/shard_map/reduce_scatter | solution.py:160
  363.7 2.9 collective-permute-start.11
  370.3 2.9 collective-permute-start.12
  450.1 3.0 collective-permute-start.13
  459.8 48.3 %collective-permute-start.15 = (bf16[96,768]{0,1:T(8,128)(2,1)S(1)}, bf16[96,768]{0,1:T(8,128)(2,1)S(1)}, u32[]{:S(2)}, u32[]{:S(2)}) collective-permute-start(bf16[96,768]{0,1:T(8,128)(2,1)S(1)} %pad_maximum_fusion.29), channel_id=1, source_target_pairs={{0,2},{2,0},{1,3},{3,1},{4,6},{6,4},{5,7},{7,5},{8,10},{10,8},{9,1... | collective-permute-start | bytes 442376 | tf_op jit(solution)/shard_map/ppermute | solution.py:186
  582.0 7.8 %collective-permute-start.14 = (bf16[96,768]{0,1:T(8,128)(2,1)S(1)}, bf16[96,768]{0,1:T(8,128)(2,1)S(1)}, u32[]{:S(2)}, u32[]{:S(2)}) collective-permute-start(bf16[96,768]{0,1:T(8,128)(2,1)S(1)} %pad_maximum_fusion.28), channel_id=1, source_target_pairs={{0,2},{2,0},{1,3},{3,1},{4,6},{6,4},{5,7},{7,5},{8,10},{10,8},{9,1... | collective-permute-start | bytes 442376 | tf_op jit(solution)/shard_map/ppermute | solution.py:186
  583.6 9.7 %collective-permute-start.16 = (bf16[96,1536]{1,0:T(8,128)(2,1)S(1)}, bf16[96,1536]{1,0:T(8,128)(2,1)S(1)}, u32[]{:S(2)}, u32[]{:S(2)}) collective-permute-start(bf16[96,1536]{1,0:T(8,128)(2,1)S(1)} %pad_maximum_fusion.26), channel_id=1, source_target_pairs={{0,2},{2,0},{1,3},{3,1},{4,6},{6,4},{5,7},{7,5},{8,10},{10,8},{9,1... | collective-permute-start | bytes 884744 | tf_op jit(solution)/shard_map/ppermute | solution.py:186
  (68 other events, 509.7 us)
Sparse Core Ops, SparseCore 0:
  19.0 53.2 all-gather.3
  75.1 50.3 all-gather.5
  128.2 77.8 all-gather.7
  339.3 67.8 reduce-scatter.5
  410.6 95.8 reduce-scatter.7
  509.9 69.1 reduce-scatter.3

commit v9 on v8

--- a/solution.py
+++ b/solution.py
@@ -1,4 +1,3 @@
-from functools import partial
 import math
 
 import jax
@@ -233,7 +232,11 @@
     )
     normed_mlp = spread_rows(normalize(after_space, norm_gains[2]).astype(jnp.bfloat16))
     hidden_pre = jnp.dot(normed_mlp, up_full, preferred_element_type=jnp.float32)
-    hidden = jax.nn.gelu(hidden_pre, approximate=False).astype(jnp.bfloat16)
+    half_cdf = 0.5 * lax.erfc(-hidden_pre * math.sqrt(0.5))
+    hidden = (hidden_pre * half_cdf).astype(jnp.bfloat16)
+    gelu_slope = half_cdf + hidden_pre * jnp.exp(-0.5 * hidden_pre * hidden_pre) * (
+        1.0 / math.sqrt(2.0 * math.pi)
+    )
     output = (
         after_space + sum_rows(jnp.dot(hidden, down_full, preferred_element_type=jnp.float32))
     ).astype(jnp.bfloat16)
@@ -242,8 +245,7 @@
     down_rows = spread_grads(grad_after.astype(jnp.bfloat16))
     grad_down = jnp.dot(down_rows.T, hidden, preferred_element_type=jnp.float32)
     grad_hidden = jnp.dot(down_rows, down_full.T, preferred_element_type=jnp.float32)
-    _, gelu_back = jax.vjp(partial(jax.nn.gelu, approximate=False), hidden_pre)
-    grad_pre = gelu_back(grad_hidden)[0].astype(jnp.bfloat16)
+    grad_pre = (grad_hidden * gelu_slope).astype(jnp.bfloat16)
     grad_up = jnp.dot(normed_mlp.T, grad_pre, preferred_element_type=jnp.float32)
     mlp_local = scatter_rows((grad_up, grad_down))
     grad_up, grad_down = finish_mlp(mlp_local, up_weight.shape, down_weight.shape)

time: 609 us -> 608 us (level)
    unnamed x148 -> x140, local copies, waits for them, and re-layouts: 28.2 us -> 28.1 us
where the time goes in v9:
time: 608 us; the launch traced here: 600 us
  matrix products  170 us (28%)
  waiting for transfers between devices  156 us (26%)
  local copies, waits for them, and re-layouts  154 us (25%)
  other arithmetic  53.2 us (9%)
  blocking collectives  40.3 us (7%)
  between operations  15.6 us (3%)
  starting transfers between devices  12.2 us (2%)
    reduce_scatter x3, waiting for transfers between devices, scatter_rows(): lax.psum_scatter(jnp.concatenate(flat, axis=1).astype(jnp.bfloat16), 'dp'...  68 us
    psum x1, blocking collectives, per_device(): lax.psum(jnp.stack([gain_time, gain_space, gain_mlp]), ('dp', 'ty', 'core'))  40.3 us
    all_gather x2, waiting for transfers between devices, gather_attention(): lax.all_gather(jnp.concatenate([qkv_local, proj_local], axis=1), 'dp', ax...  36.2 us
    dot_general x1, matrix products, per_device(): jnp.dot(normed_mlp, up_full, preferred_element_type=jnp.float32)  29.6 us
    unnamed x140, local copies, waits for them, and re-layouts  28.1 us
    another operation x3, local copies, waits for them, and re-layouts, to_groups(): shaped = values.reshape((clip_count, FRAMES, PATCH) + trailing)  25.3 us
    ppermute x5, waiting for transfers between devices, swap_ty(): return lax.ppermute(values, 'ty', perm=[(0, 1), (1, 0)])  23 us
    another operation x3, local copies, waits for them, and re-layouts, to_groups(): return values.reshape((-1, PATCH) + trailing)  21.6 us
  transfers between devices with their start and end apart: 23, of which 16 were waited for; matrix products, arithmetic and copies ran while one was open for 40% of the time, Pallas kernels for 0%

profile of v9, /device:TPU:0, one launch (start us, length us, event | category | flops | bytes accessed | tf_op | source)
XLA Modules:
  0.0 600.4 jit_solution(8372026355020946805)
XLA Ops:
  24.5 11.0 %collective-permute-done.4 = bf16[96,2304]{1,0:T(8,128)(2,1)S(1)} collective-permute-done((bf16[96,2304]{1,0:T(8,128)(2,1)}, bf16[96,2304]{1,0:T(8,128)(2,1)S(1)}, u32[]{:S(2)}, u32[]{:S(2)}) %collective-permute-start.4) | collective-permute-done | bytes 442400 | tf_op jit(solution)/shard_map/ppermute | solution.py:185
  37.2 35.1 %all-gather.4.cloned.1.call-done = bf16[768,1536]{1,0:T(8,128)(2,1)} async-done(((bf16[96,1536]{1,0:T(8,128)(2,1)}), bf16[768,1536]{1,0:T(8,128)(2,1)}) %all-gather.4.cloned.1.call-update) | async-done | bytes 2359312 | tf_op jit(solution)/shard_map/all_gather | solution.py:137
  72.3 7.1 %convolution_convert_fusion.1 = bf16[1568,1152]{1,0:T(8,128)(2,1)} fusion(bf16[768,1536]{1,0:T(8,128)(2,1)} %all-gather.4.cloned.1.call-done, bf16[784,768]{1,0:T(8,128)(2,1)} %collective-permute-done, bf16[784,768]{1,0:T(8,128)(2,1)S(1)} %fusion.29), kind=kOutput, calls=%fused_computation.33 | convolution fusion | flops 2781155328 | bytes 7790592 | tf_op jit(solution)/shard_map/dot_general | solution.py:44
  79.4 12.2 %reshape.225 = bf16[1,8,196,3,6,64]{5,4,3,2,1,0:T(8,128)(2,1)} reshape(bf16[1568,1152]{1,0:T(8,128)(2,1)} %convolution_convert_fusion.1) | data formatting | bytes 7225344 | tf_op jit(solution)/shard_map/reshape;reshape | solution.py:27
  91.6 8.4 %copy.152 = bf16[1,8,196,3,6,64]{5,1,4,2,3,0:T(8,128)(2,1)S(1)} copy(bf16[1,8,196,3,6,64]{5,4,3,2,1,0:T(8,128)(2,1)} %reshape.225) | data formatting | bytes 7225344 | tf_op jit(solution)/shard_map/reshape;reshape | solution.py:27
  126.5 7.3 %convolution_convert_fusion = bf16[1568,1152]{1,0:T(8,128)(2,1)} fusion(bf16[768,1536]{1,0:T(8,128)(2,1)} %all-gather.6.cloned.1.call-done, bf16[784,768]{1,0:T(8,128)(2,1)} %collective-permute-done.3, bf16[784,768]{1,0:T(8,128)(2,1)} %multiply_convert_fusion.8), kind=kOutput, calls=%fused_computation.32 | convolution fusion | flops 2781155328 | bytes 7790592 | tf_op jit(solution)/shard_map/dot_general | solution.py:44
  133.8 11.9 %reshape.226 = bf16[8,196,3,6,64]{4,3,2,1,0:T(8,128)(2,1)} reshape(bf16[1568,1152]{1,0:T(8,128)(2,1)} %convolution_convert_fusion) | data formatting | bytes 7225344 | tf_op jit(solution)/shard_map/reshape;reshape | solution.py:30
  145.7 6.8 %fusion.120 = (bf16[8,196,1,6,64]{4,3,2,1,0:T(8,128)(2,1)}, bf16[8,196,1,6,64]{4,3,2,1,0:T(8,128)(2,1)}, bf16[8,196,1,6,64]{4,3,2,1,0:T(8,128)(2,1)}) fusion(bf16[8,196,3,6,64]{4,3,2,1,0:T(8,128)(2,1)} %reshape.226), kind=kLoop, calls=%fused_computation.220 | loop fusion | bytes 7225344 | tf_op jit(solution)/shard_map/slice | solution.py:63
  192.8 13.3 %all-gather.8.cloned.1.call-done = bf16[768,3072]{1,0:T(8,128)(2,1)} async-done(((bf16[96,3072]{1,0:T(8,128)(2,1)}), bf16[768,3072]{1,0:T(8,128)(2,1)}) %all-gather.8.cloned.1.call-update) | async-done | bytes 4718608 | tf_op jit(solution)/shard_map/all_gather | solution.py:153
  206.1 29.6 %multiply_convert_fusion.1 = (bf16[1568,1536]{1,0:T(8,128)(2,1)S(1)}, f32[1568,1536]{1,0:T(8,128)}, f32[1568,1536]{1,0:T(8,128)}) fusion(bf16[768,3072]{1,0:T(8,128)(2,1)} %all-gather.8.cloned.1.call-done, bf16[784,768]{1,0:T(8,128)(2,1)S(1)} %collective-permute-done.6, bf16[784,768]{1,0:T(8,128)(2,1)S(1)} %multiply_convert_fusion.7), kind=kOutput, calls=%fused_computation.15 | convolution fusion | flops 3860742144 | bytes 28852224 | tf_op jit(solution)/shard_map/dot_general | solution.py:234
  235.8 11.8 %fusion.7 = bf16[1568,1536]{1,0:T(8,128)(2,1)S(1)} fusion(f32[1568,1536]{1,0:T(8,128)} %get-tuple-element.43, f32[1568,1536]{1,0:T(8,128)} %get-tuple-element.72, bf16[1568,768]{1,0:T(8,128)(2,1)} %constant_dynamic-update-slice_fusion, bf16[768,3072]{1,0:T(8,128)(2,1)S(1)} %copy-done.57), kind=kOutput, calls=%fused_computation.14 | convolution fusion | flops 3716235264 | bytes 28852224 | tf_op jit(solution)/shard_map/dot_general | solution.py:247
  278.9 7.5 %fusion.75 = bf16[8,196,1,6,64]{1,4,3,0,2:T(8,128)(2,1)} fusion(bf16[8,196,6,64]{1,3,2,0:T(8,128)(2,1)} %copy.110, f32[8,6,196,196]{2,3,1,0:T(8,128)} %copy-done, f32[8,6,196]{2,1,0:T(8,128)S(1)} %log_add_fusion.1), kind=kOutput, calls=%fused_computation.149 | convolution fusion | flops 242161920 | bytes 9821952 | tf_op jit(solution)/shard_map/bhlm,blhe->bmhe/dot_general | solution.py:87
  286.5 7.4 %multiply_reduce_fusion = (f32[8,6,196]{2,1,0:T(8,128)S(1)}, f32[8,6,196,196]{2,3,1,0:T(8,128)}) fusion(f32[8,6,196,196]{2,3,1,0:T(8,128)} %copy-done, f32[8,6,196]{2,1,0:T(8,128)S(1)} %log_add_fusion.1, bf16[8,196,6,64]{1,3,2,0:T(8,128)(2,1)S(1)} %copy-done.17, bf16[8,196,1,6,64]{1,4,3,0,2:T(8,128)(2,1)S(1)} %copy-done.24), kind=kOutput, calls=%fused_computation.3 | convolution fusion | flops 243394368 | bytes 17235456 | tf_op jit(solution)/shard_map/blhe,bmhe->bhlm/dot_general | solution.py:93
  293.9 11.4 %multiply_convert_fusion = bf16[8,6,196,196]{2,3,1,0:T(8,128)(2,1)} fusion(f32[8,6,196,196]{2,3,1,0:T(8,128)} %get-tuple-element.74, f32[8,6,196,196]{2,3,1,0:T(8,128)} %copy-done, f32[8,6,196]{2,1,0:T(8,128)S(1)} %get-tuple-element.73, f32[8,6,196]{2,1,0:T(8,128)S(1)} %log_add_fusion.1), kind=kLoop, calls=%fused_computation.2 | loop fusion | flops 9219840 | bytes 18514944 | tf_op jit(solution)/shard_map/convert_element_type | solution.py:99
  318.0 9.0 %convert_element_type.179 = bf16[1568,1152]{0,1:T(8,128)(2,1)} reshape(bf16[8,196,3,6,64]{1,0,4,3,2:T(8,128)(2,1)} %copy.115) | data formatting | bytes 7225344 | tf_op jit(solution)/shard_map/convert_element_type | solution.py:108
  338.0 7.6 %convolution_convert_fusion.5 = bf16[768,1536]{1,0:T(8,128)(2,1)S(1)} fusion(bf16[1568,1536]{1,0:T(8,128)(2,1)} %copy-done.61, bf16[784,768]{1,0:T(8,128)(2,1)} %copy-done.58, bf16[784,768]{1,0:T(8,128)(2,1)} %copy-done.31), kind=kOutput, calls=%fused_computation.65 | convolution fusion | flops 3705372672 | bytes 9584640 | tf_op jit(solution)/shard_map/dot_general | solution.py:249
  345.6 7.6 %convolution_convert_fusion.4 = bf16[768,1536]{1,0:T(8,128)(2,1)S(1)} fusion(bf16[1568,768]{1,0:T(8,128)(2,1)} %constant_dynamic-update-slice_fusion, bf16[1568,1536]{1,0:T(8,128)(2,1)} %copy-done.62), kind=kOutput, calls=%fused_computation.64 | convolution fusion | flops 3700555776 | bytes 9584640 | tf_op jit(solution)/shard_map/dot_general | solution.py:246
  356.2 6.2 %fusion.66 = f32[1568,768]{1,0:T(8,128)S(1)} fusion(bf16[1568,1152]{0,1:T(8,128)(2,1)} %convert_element_type.179, bf16[768,1536]{1,0:T(8,128)(2,1)} %all-gather.6.cloned.1.call-done), kind=kOutput, calls=%fused_computation.140 | convolution fusion | flops 2774532096 | bytes 10420224 | tf_op jit(solution)/shard_map/dot_general | solution.py:113
  389.8 7.5 %multiply_reduce_fusion.2 = (f32[196,6,8]{2,1,0:T(8,128)S(1)}, f32[196,6,8,8]{2,3,1,0:T(8,128)S(1)}) fusion(f32[196,6,8,8]{2,3,1,0:T(8,128)} %copy-done.1, f32[196,6,8]{2,1,0:T(8,128)} %log_add_fusion, bf16[196,8,6,64]{3,1,2,0:T(8,128)(2,1)} %copy.117, bf16[196,8,3,6,64]{4,1,3,0,2:T(8,128)(2,1)} %bitcast.158), kind=kOutput, calls=%fused_computation.44 | convolution fusion | flops 9925440 | bytes 10775296 | tf_op jit(solution)/shard_map/blhe,bmhe->bhlm/dot_general | solution.py:93
  410.8 12.1 %copy.120 = bf16[1,8,196,3,6,64]{2,1,5,4,3,0:T(8,128)(2,1)} copy(bf16[1,8,196,3,6,64]{5,1,4,2,3,0:T(8,128)(2,1)} %maximum_bitcast_fusion) | data formatting | bytes 7225344 | tf_op jit(solution)/shard_map/transpose | solution.py:37
  422.9 9.0 %reshape_reshape.28 = bf16[1568,1152]{0,1:T(8,128)(2,1)} reshape(bf16[1,8,196,3,6,64]{2,1,5,4,3,0:T(8,128)(2,1)} %copy.120) | data formatting | bytes 7225344 | tf_op jit(solution)/shard_map/reshape;reshape | solution.py:109
  442.6 6.1 %fusion.69 = f32[1568,768]{1,0:T(8,128)S(1)} fusion(bf16[1568,1152]{0,1:T(8,128)(2,1)} %reshape_reshape.28, bf16[768,1536]{1,0:T(8,128)(2,1)} %all-gather.4.cloned.1.call-done), kind=kOutput, calls=%fused_computation.143 | convolution fusion | flops 2774532096 | bytes 10420224 | tf_op jit(solution)/shard_map/dot_general | solution.py:113
  465.1 40.3 %psum.7 = f32[3,768]{1,0:T(4,128)} all-reduce(f32[3,768]{1,0:T(4,128)S(1)} %pad_maximum_fusion.30), channel_id=1, replica_groups=mesh['dp'=8,'ty'=2,'core'=2] {'dp','ty','core'}, use_global_device_ids=true, to_apply=%region_21.0 | all-reduce | flops 2304 | bytes 18432 | tf_op jit(solution)/shard_map/psum | solution.py:283
  510.2 67.9 %reduce-scatter.4.cloned.1.call-done = bf16[96,1536]{1,0:T(8,128)(2,1)} async-done(((bf16[768,1536]{1,0:T(8,128)(2,1)}), bf16[96,1536]{1,0:T(8,128)(2,1)}) %reduce-scatter.4.cloned.1.call-update) | async-done | bytes 294928 | tf_op jit(solution)/shard_map/reduce_scatter | solution.py:159
  (320 shorter events, 230.4 us)
Async XLA Ops:
  7.2 65.1 %all-gather.4.cloned.1.call-start = ((), (), s32[]{:S(2)}) async-start(), calls=%async_computation.3 | async-start | bytes 2654208 | tf_op jit(solution)/shard_map/all_gather | solution.py:137
  9.4 8.0 %collective-permute-start.1 = (bf16[96,768]{0,1:T(8,128)(2,1)S(1)}, bf16[96,768]{0,1:T(8,128)(2,1)S(1)}, u32[]{:S(2)}, u32[]{:S(2)}) collective-permute-start(bf16[96,768]{0,1:T(8,128)(2,1)S(1)} %pad_maximum_fusion.27), channel_id=1, source_target_pairs={{0,2},{2,0},{1,3},{3,1},{4,6},{6,4},{5,7},{7,5},{8,10},{10,8},{9,1... | collective-permute-start | bytes 442376 | tf_op jit(solution)/shard_map/ppermute | solution.py:185
  18.9 106.6 %all-gather.6.cloned.1.call-start = ((), (), s32[]{:S(2)}) async-start(), calls=%async_computation.4 | async-start | bytes 2654208 | tf_op jit(solution)/shard_map/all_gather | solution.py:137
  19.0 102.8 %copy-start.50 = (f32[768]{0:T(1024)}, f32[768]{0:T(1024)S(1)}, u32[]{:S(2)}) copy-start(f32[768]{0:T(1024)S(1)} %get-tuple-element.35) | copy-start | bytes 9220
  20.3 16.9 %collective-permute-start = (bf16[784,768]{1,0:T(8,128)(2,1)S(1)}, bf16[784,768]{1,0:T(8,128)(2,1)}, u32[]{:S(2)}, u32[]{:S(2)}) collective-permute-start(bf16[784,768]{1,0:T(8,128)(2,1)S(1)} %fusion.29), channel_id=1, source_target_pairs={{0,1},{1,0},{2,3},{3,2},{4,5},{5,4},{6,7},{7,6},{8,9},{9,8},{10,11... | collective-permute-start | bytes 3612680 | tf_op jit(solution)/shard_map/ppermute | solution.py:210
  22.7 12.8 %collective-permute-start.4 = (bf16[96,2304]{1,0:T(8,128)(2,1)}, bf16[96,2304]{1,0:T(8,128)(2,1)S(1)}, u32[]{:S(2)}, u32[]{:S(2)}) collective-permute-start(bf16[96,2304]{1,0:T(8,128)(2,1)} %concatenate.75), channel_id=1, source_target_pairs={{0,2},{2,0},{1,3},{3,1},{4,6},{6,4},{5,7},{7,5},{8,10},{10,8},{9,1... | collective-permute-start | bytes 1327112 | tf_op jit(solution)/shard_map/ppermute | solution.py:185
  37.1 169.0 %all-gather.8.cloned.1.call-start = ((), (), s32[]{:S(2)}) async-start(), calls=%async_computation.5 | async-start | bytes 5308416 | tf_op jit(solution)/shard_map/all_gather | solution.py:153
  117.9 2.9 collective-permute-start.2
  123.2 3.2 collective-permute-start.3
  124.3 331.3 %reduce-scatter.6.cloned.1.call-start = ((), (), s32[]{:S(2)}) async-start(), calls=%async_computation.7 | async-start | bytes 2654208 | tf_op jit(solution)/shard_map/reduce_scatter | solution.py:159
  185.5 2.9 collective-permute-start.5
  185.6 6.1 %collective-permute-start.8 = (bf16[784,768]{1,0:T(8,128)(2,1)S(1)}, bf16[784,768]{1,0:T(8,128)(2,1)S(1)}, u32[]{:S(2)}, u32[]{:S(2)}) collective-permute-start(bf16[784,768]{1,0:T(8,128)(2,1)S(1)} %copy-done.14), channel_id=1, source_target_pairs={{0,1},{1,0},{2,3},{3,2},{4,5},{5,4},{6,7},{7,6},{8,9},{9,8},{10,11... | collective-permute-start | bytes 3612680 | tf_op jit(solution)/shard_map/ppermute | solution.py:210
  190.3 15.8 %collective-permute-start.6 = (bf16[784,768]{1,0:T(8,128)(2,1)S(1)}, bf16[784,768]{1,0:T(8,128)(2,1)S(1)}, u32[]{:S(2)}, u32[]{:S(2)}) collective-permute-start(bf16[784,768]{1,0:T(8,128)(2,1)S(1)} %multiply_convert_fusion.7), channel_id=1, source_target_pairs={{0,1},{1,0},{2,3},{3,2},{4,5},{5,4},{6,7},{7,6},{8,9},{9,8},{10,11... | collective-permute-start | bytes 3612680 | tf_op jit(solution)/shard_map/ppermute | solution.py:210
  251.7 4.8 collective-permute-start.9
  256.0 3.1 collective-permute-start.7
  261.8 2.9 collective-permute-start.10
  337.9 171.1 %reduce-scatter.8.cloned.1.call-start = ((), (), s32[]{:S(2)}) async-start(), calls=%async_computation.8 | async-start | bytes 5308416 | tf_op jit(solution)/shard_map/reduce_scatter | solution.py:159
  355.9 222.2 %reduce-scatter.4.cloned.1.call-start = ((), (), s32[]{:S(2)}) async-start(), calls=%async_computation.6 | async-start | bytes 2654208 | tf_op jit(solution)/shard_map/reduce_scatter | solution.py:159
  362.6 2.9 collective-permute-start.11
  369.2 2.9 collective-permute-start.12
  448.9 3.0 collective-permute-start.13
  458.6 47.2 %collective-permute-start.15 = (bf16[96,768]{0,1:T(8,128)(2,1)S(1)}, bf16[96,768]{0,1:T(8,128)(2,1)S(1)}, u32[]{:S(2)}, u32[]{:S(2)}) collective-permute-start(bf16[96,768]{0,1:T(8,128)(2,1)S(1)} %pad_maximum_fusion.29), channel_id=1, source_target_pairs={{0,2},{2,0},{1,3},{3,1},{4,6},{6,4},{5,7},{7,5},{8,10},{10,8},{9,1... | collective-permute-start | bytes 442376 | tf_op jit(solution)/shard_map/ppermute | solution.py:185
  581.1 7.8 %collective-permute-start.14 = (bf16[96,768]{0,1:T(8,128)(2,1)S(1)}, bf16[96,768]{0,1:T(8,128)(2,1)S(1)}, u32[]{:S(2)}, u32[]{:S(2)}) collective-permute-start(bf16[96,768]{0,1:T(8,128)(2,1)S(1)} %pad_maximum_fusion.28), channel_id=1, source_target_pairs={{0,2},{2,0},{1,3},{3,1},{4,6},{6,4},{5,7},{7,5},{8,10},{10,8},{9,1... | collective-permute-start | bytes 442376 | tf_op jit(solution)/shard_map/ppermute | solution.py:185
  582.7 9.7 %collective-permute-start.16 = (bf16[96,1536]{1,0:T(8,128)(2,1)S(1)}, bf16[96,1536]{1,0:T(8,128)(2,1)S(1)}, u32[]{:S(2)}, u32[]{:S(2)}) collective-permute-start(bf16[96,1536]{1,0:T(8,128)(2,1)S(1)} %pad_maximum_fusion.26), channel_id=1, source_target_pairs={{0,2},{2,0},{1,3},{3,1},{4,6},{6,4},{5,7},{7,5},{8,10},{10,8},{9,1... | collective-permute-start | bytes 884744 | tf_op jit(solution)/shard_map/ppermute | solution.py:185
  (64 other events, 500.5 us)
Sparse Core Ops, SparseCore 0:
  19.0 53.2 all-gather.3
  75.1 50.3 all-gather.5
  128.2 77.8 all-gather.7
  338.1 67.8 reduce-scatter.5
  409.5 95.8 reduce-scatter.7
  508.7 69.3 reduce-scatter.3

commit v10 on v8

--- a/solution.py
+++ b/solution.py
@@ -151,8 +151,36 @@
     local = jnp.concatenate(
         [mine[:, :width], other[:, :width], mine[:, width:], other[:, width:]], axis=1
     )
-    full = lax.all_gather(local, "dp", axis=0, tiled=True)
+    full = ring_gather(local)
     return full[:, : 2 * width], full[:, 2 * width :].T
+
+
+DP_RING = (0, 2, 4, 6, 7, 5, 3, 1)
+
+
+def ring_gather(local):
+    count = lax.axis_size("dp")
+    if count != len(DP_RING):
+        return lax.all_gather(local, "dp", axis=0, tiled=True)
+    ring = jnp.array(DP_RING, jnp.int32)
+    place = jnp.array([DP_RING.index(d) for d in range(count)], jnp.int32)
+    forward = [(DP_RING[i], DP_RING[(i + 1) % count]) for i in range(count)]
+    backward = [(DP_RING[(i + 1) % count], DP_RING[i]) for i in range(count)]
+    here = place[lax.axis_index("dp")]
+    blocks = [local]
+    owners = [ring[here]]
+    ahead = behind = local
+    for step in range(1, count // 2 + 1):
+        ahead = lax.ppermute(ahead, "dp", forward)
+        blocks.append(ahead)
+        owners.append(ring[(here - step) % count])
+        if step < count - count // 2:
+            behind = lax.ppermute(behind, "dp", backward)
+            blocks.append(behind)
+            owners.append(ring[(here + step) % count])
+    order = jnp.zeros((count,), jnp.int32).at[jnp.stack(owners)].set(jnp.arange(count, dtype=jnp.int32))
+    stacked = jnp.stack(blocks)
+    return jnp.take(stacked, order, axis=0).reshape(count * local.shape[0], local.shape[1])
 
 
 def scatter_rows(pieces):

time: 609 us -> 632 us (1.038)
  waiting for transfers between devices: 154 us -> 126 us
  local copies, waits for them, and re-layouts: 154 us -> 180 us
  starting transfers between devices: 12.3 us -> 28.7 us
  between operations: 15.6 us -> 22.1 us
    all_gather x2, waiting for transfers between devices: 36.1 us -> 13 us  [gather_attention(): lax.all_gather(jnp.concatenate([qkv_local, proj_local], axis=1), 'dp', ax...]
    ppermute x0 -> x7, waiting for transfers between devices: none -> 23 us  [the longest x4 21 us: ring_gather(): ahead = lax.ppermute(ahead, 'dp', forward)]
    ppermute x0 -> x7, starting transfers between devices: none -> 16.5 us  [the longest x4 16 us: ring_gather(): ahead = lax.ppermute(ahead, 'dp', forward)]
    all_gather x1 -> x0, waiting for transfers between devices: 13 us -> none  [gather_mlp(): full = lax.all_gather(local, 'dp', axis=0, tiled=True)]
    unnamed x148 -> x158, local copies, waits for them, and re-layouts: 28.2 us -> 39.5 us
    ppermute x5, waiting for transfers between devices: 23 us -> 11.9 us  [swap_ty(): return lax.ppermute(values, 'ty', perm=[(0, 1), (1, 0)])]
    another operation x0 -> x2, local copies, waits for them, and re-layouts: none -> 7.05 us  [the longest x1 5.13 us: ring_gather(): jnp.stack(owners)]
  transfers between devices with their start and end apart: 23 -> 29, of which waited for: 16 -> 13; matrix products, arithmetic and copies ran while one was open for 40% -> 43% of each run, Pallas kernels for 0% -> 0%
where the time goes in v10:
time: 632 us; the launch traced here: 623 us
  local copies, waits for them, and re-layouts  180 us (28%)
  matrix products  167 us (26%)
  waiting for transfers between devices  126 us (20%)
  other arithmetic  58.4 us (9%)
  blocking collectives  41.2 us (7%)
  starting transfers between devices  28.7 us (5%)
  between operations  22.1 us (3%)
    reduce_scatter x3, waiting for transfers between devices, scatter_rows(): lax.psum_scatter(jnp.concatenate(flat, axis=1).astype(jnp.bfloat16), 'dp'...  67.7 us
    psum x1, blocking collectives, per_device(): lax.psum(jnp.stack([gain_time, gain_space, gain_mlp]), ('dp', 'ty', 'core'))  41.2 us
    unnamed x158, local copies, waits for them, and re-layouts  39.5 us
    dot_general x1, matrix products, per_device(): jnp.dot(normed_mlp, up_full, preferred_element_type=jnp.float32)  26.7 us
    another operation x3, local copies, waits for them, and re-layouts, to_groups(): shaped = values.reshape((clip_count, FRAMES, PATCH) + trailing)  25 us
    another operation x3, local copies, waits for them, and re-layouts, to_groups(): return values.reshape((-1, PATCH) + trailing)  21.6 us
    ppermute x4, waiting for transfers between devices, ring_gather(): ahead = lax.ppermute(ahead, 'dp', forward)  21 us
    transpose x2, local copies, waits for them, and re-layouts, from_groups(): jnp.swapaxes(values.reshape((clip_count, PATCH, FRAMES) + trailing), 1, 2)  16.2 us
  transfers between devices with their start and end apart: 29, of which 13 were waited for; matrix products, arithmetic and copies ran while one was open for 43% of the time, Pallas kernels for 0%

profile of v10, /device:TPU:0, one launch (start us, length us, event | category | flops | bytes accessed | tf_op | source)
XLA Modules:
  0.0 622.6 jit_solution(5373446075845795110)
XLA Ops:
  46.5 12.9 %collective-permute-done.7 = bf16[96,3072]{1,0:T(8,128)(2,1)} collective-permute-done((bf16[96,3072]{1,0:T(8,128)(2,1)S(1)}, bf16[96,3072]{1,0:T(8,128)(2,1)}, u32[]{:S(2)}, u32[]{:S(2)}) %collective-permute-start.7) | collective-permute-done | bytes 589856 | tf_op jit(solution)/shard_map/ppermute | solution.py:174
  59.4 6.3 %collective-permute-start.9 = (bf16[96,3072]{1,0:T(8,128)(2,1)}, bf16[96,3072]{1,0:T(8,128)(2,1)}, u32[]{:S(2)}, u32[]{:S(2)}) collective-permute-start(bf16[96,3072]{1,0:T(8,128)(2,1)} %collective-permute-done.7), channel_id=1, source_target_pairs={{0,8},{8,16},{16,24},{24,28},{28,20},{20,12},{12,4},{4,0},{1,9},{9... | collective-permute-start | bytes 1769480 | tf_op jit(solution)/shard_map/ppermute | solution.py:174
  67.8 13.0 %all-gather.3.cloned.1.call-done = bf16[768,1536]{1,0:T(8,128)(2,1)} async-done(((bf16[96,1536]{1,0:T(8,128)(2,1)}), bf16[768,1536]{1,0:T(8,128)(2,1)}) %all-gather.3.cloned.1.call-update) | async-done | bytes 2359312 | tf_op jit(solution)/shard_map/all_gather | solution.py:138
  80.8 7.0 %convolution_convert_fusion.1 = bf16[1568,1152]{1,0:T(8,128)(2,1)} fusion(bf16[768,1536]{1,0:T(8,128)(2,1)} %all-gather.3.cloned.1.call-done, bf16[784,768]{1,0:T(8,128)(2,1)} %collective-permute-done, bf16[784,768]{1,0:T(8,128)(2,1)S(1)} %fusion.21), kind=kOutput, calls=%fused_computation.27 | convolution fusion | flops 2781155328 | bytes 7790592 | tf_op jit(solution)/shard_map/dot_general | solution.py:45
  87.8 11.9 %reshape.555 = bf16[1,8,196,3,6,64]{5,4,3,2,1,0:T(8,128)(2,1)} reshape(bf16[1568,1152]{1,0:T(8,128)(2,1)} %convolution_convert_fusion.1) | data formatting | bytes 7225344 | tf_op jit(solution)/shard_map/reshape;reshape | solution.py:28
  99.7 8.4 %copy.199 = bf16[1,8,196,3,6,64]{5,1,4,2,3,0:T(8,128)(2,1)S(1)} copy(bf16[1,8,196,3,6,64]{5,4,3,2,1,0:T(8,128)(2,1)} %reshape.555) | data formatting | bytes 7225344 | tf_op jit(solution)/shard_map/reshape;reshape | solution.py:28
  142.5 8.1 %collective-permute-done.11 = bf16[96,3072]{1,0:T(8,128)(2,1)} collective-permute-done((bf16[96,3072]{1,0:T(8,128)(2,1)}, bf16[96,3072]{1,0:T(8,128)(2,1)}, u32[]{:S(2)}, u32[]{:S(2)}) %collective-permute-start.11) | collective-permute-done | bytes 589856 | tf_op jit(solution)/shard_map/ppermute | solution.py:174
  153.1 7.3 %convolution_convert_fusion = bf16[1568,1152]{1,0:T(8,128)(2,1)} fusion(bf16[768,1536]{1,0:T(8,128)(2,1)} %all-gather.5.cloned.1.call-done, bf16[784,768]{1,0:T(8,128)(2,1)} %collective-permute-done.3, bf16[784,768]{1,0:T(8,128)(2,1)} %multiply_convert_fusion.8), kind=kOutput, calls=%fused_computation.26 | convolution fusion | flops 2781155328 | bytes 7790592 | tf_op jit(solution)/shard_map/dot_general | solution.py:45
  160.4 12.1 %reshape.556 = bf16[8,196,3,6,64]{4,3,2,1,0:T(8,128)(2,1)} reshape(bf16[1568,1152]{1,0:T(8,128)(2,1)} %convolution_convert_fusion) | data formatting | bytes 7225344 | tf_op jit(solution)/shard_map/reshape;reshape | solution.py:31
  172.5 6.7 %fusion.115 = (bf16[8,196,1,6,64]{4,3,2,1,0:T(8,128)(2,1)}, bf16[8,196,1,6,64]{4,3,2,1,0:T(8,128)(2,1)}, bf16[8,196,1,6,64]{4,3,2,1,0:T(8,128)(2,1)}) fusion(bf16[8,196,3,6,64]{4,3,2,1,0:T(8,128)(2,1)} %reshape.556), kind=kLoop, calls=%fused_computation.230 | loop fusion | bytes 7225344 | tf_op jit(solution)/shard_map/slice | solution.py:64
  228.1 26.7 %multiply_convert_fusion.1 = (bf16[1568,1536]{1,0:T(8,128)(2,1)S(1)}, f32[1568,1536]{1,0:T(8,128)}, f32[1568,1536]{1,0:T(8,128)}) fusion(bf16[768,3072]{1,0:T(8,128)(2,1)S(1)} %bitcast_select_fusion, bf16[784,768]{1,0:T(8,128)(2,1)S(1)} %collective-permute-done.6, bf16[784,768]{1,0:T(8,128)(2,1)S(1)} %multiply_convert_fusion.7), kind=kOutput, calls=%fused_computation.10 | convolution fusion | flops 3860742144 | bytes 28852224 | tf_op jit(solution)/shard_map/dot_general | solution.py:263
  254.9 12.6 %add_convert_fusion = bf16[1568,1536]{1,0:T(8,128)(2,1)S(1)} fusion(f32[1568,1536]{1,0:T(8,128)} %get-tuple-element.52, bf16[1568,768]{1,0:T(8,128)(2,1)S(1)} %copy-done.33, f32[1568,1536]{1,0:T(8,128)} %get-tuple-element.89, bf16[768,3072]{1,0:T(8,128)(2,1)S(1)} %bitcast_select_fusion), kind=kOutput, calls=%fused_computation.9 | convolution fusion | flops 3733094400 | bytes 28852224 | tf_op jit(solution)/shard_map/dot_general | solution.py:272
  300.2 7.5 %fusion.67 = bf16[8,196,1,6,64]{1,4,3,0,2:T(8,128)(2,1)} fusion(bf16[8,196,6,64]{1,3,2,0:T(8,128)(2,1)} %copy.157, f32[8,6,196,196]{2,3,1,0:T(8,128)} %copy-done, f32[8,6,196]{2,1,0:T(8,128)S(1)} %log_add_fusion.1), kind=kOutput, calls=%fused_computation.144 | convolution fusion | flops 242161920 | bytes 9821952 | tf_op jit(solution)/shard_map/bhlm,blhe->bmhe/dot_general | solution.py:88
  307.7 7.4 %multiply_reduce_fusion = (f32[8,6,196]{2,1,0:T(8,128)S(1)}, f32[8,6,196,196]{2,3,1,0:T(8,128)}) fusion(f32[8,6,196,196]{2,3,1,0:T(8,128)} %copy-done, f32[8,6,196]{2,1,0:T(8,128)S(1)} %log_add_fusion.1, bf16[8,196,6,64]{1,3,2,0:T(8,128)(2,1)S(1)} %copy-done.14, bf16[8,196,1,6,64]{1,4,3,0,2:T(8,128)(2,1)S(1)} %copy-done.21), kind=kOutput, calls=%fused_computation.4 | convolution fusion | flops 243394368 | bytes 17235456 | tf_op jit(solution)/shard_map/blhe,bmhe->bhlm/dot_general | solution.py:94
  315.1 11.4 %multiply_convert_fusion = bf16[8,6,196,196]{2,3,1,0:T(8,128)(2,1)} fusion(f32[8,6,196,196]{2,3,1,0:T(8,128)} %get-tuple-element.91, f32[8,6,196,196]{2,3,1,0:T(8,128)} %copy-done, f32[8,6,196]{2,1,0:T(8,128)S(1)} %get-tuple-element.90, f32[8,6,196]{2,1,0:T(8,128)S(1)} %log_add_fusion.1), kind=kLoop, calls=%fused_computation.3 | loop fusion | flops 9219840 | bytes 18514944 | tf_op jit(solution)/shard_map/convert_element_type | solution.py:100
  339.2 9.0 %convert_element_type.179 = bf16[1568,1152]{0,1:T(8,128)(2,1)} reshape(bf16[8,196,3,6,64]{1,0,4,3,2:T(8,128)(2,1)} %copy.162) | data formatting | bytes 7225344 | tf_op jit(solution)/shard_map/convert_element_type | solution.py:109
  359.2 7.7 %convolution_convert_fusion.5 = bf16[768,1536]{1,0:T(8,128)(2,1)S(1)} fusion(bf16[1568,1536]{1,0:T(8,128)(2,1)} %copy-done.68, bf16[784,768]{1,0:T(8,128)(2,1)} %copy-done.63, bf16[784,768]{1,0:T(8,128)(2,1)} %copy-done.28), kind=kOutput, calls=%fused_computation.60 | convolution fusion | flops 3705372672 | bytes 9584640 | tf_op jit(solution)/shard_map/dot_general | solution.py:275
  366.9 7.1 %convolution_convert_fusion.4 = bf16[768,1536]{1,0:T(8,128)(2,1)S(1)} fusion(bf16[1568,768]{1,0:T(8,128)(2,1)S(1)} %copy-done.34, bf16[1568,1536]{1,0:T(8,128)(2,1)} %copy-done.67), kind=kOutput, calls=%fused_computation.59 | convolution fusion | flops 3700555776 | bytes 9584640 | tf_op jit(solution)/shard_map/dot_general | solution.py:271
  411.6 7.6 %multiply_reduce_fusion.2 = (f32[196,6,8]{2,1,0:T(8,128)S(1)}, f32[196,6,8,8]{2,3,1,0:T(8,128)S(1)}) fusion(f32[196,6,8,8]{2,3,1,0:T(8,128)} %copy-done.1, f32[196,6,8]{2,1,0:T(8,128)} %log_add_fusion, bf16[196,8,6,64]{3,1,2,0:T(8,128)(2,1)} %copy.164, bf16[196,8,3,6,64]{4,1,3,0,2:T(8,128)(2,1)} %bitcast.188), kind=kOutput, calls=%fused_computation.38 | convolution fusion | flops 9925440 | bytes 10775296 | tf_op jit(solution)/shard_map/blhe,bmhe->bhlm/dot_general | solution.py:94
  432.7 12.1 %copy.167 = bf16[1,8,196,3,6,64]{2,1,5,4,3,0:T(8,128)(2,1)} copy(bf16[1,8,196,3,6,64]{5,1,4,2,3,0:T(8,128)(2,1)} %maximum_bitcast_fusion) | data formatting | bytes 7225344 | tf_op jit(solution)/shard_map/transpose | solution.py:38
  444.7 9.0 %reshape_reshape.28 = bf16[1568,1152]{0,1:T(8,128)(2,1)} reshape(bf16[1,8,196,3,6,64]{2,1,5,4,3,0:T(8,128)(2,1)} %copy.167) | data formatting | bytes 7225344 | tf_op jit(solution)/shard_map/reshape;reshape | solution.py:110
  464.4 6.1 fusion.61
  487.0 41.2 %psum.7 = f32[3,768]{1,0:T(4,128)} all-reduce(f32[3,768]{1,0:T(4,128)S(1)} %pad_maximum_fusion.30), channel_id=1, replica_groups=mesh['dp'=8,'ty'=2,'core'=2] {'dp','ty','core'}, use_global_device_ids=true, to_apply=%region_22.23 | all-reduce | flops 2304 | bytes 18432 | tf_op jit(solution)/shard_map/psum | solution.py:309
  532.9 67.7 %reduce-scatter.4.cloned.1.call-done = bf16[96,1536]{1,0:T(8,128)(2,1)} async-done(((bf16[768,1536]{1,0:T(8,128)(2,1)}), bf16[96,1536]{1,0:T(8,128)(2,1)}) %reduce-scatter.4.cloned.1.call-update) | async-done | bytes 294928 | tf_op jit(solution)/shard_map/reduce_scatter | solution.py:188
  (365 shorter events, 273.7 us)
Async XLA Ops:
  7.2 73.6 %all-gather.3.cloned.1.call-start = ((), (), s32[]{:S(2)}) async-start(), calls=%async_computation.3 | async-start | bytes 2654208 | tf_op jit(solution)/shard_map/all_gather | solution.py:138
  9.4 8.0 %collective-permute-start.1 = (bf16[96,768]{0,1:T(8,128)(2,1)S(1)}, bf16[96,768]{0,1:T(8,128)(2,1)S(1)}, u32[]{:S(2)}, u32[]{:S(2)}) collective-permute-start(bf16[96,768]{0,1:T(8,128)(2,1)S(1)} %pad_maximum_fusion.27), channel_id=1, source_target_pairs={{0,2},{2,0},{1,3},{3,1},{4,6},{6,4},{5,7},{7,5},{8,10},{10,8},{9,1... | collective-permute-start | bytes 442376 | tf_op jit(solution)/shard_map/ppermute | solution.py:214
  18.9 134.2 %all-gather.5.cloned.1.call-start = ((), (), s32[]{:S(2)}) async-start(), calls=%async_computation.4 | async-start | bytes 2654208 | tf_op jit(solution)/shard_map/all_gather | solution.py:138
  20.3 17.4 %collective-permute-start.4 = (bf16[96,2304]{1,0:T(8,128)(2,1)}, bf16[96,2304]{1,0:T(8,128)(2,1)S(1)}, u32[]{:S(2)}, u32[]{:S(2)}) collective-permute-start(bf16[96,2304]{1,0:T(8,128)(2,1)} %concatenate.94), channel_id=1, source_target_pairs={{0,2},{2,0},{1,3},{3,1},{4,6},{6,4},{5,7},{7,5},{8,10},{10,8},{9,1... | collective-permute-start | bytes 1327112 | tf_op jit(solution)/shard_map/ppermute | solution.py:214
  23.4 44.4 %collective-permute-start = (bf16[784,768]{1,0:T(8,128)(2,1)S(1)}, bf16[784,768]{1,0:T(8,128)(2,1)}, u32[]{:S(2)}, u32[]{:S(2)}) collective-permute-start(bf16[784,768]{1,0:T(8,128)(2,1)S(1)} %fusion.21), channel_id=1, source_target_pairs={{0,1},{1,0},{2,3},{3,2},{4,5},{5,4},{6,7},{7,6},{8,9},{9,8},{10,11... | collective-permute-start | bytes 3612680 | tf_op jit(solution)/shard_map/ppermute | solution.py:239
  23.5 106.6 %collective-permute-start.15 = (bf16[784,768]{1,0:T(8,128)(2,1)}, bf16[784,768]{1,0:T(8,128)(2,1)}, u32[]{:S(2)}, u32[]{:S(2)}) collective-permute-start(bf16[784,768]{1,0:T(8,128)(2,1)} %param.12), channel_id=1, source_target_pairs={{0,1},{1,0},{2,3},{3,2},{4,5},{5,4},{6,7},{7,6},{8,9},{9,8},{10,11... | collective-permute-start | bytes 3612680 | tf_op jit(solution)/shard_map/ppermute | solution.py:239
  38.5 20.9 %collective-permute-start.7 = (bf16[96,3072]{1,0:T(8,128)(2,1)S(1)}, bf16[96,3072]{1,0:T(8,128)(2,1)}, u32[]{:S(2)}, u32[]{:S(2)}) collective-permute-start(bf16[96,3072]{1,0:T(8,128)(2,1)S(1)} %pad_maximum_fusion.23), channel_id=1, source_target_pairs={{0,8},{8,16},{16,24},{24,28},{28,20},{20,12},{12,4},{4,0},{1,9},{9... | collective-permute-start | bytes 1769480 | tf_op jit(solution)/shard_map/ppermute | solution.py:174
  40.1 27.7 %collective-permute-start.8 = (bf16[96,3072]{1,0:T(8,128)(2,1)S(1)}, bf16[96,3072]{1,0:T(8,128)(2,1)}, u32[]{:S(2)}, u32[]{:S(2)}) collective-permute-start(bf16[96,3072]{1,0:T(8,128)(2,1)S(1)} %pad_maximum_fusion.23), channel_id=1, source_target_pairs={{8,0},{16,8},{24,16},{28,24},{20,28},{12,20},{4,12},{0,4},{9,1},{1... | collective-permute-start | bytes 1769480 | tf_op jit(solution)/shard_map/ppermute | solution.py:178
  45.6 431.7 %reduce-scatter.6.cloned.1.call-start = ((), (), s32[]{:S(2)}) async-start(), calls=%async_computation.6 | async-start | bytes 2654208 | tf_op jit(solution)/shard_map/reduce_scatter | solution.py:188
  59.4 72.1 %collective-permute-start.9 = (bf16[96,3072]{1,0:T(8,128)(2,1)}, bf16[96,3072]{1,0:T(8,128)(2,1)}, u32[]{:S(2)}, u32[]{:S(2)}) collective-permute-start(bf16[96,3072]{1,0:T(8,128)(2,1)} %collective-permute-done.7), channel_id=1, source_target_pairs={{0,8},{8,16},{16,24},{24,28},{28,20},{20,12},{12,4},{4,0},{1,9},{9... | collective-permute-start | bytes 1769480 | tf_op jit(solution)/shard_map/ppermute | solution.py:174
  67.8 69.4 %collective-permute-start.10 = (bf16[96,3072]{1,0:T(8,128)(2,1)}, bf16[96,3072]{1,0:T(8,128)(2,1)S(1)}, u32[]{:S(2)}, u32[]{:S(2)}) collective-permute-start(bf16[96,3072]{1,0:T(8,128)(2,1)} %collective-permute-done.8), channel_id=1, source_target_pairs={{8,0},{16,8},{24,16},{28,24},{20,28},{12,20},{4,12},{0,4},{9,1},{1... | collective-permute-start | bytes 1769480 | tf_op jit(solution)/shard_map/ppermute | solution.py:178
  126.0 11.1 %collective-permute-start.2 = (bf16[784,768]{1,0:T(8,128)(2,1)S(1)}, bf16[784,768]{1,0:T(8,128)(2,1)S(1)}, u32[]{:S(2)}, u32[]{:S(2)}) collective-permute-start(bf16[784,768]{1,0:T(8,128)(2,1)S(1)} %slice.375), channel_id=1, source_target_pairs={{0,1},{1,0},{2,3},{3,2},{4,5},{5,4},{6,7},{7,6},{8,9},{9,8},{10,11... | collective-permute-start | bytes 3612680 | tf_op jit(solution)/shard_map/ppermute | solution.py:239
  131.5 19.0 %collective-permute-start.11 = (bf16[96,3072]{1,0:T(8,128)(2,1)}, bf16[96,3072]{1,0:T(8,128)(2,1)}, u32[]{:S(2)}, u32[]{:S(2)}) collective-permute-start(bf16[96,3072]{1,0:T(8,128)(2,1)} %collective-permute-done.9), channel_id=1, source_target_pairs={{0,8},{8,16},{16,24},{24,28},{28,20},{20,12},{12,4},{4,0},{1,9},{9... | collective-permute-start | bytes 1769480 | tf_op jit(solution)/shard_map/ppermute | solution.py:174
  137.2 76.7 %collective-permute-start.12 = (bf16[96,3072]{1,0:T(8,128)(2,1)S(1)}, bf16[96,3072]{1,0:T(8,128)(2,1)}, u32[]{:S(2)}, u32[]{:S(2)}) collective-permute-start(bf16[96,3072]{1,0:T(8,128)(2,1)S(1)} %collective-permute-done.10), channel_id=1, source_target_pairs={{8,0},{16,8},{24,16},{28,24},{20,28},{12,20},{4,12},{0,4},{9,1},{1... | collective-permute-start | bytes 1769480 | tf_op jit(solution)/shard_map/ppermute | solution.py:178
  139.6 13.5 %collective-permute-start.3 = (bf16[784,768]{1,0:T(8,128)(2,1)}, bf16[784,768]{1,0:T(8,128)(2,1)}, u32[]{:S(2)}, u32[]{:S(2)}) collective-permute-start(bf16[784,768]{1,0:T(8,128)(2,1)} %multiply_convert_fusion.8), channel_id=1, source_target_pairs={{0,1},{1,0},{2,3},{3,2},{4,5},{5,4},{6,7},{7,6},{8,9},{9,8},{10,11... | collective-permute-start | bytes 3612680 | tf_op jit(solution)/shard_map/ppermute | solution.py:239
  150.6 67.5 %collective-permute-start.13 = (bf16[96,3072]{1,0:T(8,128)(2,1)}, bf16[96,3072]{1,0:T(8,128)(2,1)}, u32[]{:S(2)}, u32[]{:S(2)}) collective-permute-start(bf16[96,3072]{1,0:T(8,128)(2,1)} %collective-permute-done.11), channel_id=1, source_target_pairs={{0,8},{8,16},{16,24},{24,28},{28,20},{20,12},{12,4},{4,0},{1,9},{9... | collective-permute-start | bytes 1769480 | tf_op jit(solution)/shard_map/ppermute | solution.py:174
  211.9 3.9 collective-permute-start.5
  217.6 10.5 %collective-permute-start.6 = (bf16[784,768]{1,0:T(8,128)(2,1)S(1)}, bf16[784,768]{1,0:T(8,128)(2,1)S(1)}, u32[]{:S(2)}, u32[]{:S(2)}) collective-permute-start(bf16[784,768]{1,0:T(8,128)(2,1)S(1)} %multiply_convert_fusion.7), channel_id=1, source_target_pairs={{0,1},{1,0},{2,3},{3,2},{4,5},{5,4},{6,7},{7,6},{8,9},{9,8},{10,11... | collective-permute-start | bytes 3612680 | tf_op jit(solution)/shard_map/ppermute | solution.py:239
  271.6 4.8 collective-permute-start.16
  359.1 172.6 %reduce-scatter.8.cloned.1.call-start = ((), (), s32[]{:S(2)}) async-start(), calls=%async_computation.7 | async-start | bytes 5308416 | tf_op jit(solution)/shard_map/reduce_scatter | solution.py:188
  376.7 224.0 %reduce-scatter.4.cloned.1.call-start = ((), (), s32[]{:S(2)}) async-start(), calls=%async_computation.5 | async-start | bytes 2654208 | tf_op jit(solution)/shard_map/reduce_scatter | solution.py:188
  480.3 48.3 %collective-permute-start.22 = (bf16[96,768]{0,1:T(8,128)(2,1)S(1)}, bf16[96,768]{0,1:T(8,128)(2,1)S(1)}, u32[]{:S(2)}, u32[]{:S(2)}) collective-permute-start(bf16[96,768]{0,1:T(8,128)(2,1)S(1)} %pad_maximum_fusion.29), channel_id=1, source_target_pairs={{0,2},{2,0},{1,3},{3,1},{4,6},{6,4},{5,7},{7,5},{8,10},{10,8},{9,1... | collective-permute-start | bytes 442376 | tf_op jit(solution)/shard_map/ppermute | solution.py:214
  603.7 7.8 %collective-permute-start.21 = (bf16[96,768]{0,1:T(8,128)(2,1)S(1)}, bf16[96,768]{0,1:T(8,128)(2,1)S(1)}, u32[]{:S(2)}, u32[]{:S(2)}) collective-permute-start(bf16[96,768]{0,1:T(8,128)(2,1)S(1)} %pad_maximum_fusion.28), channel_id=1, source_target_pairs={{0,2},{2,0},{1,3},{3,1},{4,6},{6,4},{5,7},{7,5},{8,10},{10,8},{9,1... | collective-permute-start | bytes 442376 | tf_op jit(solution)/shard_map/ppermute | solution.py:214
  605.2 9.7 %collective-permute-start.23 = (bf16[96,1536]{1,0:T(8,128)(2,1)S(1)}, bf16[96,1536]{1,0:T(8,128)(2,1)S(1)}, u32[]{:S(2)}, u32[]{:S(2)}) collective-permute-start(bf16[96,1536]{1,0:T(8,128)(2,1)S(1)} %pad_maximum_fusion.26), channel_id=1, source_target_pairs={{0,2},{2,0},{1,3},{3,1},{4,6},{6,4},{5,7},{7,5},{8,10},{10,8},{9,1... | collective-permute-start | bytes 884744 | tf_op jit(solution)/shard_map/ppermute | solution.py:214
  (77 other events, 679.5 us)
Sparse Core Ops, SparseCore 0:
  19.0 61.7 all-gather.2
  83.6 55.5 all-gather.4
  359.3 69.5 reduce-scatter.5
  432.3 95.9 reduce-scatter.7
  531.7 68.9 reduce-scatter.3

commit v11 on v8

--- a/solution.py
+++ b/solution.py
@@ -148,11 +148,13 @@
 
 
 def gather_mlp(mine, other, width):
-    local = jnp.concatenate(
-        [mine[:, :width], other[:, :width], mine[:, width:], other[:, width:]], axis=1
-    )
-    full = lax.all_gather(local, "dp", axis=0, tiled=True)
-    return full[:, : 2 * width], full[:, 2 * width :].T
+    up = lax.all_gather(
+        jnp.concatenate([mine[:, :width], other[:, :width]], axis=1), "dp", axis=0, tiled=True
+    )
+    down = lax.all_gather(
+        jnp.concatenate([mine[:, width:], other[:, width:]], axis=1), "dp", axis=0, tiled=True
+    )
+    return up, down.T
 
 
 def scatter_rows(pieces):
@@ -234,9 +236,6 @@
     normed_mlp = spread_rows(normalize(after_space, norm_gains[2]).astype(jnp.bfloat16))
     hidden_pre = jnp.dot(normed_mlp, up_full, preferred_element_type=jnp.float32)
     hidden = jax.nn.gelu(hidden_pre, approximate=False).astype(jnp.bfloat16)
-    output = (
-        after_space + sum_rows(jnp.dot(hidden, down_full, preferred_element_type=jnp.float32))
-    ).astype(jnp.bfloat16)
 
     grad_after = cotangent.astype(jnp.float32)
     down_rows = spread_grads(grad_after.astype(jnp.bfloat16))
@@ -272,9 +271,13 @@
     grad_qkv_time, grad_proj_time, grad_normed = attend_backward(
         normed_time, time_qkv, time_proj, grouped_time, summary_time, merged_time, time_rows, True
     )
-    grad_qkv_time, grad_proj_time = finish_attention(
-        scatter_rows((grad_qkv_time, grad_proj_time)), qkv_time.shape, proj_time.shape
-    )
+    time_local = scatter_rows((grad_qkv_time, grad_proj_time))
+    late_hidden, late_rows, _ = lax.optimization_barrier((hidden, after_space, grad_qkv_time))
+    output = (
+        late_rows
+        + sum_rows(jnp.dot(late_hidden, down_full, preferred_element_type=jnp.float32))
+    ).astype(jnp.bfloat16)
+    grad_qkv_time, grad_proj_time = finish_attention(time_local, qkv_time.shape, proj_time.shape)
     _, norm_back = jax.vjp(normalize, inputs, norm_gains[0])
     back_rows, gain_time = norm_back(sum_grads(grad_normed))
     grad_tokens = grad_after + back_rows

time: 609 us -> 605 us (level)
    all_gather x1 -> x2, waiting for transfers between devices: 13 us -> 21.3 us  [the longest x1 21.3 us: gather_mlp(): lax.all_gather(jnp.concatenate([mine[:, width:], other[:, width:]], axis=...]
    unnamed x148 -> x158, local copies, waits for them, and re-layouts: 28.2 us -> 27.1 us
  transfers between devices with their start and end apart: 23 -> 24, of which waited for: 16 -> 14; matrix products, arithmetic and copies ran while one was open for 40% -> 44% of each run, Pallas kernels for 0% -> 0%
where the time goes in v11:
time: 605 us; the launch traced here: 598 us
  matrix products  165 us (27%)
  waiting for transfers between devices  156 us (26%)
  local copies, waits for them, and re-layouts  150 us (25%)
  other arithmetic  57.3 us (9%)
  blocking collectives  41.2 us (7%)
  between operations  15.9 us (3%)
  starting transfers between devices  11.7 us (2%)
    reduce_scatter x3, waiting for transfers between devices, scatter_rows(): lax.psum_scatter(jnp.concatenate(flat, axis=1).astype(jnp.bfloat16), 'dp'...  60.7 us
    psum x1, blocking collectives, per_device(): lax.psum(jnp.stack([gain_time, gain_space, gain_mlp]), ('dp', 'ty', 'core'))  41.2 us
    all_gather x2, waiting for transfers between devices, gather_attention(): lax.all_gather(jnp.concatenate([qkv_local, proj_local], axis=1), 'dp', ax...  37.5 us
    unnamed x158, local copies, waits for them, and re-layouts  27.1 us
    dot_general x1, matrix products, per_device(): jnp.dot(normed_mlp, up_full, preferred_element_type=jnp.float32)  27 us
    another operation x3, local copies, waits for them, and re-layouts, to_groups(): shaped = values.reshape((clip_count, FRAMES, PATCH) + trailing)  25.4 us
    ppermute x5, waiting for transfers between devices, swap_ty(): return lax.ppermute(values, 'ty', perm=[(0, 1), (1, 0)])  22.8 us
    all_gather x1, waiting for transfers between devices, gather_mlp(): lax.all_gather(jnp.concatenate([mine[:, width:], other[:, width:]], axis=...  21.3 us
  transfers between devices with their start and end apart: 24, of which 14 were waited for; matrix products, arithmetic and copies ran while one was open for 44% of the time, Pallas kernels for 0%

profile of v11, /device:TPU:0, one launch (start us, length us, event | category | flops | bytes accessed | tf_op | source)
XLA Modules:
  0.0 597.6 jit_solution(16160195071841414572)
XLA Ops:
  23.8 10.8 %collective-permute-done.4 = bf16[96,2304]{1,0:T(8,128)(2,1)S(1)} collective-permute-done((bf16[96,2304]{1,0:T(8,128)(2,1)S(1)}, bf16[96,2304]{1,0:T(8,128)(2,1)S(1)}, u32[]{:S(2)}, u32[]{:S(2)}) %collective-permute-start.4) | collective-permute-done | bytes 442400 | tf_op jit(solution)/shard_map/ppermute | solution.py:188
  36.3 36.0 %all-gather.5.cloned.1.call-done = bf16[768,1536]{1,0:T(8,128)(2,1)} async-done(((bf16[96,1536]{1,0:T(8,128)(2,1)}), bf16[768,1536]{1,0:T(8,128)(2,1)}) %all-gather.5.cloned.1.call-update) | async-done | bytes 2359312 | tf_op jit(solution)/shard_map/all_gather | solution.py:138
  72.3 7.1 %convolution_convert_fusion.1 = bf16[1568,1152]{1,0:T(8,128)(2,1)} fusion(bf16[768,1536]{1,0:T(8,128)(2,1)} %all-gather.5.cloned.1.call-done, bf16[784,768]{1,0:T(8,128)(2,1)} %collective-permute-done, bf16[784,768]{1,0:T(8,128)(2,1)S(1)} %fusion.21), kind=kOutput, calls=%fused_computation.25 | convolution fusion | flops 2781155328 | bytes 7790592 | tf_op jit(solution)/shard_map/dot_general | solution.py:45
  79.4 12.3 %reshape.226 = bf16[1,8,196,3,6,64]{5,4,3,2,1,0:T(8,128)(2,1)} reshape(bf16[1568,1152]{1,0:T(8,128)(2,1)} %convolution_convert_fusion.1) | data formatting | bytes 7225344 | tf_op jit(solution)/shard_map/reshape;reshape | solution.py:28
  91.7 8.4 %copy.152 = bf16[1,8,196,3,6,64]{5,1,4,2,3,0:T(8,128)(2,1)S(1)} copy(bf16[1,8,196,3,6,64]{5,4,3,2,1,0:T(8,128)(2,1)} %reshape.226) | data formatting | bytes 7225344 | tf_op jit(solution)/shard_map/reshape;reshape | solution.py:28
  125.7 7.8 %convolution_convert_fusion = bf16[1568,1152]{1,0:T(8,128)(2,1)} fusion(bf16[768,1536]{1,0:T(8,128)(2,1)} %all-gather.7.cloned.1.call-done, bf16[784,768]{1,0:T(8,128)(2,1)S(1)} %collective-permute-done.3, bf16[784,768]{1,0:T(8,128)(2,1)S(1)} %multiply_convert_fusion.8), kind=kOutput, calls=%fused_computation.24 | convolution fusion | flops 2781155328 | bytes 7790592 | tf_op jit(solution)/shard_map/dot_general | solution.py:45
  133.6 11.8 %reshape.227 = bf16[8,196,3,6,64]{4,3,2,1,0:T(8,128)(2,1)} reshape(bf16[1568,1152]{1,0:T(8,128)(2,1)} %convolution_convert_fusion) | data formatting | bytes 7225344 | tf_op jit(solution)/shard_map/reshape;reshape | solution.py:31
  145.3 6.4 %fusion.106 = (bf16[8,196,1,6,64]{4,3,2,1,0:T(8,128)(2,1)S(1)}, bf16[8,196,1,6,64]{4,3,2,1,0:T(8,128)(2,1)}, bf16[8,196,1,6,64]{4,3,2,1,0:T(8,128)(2,1)}) fusion(bf16[8,196,3,6,64]{4,3,2,1,0:T(8,128)(2,1)} %reshape.227), kind=kLoop, calls=%fused_computation.207 | loop fusion | bytes 7225344 | tf_op jit(solution)/shard_map/slice | solution.py:64
  186.8 27.0 %multiply_convert_fusion.1 = (bf16[1568,1536]{1,0:T(8,128)(2,1)}, f32[1568,1536]{1,0:T(8,128)}, f32[1568,1536]{1,0:T(8,128)}) fusion(bf16[768,1536]{1,0:T(8,128)(2,1)} %all-gather.9.cloned.1.call-done, bf16[784,768]{1,0:T(8,128)(2,1)} %collective-permute-done.6, bf16[784,768]{1,0:T(8,128)(2,1)} %multiply_convert_fusion.7), kind=kOutput, calls=%fused_computation.8 | convolution fusion | flops 3860742144 | bytes 28852224 | tf_op jit(solution)/shard_map/dot_general | solution.py:237
  213.9 21.3 %all-gather.11.cloned.1.call-done = bf16[768,1536]{1,0:T(8,128)(2,1)} async-done(((bf16[96,1536]{1,0:T(8,128)(2,1)}), bf16[768,1536]{1,0:T(8,128)(2,1)}) %all-gather.11.cloned.1.call-update) | async-done | bytes 2359312 | tf_op jit(solution)/shard_map/all_gather | solution.py:154
  235.2 13.1 %add_convert_fusion = bf16[1568,1536]{1,0:T(8,128)(2,1)S(1)} fusion(f32[1568,1536]{1,0:T(8,128)} %get-tuple-element.47, bf16[1568,768]{1,0:T(8,128)(2,1)} %constant_dynamic-update-slice_fusion, bf16[768,1536]{1,0:T(8,128)(2,1)} %all-gather.11.cloned.1.call-done, f32[1568,1536]{1,0:T(8,128)} %get-tuple-element.75), kind=kOutput, calls=%fused_computation.7 | convolution fusion | flops 3733094400 | bytes 28852224 | tf_op jit(solution)/shard_map/dot_general | solution.py:243
  277.0 7.5 %fusion.61 = bf16[8,196,1,6,64]{1,4,3,0,2:T(8,128)(2,1)} fusion(bf16[8,196,6,64]{1,3,2,0:T(8,128)(2,1)} %copy.110, f32[8,6,196,196]{2,3,1,0:T(8,128)} %copy-done, f32[8,6,196]{2,1,0:T(8,128)S(1)} %log_add_fusion.1), kind=kOutput, calls=%fused_computation.135 | convolution fusion | flops 242161920 | bytes 9821952 | tf_op jit(solution)/shard_map/bhlm,blhe->bmhe/dot_general | solution.py:88
  284.4 7.5 %multiply_reduce_fusion = (f32[8,6,196]{2,1,0:T(8,128)S(1)}, f32[8,6,196,196]{2,3,1,0:T(8,128)}) fusion(f32[8,6,196,196]{2,3,1,0:T(8,128)} %copy-done, f32[8,6,196]{2,1,0:T(8,128)S(1)} %log_add_fusion.1, bf16[8,196,6,64]{1,3,2,0:T(8,128)(2,1)S(1)} %copy-done.17, bf16[8,196,1,6,64]{1,4,3,0,2:T(8,128)(2,1)S(1)} %copy-done.26), kind=kOutput, calls=%fused_computation.2 | convolution fusion | flops 243394368 | bytes 17235456 | tf_op jit(solution)/shard_map/blhe,bmhe->bhlm/dot_general | solution.py:94
  292.0 11.4 %multiply_convert_fusion = bf16[8,6,196,196]{2,3,1,0:T(8,128)(2,1)} fusion(f32[8,6,196,196]{2,3,1,0:T(8,128)} %get-tuple-element.77, f32[8,6,196,196]{2,3,1,0:T(8,128)} %copy-done, f32[8,6,196]{2,1,0:T(8,128)S(1)} %get-tuple-element.76, f32[8,6,196]{2,1,0:T(8,128)S(1)} %log_add_fusion.1), kind=kLoop, calls=%fused_computation.1 | loop fusion | flops 9219840 | bytes 18514944 | tf_op jit(solution)/shard_map/convert_element_type | solution.py:100
  316.2 9.0 %convert_element_type.179 = bf16[1568,1152]{0,1:T(8,128)(2,1)} reshape(bf16[8,196,3,6,64]{1,0,4,3,2:T(8,128)(2,1)} %copy.115) | data formatting | bytes 7225344 | tf_op jit(solution)/shard_map/convert_element_type | solution.py:109
  334.7 7.7 %convolution_convert_fusion.5 = bf16[768,1536]{1,0:T(8,128)(2,1)S(1)} fusion(bf16[1568,1536]{1,0:T(8,128)(2,1)} %copy-done.67, bf16[784,768]{1,0:T(8,128)(2,1)} %collective-permute-done.6, bf16[784,768]{1,0:T(8,128)(2,1)} %multiply_convert_fusion.7), kind=kOutput, calls=%fused_computation.57 | convolution fusion | flops 3705372672 | bytes 9584640 | tf_op jit(solution)/shard_map/dot_general | solution.py:246
  342.4 7.1 %convolution_convert_fusion.4 = bf16[768,1536]{1,0:T(8,128)(2,1)S(1)} fusion(bf16[1568,768]{1,0:T(8,128)(2,1)S(1)} %copy-done.38, bf16[1568,1536]{1,0:T(8,128)(2,1)} %get-tuple-element.12), kind=kOutput, calls=%fused_computation.56 | convolution fusion | flops 3700555776 | bytes 9584640 | tf_op jit(solution)/shard_map/dot_general | solution.py:242
  352.7 6.2 %fusion.51 = f32[1568,768]{1,0:T(8,128)S(1)} fusion(bf16[1568,1152]{0,1:T(8,128)(2,1)} %convert_element_type.179, bf16[768,1536]{1,0:T(8,128)(2,1)} %all-gather.7.cloned.1.call-done), kind=kOutput, calls=%fused_computation.125 | convolution fusion | flops 2774532096 | bytes 10420224 | tf_op jit(solution)/shard_map/dot_general | solution.py:114
  394.6 7.4 %multiply_reduce_fusion.2 = (f32[196,6,8]{2,1,0:T(8,128)S(1)}, f32[196,6,8,8]{2,3,1,0:T(8,128)S(1)}) fusion(f32[196,6,8,8]{2,3,1,0:T(8,128)} %copy-done.1, f32[196,6,8]{2,1,0:T(8,128)} %log_add_fusion, bf16[196,8,6,64]{3,1,2,0:T(8,128)(2,1)} %copy.117, bf16[196,8,3,6,64]{4,1,3,0,2:T(8,128)(2,1)} %bitcast.162), kind=kOutput, calls=%fused_computation.36 | convolution fusion | flops 9925440 | bytes 10775296 | tf_op jit(solution)/shard_map/blhe,bmhe->bhlm/dot_general | solution.py:94
  415.5 12.0 %copy.120 = bf16[1,8,196,3,6,64]{2,1,5,4,3,0:T(8,128)(2,1)} copy(bf16[1,8,196,3,6,64]{5,1,4,2,3,0:T(8,128)(2,1)} %maximum_bitcast_fusion) | data formatting | bytes 7225344 | tf_op jit(solution)/shard_map/transpose | solution.py:38
  427.5 9.0 %reshape_reshape.28 = bf16[1568,1152]{0,1:T(8,128)(2,1)} reshape(bf16[1,8,196,3,6,64]{2,1,5,4,3,0:T(8,128)(2,1)} %copy.120) | data formatting | bytes 7225344 | tf_op jit(solution)/shard_map/reshape;reshape | solution.py:110
  447.2 6.3 %fusion.54 = f32[1568,768]{1,0:T(8,128)S(1)} fusion(bf16[1568,1152]{0,1:T(8,128)(2,1)} %reshape_reshape.28, bf16[768,1536]{1,0:T(8,128)(2,1)} %all-gather.5.cloned.1.call-done), kind=kOutput, calls=%fused_computation.128 | convolution fusion | flops 2774532096 | bytes 10420224 | tf_op jit(solution)/shard_map/dot_general | solution.py:114
  470.3 41.2 %psum.7 = f32[3,768]{1,0:T(4,128)} all-reduce(f32[3,768]{1,0:T(4,128)S(1)} %pad_maximum_fusion.31), channel_id=1, replica_groups=mesh['dp'=8,'ty'=2,'core'=2] {'dp','ty','core'}, use_global_device_ids=true, to_apply=%region_21.0 | all-reduce | flops 2304 | bytes 18432 | tf_op jit(solution)/shard_map/psum | solution.py:284
  514.6 60.7 %reduce-scatter.4.cloned.1.call-done = bf16[96,1536]{1,0:T(8,128)(2,1)} async-done(((bf16[768,1536]{1,0:T(8,128)(2,1)}), bf16[96,1536]{1,0:T(8,128)(2,1)}) %reduce-scatter.4.cloned.1.call-update) | async-done | bytes 294928 | tf_op jit(solution)/shard_map/reduce_scatter | solution.py:162
  (345 shorter events, 226.6 us)
Async XLA Ops:
  7.2 65.1 %all-gather.5.cloned.1.call-start = ((), (), s32[]{:S(2)}) async-start(), calls=%async_computation.3 | async-start | bytes 2654208 | tf_op jit(solution)/shard_map/all_gather | solution.py:138
  9.4 8.0 %collective-permute-start.1 = (bf16[96,768]{0,1:T(8,128)(2,1)S(1)}, bf16[96,768]{0,1:T(8,128)(2,1)S(1)}, u32[]{:S(2)}, u32[]{:S(2)}) collective-permute-start(bf16[96,768]{0,1:T(8,128)(2,1)S(1)} %pad_maximum_fusion.28), channel_id=1, source_target_pairs={{0,2},{2,0},{1,3},{3,1},{4,6},{6,4},{5,7},{7,5},{8,10},{10,8},{9,1... | collective-permute-start | bytes 442376 | tf_op jit(solution)/shard_map/ppermute | solution.py:188
  18.9 106.6 %all-gather.7.cloned.1.call-start = ((), (), s32[]{:S(2)}) async-start(), calls=%async_computation.4 | async-start | bytes 2654208 | tf_op jit(solution)/shard_map/all_gather | solution.py:138
  20.3 16.0 %collective-permute-start = (bf16[784,768]{1,0:T(8,128)(2,1)S(1)}, bf16[784,768]{1,0:T(8,128)(2,1)}, u32[]{:S(2)}, u32[]{:S(2)}) collective-permute-start(bf16[784,768]{1,0:T(8,128)(2,1)S(1)} %fusion.21), channel_id=1, source_target_pairs={{0,1},{1,0},{2,3},{3,2},{4,5},{5,4},{6,7},{7,6},{8,9},{9,8},{10,11... | collective-permute-start | bytes 3612680 | tf_op jit(solution)/shard_map/ppermute | solution.py:213
  22.0 12.6 %collective-permute-start.4 = (bf16[96,2304]{1,0:T(8,128)(2,1)S(1)}, bf16[96,2304]{1,0:T(8,128)(2,1)S(1)}, u32[]{:S(2)}, u32[]{:S(2)}) collective-permute-start(bf16[96,2304]{1,0:T(8,128)(2,1)S(1)} %concatenate.78), channel_id=1, source_target_pairs={{0,2},{2,0},{1,3},{3,1},{4,6},{6,4},{5,7},{7,5},{8,10},{10,8},{9,1... | collective-permute-start | bytes 1327112 | tf_op jit(solution)/shard_map/ppermute | solution.py:188
  36.2 150.6 %all-gather.9.cloned.1.call-start = ((), (), s32[]{:S(2)}) async-start(), calls=%async_computation.5 | async-start | bytes 2654208 | tf_op jit(solution)/shard_map/all_gather | solution.py:151
  117.9 2.9 collective-permute-start.2
  122.8 2.9 collective-permute-start.3
  123.9 111.3 %all-gather.11.cloned.1.call-start = ((), (), s32[]{:S(2)}) async-start(), calls=%async_computation.6 | async-start | bytes 2654208 | tf_op jit(solution)/shard_map/all_gather | solution.py:154
  175.9 2.9 collective-permute-start.5
  176.1 8.3 %collective-permute-start.8 = (bf16[784,768]{1,0:T(8,128)(2,1)}, bf16[784,768]{1,0:T(8,128)(2,1)}, u32[]{:S(2)}, u32[]{:S(2)}) collective-permute-start(bf16[784,768]{1,0:T(8,128)(2,1)} %param.10), channel_id=1, source_target_pairs={{0,1},{1,0},{2,3},{3,2},{4,5},{5,4},{6,7},{7,6},{8,9},{9,8},{10,11... | collective-permute-start | bytes 3612680 | tf_op jit(solution)/shard_map/ppermute | solution.py:213
  181.1 5.7 collective-permute-start.6
  184.4 276.3 %reduce-scatter.6.cloned.1.call-start = ((), (), s32[]{:S(2)}) async-start(), calls=%async_computation.8 | async-start | bytes 2654208 | tf_op jit(solution)/shard_map/reduce_scatter | solution.py:162
  252.7 2.9 collective-permute-start.9
  260.1 2.9 collective-permute-start.10
  334.6 178.9 %reduce-scatter.8.cloned.1.call-start = ((), (), s32[]{:S(2)}) async-start(), calls=%async_computation.9 | async-start | bytes 5308416 | tf_op jit(solution)/shard_map/reduce_scatter | solution.py:162
  352.2 223.1 %reduce-scatter.4.cloned.1.call-start = ((), (), s32[]{:S(2)}) async-start(), calls=%async_computation.7 | async-start | bytes 2654208 | tf_op jit(solution)/shard_map/reduce_scatter | solution.py:162
  359.0 2.9 collective-permute-start.11
  367.0 10.1 %collective-permute-start.12 = (bf16[784,768]{1,0:T(8,128)(2,1)S(1)}, bf16[784,768]{1,0:T(8,128)(2,1)S(1)}, u32[]{:S(2)}, u32[]{:S(2)}) collective-permute-start(bf16[784,768]{1,0:T(8,128)(2,1)S(1)} %fusion.98), channel_id=1, source_target_pairs={{0,1},{1,0},{2,3},{3,2},{4,5},{5,4},{6,7},{7,6},{8,9},{9,8},{10,11... | collective-permute-start | bytes 3612680 | tf_op jit(solution)/shard_map/ppermute | solution.py:213
  376.9 77.1 %collective-permute-start.7 = (bf16[784,768]{1,0:T(8,128)(2,1)}, bf16[784,768]{1,0:T(8,128)(2,1)}, u32[]{:S(2)}, u32[]{:S(2)}) collective-permute-start(bf16[784,768]{1,0:T(8,128)(2,1)} %slice.353), channel_id=1, source_target_pairs={{0,1},{1,0},{2,3},{3,2},{4,5},{5,4},{6,7},{7,6},{8,9},{9,8},{10,11... | collective-permute-start | bytes 3612680 | tf_op jit(solution)/shard_map/ppermute | solution.py:213
  453.6 3.3 collective-permute-start.13
  464.0 47.9 %collective-permute-start.15 = (bf16[96,768]{0,1:T(8,128)(2,1)S(1)}, bf16[96,768]{0,1:T(8,128)(2,1)S(1)}, u32[]{:S(2)}, u32[]{:S(2)}) collective-permute-start(bf16[96,768]{0,1:T(8,128)(2,1)S(1)} %pad_maximum_fusion.30), channel_id=1, source_target_pairs={{0,2},{2,0},{1,3},{3,1},{4,6},{6,4},{5,7},{7,5},{8,10},{10,8},{9,1... | collective-permute-start | bytes 442376 | tf_op jit(solution)/shard_map/ppermute | solution.py:188
  578.3 7.8 %collective-permute-start.14 = (bf16[96,768]{0,1:T(8,128)(2,1)S(1)}, bf16[96,768]{0,1:T(8,128)(2,1)S(1)}, u32[]{:S(2)}, u32[]{:S(2)}) collective-permute-start(bf16[96,768]{0,1:T(8,128)(2,1)S(1)} %pad_maximum_fusion.29), channel_id=1, source_target_pairs={{0,2},{2,0},{1,3},{3,1},{4,6},{6,4},{5,7},{7,5},{8,10},{10,8},{9,1... | collective-permute-start | bytes 442376 | tf_op jit(solution)/shard_map/ppermute | solution.py:188
  579.9 9.7 %collective-permute-start.16 = (bf16[96,1536]{1,0:T(8,128)(2,1)S(1)}, bf16[96,1536]{1,0:T(8,128)(2,1)S(1)}, u32[]{:S(2)}, u32[]{:S(2)}) collective-permute-start(bf16[96,1536]{1,0:T(8,128)(2,1)S(1)} %pad_maximum_fusion.27), channel_id=1, source_target_pairs={{0,2},{2,0},{1,3},{3,1},{4,6},{6,4},{5,7},{7,5},{8,10},{10,8},{9,1... | collective-permute-start | bytes 884744 | tf_op jit(solution)/shard_map/ppermute | solution.py:188
  (74 other events, 507.7 us)
Sparse Core Ops, SparseCore 0:
  19.0 53.2 all-gather.4
  75.1 50.3 all-gather.6
  128.2 50.3 all-gather.8
  184.5 50.6 all-gather.10
  334.7 68.2 reduce-scatter.5
  406.6 95.8 reduce-scatter.7
  505.9 69.3 reduce-scatter.3

commit v12 on v8

--- a/solution.py
+++ b/solution.py
@@ -76,7 +76,8 @@
     grad_merged = jnp.dot(grad_rows, w_proj.T, preferred_element_type=jnp.float32).astype(
         jnp.bfloat16
     )
-    grad_attended = to_groups(grad_merged.reshape(normed.shape[0], width_here // HD, HD), temporal)
+    grad_attended = to_groups(grad_merged, temporal)
+    grad_attended = grad_attended.reshape(grad_attended.shape[:2] + (width_here // HD, HD))
     query_rows = grouped[:, :, 0]
     key_rows = grouped[:, :, 1]
     value_rows = grouped[:, :, 2]
@@ -148,11 +149,13 @@
 
 
 def gather_mlp(mine, other, width):
-    local = jnp.concatenate(
-        [mine[:, :width], other[:, :width], mine[:, width:], other[:, width:]], axis=1
-    )
-    full = lax.all_gather(local, "dp", axis=0, tiled=True)
-    return full[:, : 2 * width], full[:, 2 * width :].T
+    up = lax.all_gather(
+        jnp.concatenate([mine[:, :width], other[:, :width]], axis=1), "dp", axis=0, tiled=True
+    )
+    down = lax.all_gather(
+        jnp.concatenate([mine[:, width:], other[:, width:]], axis=1), "dp", axis=0, tiled=True
+    )
+    return up, down.T
 
 
 def scatter_rows(pieces):

time: 609 us -> 621 us (1.020)
  waiting for transfers between devices: 154 us -> 167 us
    another operation x0 -> x3, local copies, waits for them, and re-layouts: none -> 14.2 us  [attend_backward(): grad_attended.reshape(grad_attended.shape[:2] + (width_here // HD, HD))]
    another operation x3 -> x1, local copies, waits for them, and re-layouts: 21.6 us -> 11.9 us  [to_groups(): return values.reshape((-1, PATCH) + trailing)]
    all_gather x1 -> x2, waiting for transfers between devices: 13 us -> 20 us  [the longest x1 20 us: gather_mlp(): lax.all_gather(jnp.concatenate([mine[:, width:], other[:, width:]], axis=...]
    another operation x3 -> x2, local copies, waits for them, and re-layouts: 25.3 us -> 20.7 us  [to_groups(): shaped = values.reshape((clip_count, FRAMES, PATCH) + trailing)]
    unnamed x148 -> x140, local copies, waits for them, and re-layouts: 28.2 us -> 30 us
  transfers between devices with their start and end apart: 23 -> 24, of which waited for: 16 -> 16; matrix products, arithmetic and copies ran while one was open for 40% -> 44% of each run, Pallas kernels for 0% -> 0%
where the time goes in v12:
time: 621 us; the launch traced here: 613 us
  matrix products  169 us (27%)
  waiting for transfers between devices  167 us (27%)
  local copies, waits for them, and re-layouts  154 us (25%)
  other arithmetic  56.3 us (9%)
  blocking collectives  40.7 us (7%)
  between operations  16 us (3%)
  starting transfers between devices  11 us (2%)
    reduce_scatter x3, waiting for transfers between devices, scatter_rows(): lax.psum_scatter(jnp.concatenate(flat, axis=1).astype(jnp.bfloat16), 'dp'...  70.6 us
    psum x1, blocking collectives, per_device(): lax.psum(jnp.stack([gain_time, gain_space, gain_mlp]), ('dp', 'ty', 'core'))  40.7 us
    all_gather x2, waiting for transfers between devices, gather_attention(): lax.all_gather(jnp.concatenate([qkv_local, proj_local], axis=1), 'dp', ax...  37.4 us
    unnamed x140, local copies, waits for them, and re-layouts  30 us
    dot_general x1, matrix products, per_device(): jnp.dot(normed_mlp, up_full, preferred_element_type=jnp.float32)  28.3 us
    ppermute x5, waiting for transfers between devices, swap_ty(): return lax.ppermute(values, 'ty', perm=[(0, 1), (1, 0)])  22.9 us
    another operation x2, local copies, waits for them, and re-layouts, to_groups(): shaped = values.reshape((clip_count, FRAMES, PATCH) + trailing)  20.7 us
    all_gather x1, waiting for transfers between devices, gather_mlp(): lax.all_gather(jnp.concatenate([mine[:, width:], other[:, width:]], axis=...  20 us
  transfers between devices with their start and end apart: 24, of which 16 were waited for; matrix products, arithmetic and copies ran while one was open for 44% of the time, Pallas kernels for 0%

profile of v12, /device:TPU:0, one launch (start us, length us, event | category | flops | bytes accessed | tf_op | source)
XLA Modules:
  0.0 613.5 jit_solution(6746014440682097852)
XLA Ops:
  23.5 11.0 %collective-permute-done.4 = bf16[96,2304]{1,0:T(8,128)(2,1)S(1)} collective-permute-done((bf16[96,2304]{1,0:T(8,128)(2,1)}, bf16[96,2304]{1,0:T(8,128)(2,1)S(1)}, u32[]{:S(2)}, u32[]{:S(2)}) %collective-permute-start.4) | collective-permute-done | bytes 442400 | tf_op jit(solution)/shard_map/ppermute | solution.py:189
  36.2 36.1 %all-gather.5.cloned.1.call-done = bf16[768,1536]{1,0:T(8,128)(2,1)} async-done(((bf16[96,1536]{1,0:T(8,128)(2,1)}), bf16[768,1536]{1,0:T(8,128)(2,1)}) %all-gather.5.cloned.1.call-update) | async-done | bytes 2359312 | tf_op jit(solution)/shard_map/all_gather | solution.py:139
  72.3 7.1 %convolution_convert_fusion.1 = bf16[1568,1152]{1,0:T(8,128)(2,1)} fusion(bf16[768,1536]{1,0:T(8,128)(2,1)} %all-gather.5.cloned.1.call-done, bf16[784,768]{1,0:T(8,128)(2,1)} %collective-permute-done, bf16[784,768]{1,0:T(8,128)(2,1)S(1)} %fusion.21), kind=kOutput, calls=%fused_computation.25 | convolution fusion | flops 2781155328 | bytes 7790592 | tf_op jit(solution)/shard_map/dot_general | solution.py:45
  79.4 12.2 %reshape.225 = bf16[1,8,196,3,6,64]{5,4,3,2,1,0:T(8,128)(2,1)} reshape(bf16[1568,1152]{1,0:T(8,128)(2,1)} %convolution_convert_fusion.1) | data formatting | bytes 7225344 | tf_op jit(solution)/shard_map/reshape;reshape | solution.py:28
  91.6 8.4 %copy.151 = bf16[1,8,196,3,6,64]{5,1,4,2,3,0:T(8,128)(2,1)S(1)} copy(bf16[1,8,196,3,6,64]{5,4,3,2,1,0:T(8,128)(2,1)} %reshape.225) | data formatting | bytes 7225344 | tf_op jit(solution)/shard_map/reshape;reshape | solution.py:28
  126.4 7.4 %convolution_convert_fusion = bf16[1568,1152]{1,0:T(8,128)(2,1)} fusion(bf16[768,1536]{1,0:T(8,128)(2,1)} %all-gather.7.cloned.1.call-done, bf16[784,768]{1,0:T(8,128)(2,1)} %collective-permute-done.3, bf16[784,768]{1,0:T(8,128)(2,1)} %multiply_convert_fusion.8), kind=kOutput, calls=%fused_computation.24 | convolution fusion | flops 2781155328 | bytes 7790592 | tf_op jit(solution)/shard_map/dot_general | solution.py:45
  133.8 11.9 %reshape.226 = bf16[8,196,3,6,64]{4,3,2,1,0:T(8,128)(2,1)} reshape(bf16[1568,1152]{1,0:T(8,128)(2,1)} %convolution_convert_fusion) | data formatting | bytes 7225344 | tf_op jit(solution)/shard_map/reshape;reshape | solution.py:31
  145.8 6.7 %fusion.106 = (bf16[8,196,1,6,64]{4,3,2,1,0:T(8,128)(2,1)}, bf16[8,196,1,6,64]{4,3,2,1,0:T(8,128)(2,1)}, bf16[8,196,1,6,64]{4,3,2,1,0:T(8,128)(2,1)}) fusion(bf16[8,196,3,6,64]{4,3,2,1,0:T(8,128)(2,1)} %reshape.226), kind=kLoop, calls=%fused_computation.207 | loop fusion | bytes 7225344 | tf_op jit(solution)/shard_map/slice | solution.py:64
  196.3 28.3 %multiply_convert_fusion.1 = (bf16[1568,1536]{1,0:T(8,128)(2,1)}, f32[1568,1536]{1,0:T(8,128)}, f32[1568,1536]{1,0:T(8,128)}) fusion(bf16[768,1536]{1,0:T(8,128)(2,1)} %all-gather.9.cloned.1.call-done, bf16[784,768]{1,0:T(8,128)(2,1)S(1)} %collective-permute-done.6, bf16[784,768]{1,0:T(8,128)(2,1)S(1)} %multiply_convert_fusion.7), kind=kOutput, calls=%fused_computation.8 | convolution fusion | flops 3860742144 | bytes 28852224 | tf_op jit(solution)/shard_map/dot_general | solution.py:238
  224.6 20.0 %all-gather.11.cloned.1.call-done = bf16[768,1536]{1,0:T(8,128)(2,1)} async-done(((bf16[96,1536]{1,0:T(8,128)(2,1)}), bf16[768,1536]{1,0:T(8,128)(2,1)}) %all-gather.11.cloned.1.call-update) | async-done | bytes 2359312 | tf_op jit(solution)/shard_map/all_gather | solution.py:155
  244.6 12.9 %add_convert_fusion = bf16[1568,1536]{1,0:T(8,128)(2,1)S(1)} fusion(f32[1568,1536]{1,0:T(8,128)} %get-tuple-element.43, bf16[1568,768]{1,0:T(8,128)(2,1)} %constant_dynamic-update-slice_fusion, bf16[768,1536]{1,0:T(8,128)(2,1)} %all-gather.11.cloned.1.call-done, f32[1568,1536]{1,0:T(8,128)} %get-tuple-element.72), kind=kOutput, calls=%fused_computation.7 | convolution fusion | flops 3733094400 | bytes 28852224 | tf_op jit(solution)/shard_map/dot_general | solution.py:247
  291.5 7.4 %fusion.61 = bf16[8,196,1,6,64]{1,4,3,0,2:T(8,128)(2,1)} fusion(bf16[8,196,6,64]{1,3,2,0:T(8,128)(2,1)} %copy.109, f32[8,6,196,196]{2,3,1,0:T(8,128)} %copy-done, f32[8,6,196]{2,1,0:T(8,128)S(1)} %log_add_fusion.1), kind=kOutput, calls=%fused_computation.135 | convolution fusion | flops 242161920 | bytes 9821952 | tf_op jit(solution)/shard_map/bhlm,blhe->bmhe/dot_general | solution.py:89
  299.0 7.4 %multiply_reduce_fusion = (f32[8,6,196]{2,1,0:T(8,128)S(1)}, f32[8,6,196,196]{2,3,1,0:T(8,128)}) fusion(f32[8,6,196,196]{2,3,1,0:T(8,128)} %copy-done, f32[8,6,196]{2,1,0:T(8,128)S(1)} %log_add_fusion.1, bf16[8,196,6,64]{1,3,2,0:T(8,128)(2,1)S(1)} %copy-done.14, bf16[8,196,1,6,64]{1,4,3,0,2:T(8,128)(2,1)S(1)} %copy-done.21), kind=kOutput, calls=%fused_computation.2 | convolution fusion | flops 243394368 | bytes 17235456 | tf_op jit(solution)/shard_map/blhe,bmhe->bhlm/dot_general | solution.py:95
  306.4 11.4 %multiply_convert_fusion = bf16[8,6,196,196]{2,3,1,0:T(8,128)(2,1)} fusion(f32[8,6,196,196]{2,3,1,0:T(8,128)} %get-tuple-element.74, f32[8,6,196,196]{2,3,1,0:T(8,128)} %copy-done, f32[8,6,196]{2,1,0:T(8,128)S(1)} %get-tuple-element.73, f32[8,6,196]{2,1,0:T(8,128)S(1)} %log_add_fusion.1), kind=kLoop, calls=%fused_computation.1 | loop fusion | flops 9219840 | bytes 18514944 | tf_op jit(solution)/shard_map/convert_element_type | solution.py:101
  330.5 9.2 %convert_element_type.179 = bf16[1568,1152]{0,1:T(8,128)(2,1)} reshape(bf16[8,196,3,6,64]{1,0,4,3,2:T(8,128)(2,1)} %copy.114) | data formatting | bytes 7225344 | tf_op jit(solution)/shard_map/convert_element_type | solution.py:110
  350.7 7.7 %convolution_convert_fusion.5 = bf16[768,1536]{1,0:T(8,128)(2,1)S(1)} fusion(bf16[1568,1536]{1,0:T(8,128)(2,1)} %copy-done.62, bf16[784,768]{1,0:T(8,128)(2,1)} %copy-done.58, bf16[784,768]{1,0:T(8,128)(2,1)} %copy-done.28), kind=kOutput, calls=%fused_computation.57 | convolution fusion | flops 3705372672 | bytes 9584640 | tf_op jit(solution)/shard_map/dot_general | solution.py:250
  358.4 7.1 %convolution_convert_fusion.4 = bf16[768,1536]{1,0:T(8,128)(2,1)S(1)} fusion(bf16[1568,768]{1,0:T(8,128)(2,1)S(1)} %copy-done.31, bf16[1568,1536]{1,0:T(8,128)(2,1)} %get-tuple-element.42), kind=kOutput, calls=%fused_computation.56 | convolution fusion | flops 3700555776 | bytes 9584640 | tf_op jit(solution)/shard_map/dot_general | solution.py:246
  368.5 6.2 %fusion.51 = f32[1568,768]{1,0:T(8,128)S(1)} fusion(bf16[1568,1152]{0,1:T(8,128)(2,1)} %convert_element_type.179, bf16[768,1536]{1,0:T(8,128)(2,1)} %all-gather.7.cloned.1.call-done), kind=kOutput, calls=%fused_computation.125 | convolution fusion | flops 2774532096 | bytes 10420224 | tf_op jit(solution)/shard_map/dot_general | solution.py:115
  399.9 7.4 %multiply_reduce_fusion.2 = (f32[196,6,8]{2,1,0:T(8,128)S(1)}, f32[196,6,8,8]{2,3,1,0:T(8,128)S(1)}) fusion(f32[196,6,8,8]{2,3,1,0:T(8,128)} %copy-done.1, f32[196,6,8]{2,1,0:T(8,128)} %log_add_fusion, bf16[196,8,6,64]{3,1,2,0:T(8,128)(2,1)} %copy.116, bf16[196,8,3,6,64]{4,1,3,0,2:T(8,128)(2,1)} %bitcast.159), kind=kOutput, calls=%fused_computation.36 | convolution fusion | flops 9925440 | bytes 10775296 | tf_op jit(solution)/shard_map/blhe,bmhe->bhlm/dot_general | solution.py:95
  420.8 12.0 %copy.119 = bf16[1,8,196,3,6,64]{2,1,5,4,3,0:T(8,128)(2,1)} copy(bf16[1,8,196,3,6,64]{5,1,4,2,3,0:T(8,128)(2,1)} %maximum_bitcast_fusion) | data formatting | bytes 7225344 | tf_op jit(solution)/shard_map/transpose | solution.py:38
  432.8 9.0 %reshape_reshape.28 = bf16[1568,1152]{0,1:T(8,128)(2,1)} reshape(bf16[1,8,196,3,6,64]{2,1,5,4,3,0:T(8,128)(2,1)} %copy.119) | data formatting | bytes 7225344 | tf_op jit(solution)/shard_map/reshape;reshape | solution.py:111
  452.5 6.1 fusion.54
  475.0 40.7 %psum.7 = f32[3,768]{1,0:T(4,128)} all-reduce(f32[3,768]{1,0:T(4,128)S(1)} %pad_maximum_fusion.31), channel_id=1, replica_groups=mesh['dp'=8,'ty'=2,'core'=2] {'dp','ty','core'}, use_global_device_ids=true, to_apply=%region_21.0 | all-reduce | flops 2304 | bytes 18432 | tf_op jit(solution)/shard_map/psum | solution.py:284
  520.5 70.6 %reduce-scatter.4.cloned.1.call-done = bf16[96,1536]{1,0:T(8,128)(2,1)} async-done(((bf16[768,1536]{1,0:T(8,128)(2,1)}), bf16[96,1536]{1,0:T(8,128)(2,1)}) %reduce-scatter.4.cloned.1.call-update) | async-done | bytes 294928 | tf_op jit(solution)/shard_map/reduce_scatter | solution.py:163
  (324 shorter events, 233.1 us)
Async XLA Ops:
  7.2 65.1 %all-gather.5.cloned.1.call-start = ((), (), s32[]{:S(2)}) async-start(), calls=%async_computation.3 | async-start | bytes 2654208 | tf_op jit(solution)/shard_map/all_gather | solution.py:139
  9.4 8.0 %collective-permute-start.1 = (bf16[96,768]{0,1:T(8,128)(2,1)S(1)}, bf16[96,768]{0,1:T(8,128)(2,1)S(1)}, u32[]{:S(2)}, u32[]{:S(2)}) collective-permute-start(bf16[96,768]{0,1:T(8,128)(2,1)S(1)} %pad_maximum_fusion.28), channel_id=1, source_target_pairs={{0,2},{2,0},{1,3},{3,1},{4,6},{6,4},{5,7},{7,5},{8,10},{10,8},{9,1... | collective-permute-start | bytes 442376 | tf_op jit(solution)/shard_map/ppermute | solution.py:189
  18.9 106.6 %all-gather.7.cloned.1.call-start = ((), (), s32[]{:S(2)}) async-start(), calls=%async_computation.4 | async-start | bytes 2654208 | tf_op jit(solution)/shard_map/all_gather | solution.py:139
  20.3 15.9 %collective-permute-start = (bf16[784,768]{1,0:T(8,128)(2,1)S(1)}, bf16[784,768]{1,0:T(8,128)(2,1)}, u32[]{:S(2)}, u32[]{:S(2)}) collective-permute-start(bf16[784,768]{1,0:T(8,128)(2,1)S(1)} %fusion.21), channel_id=1, source_target_pairs={{0,1},{1,0},{2,3},{3,2},{4,5},{5,4},{6,7},{7,6},{8,9},{9,8},{10,11... | collective-permute-start | bytes 3612680 | tf_op jit(solution)/shard_map/ppermute | solution.py:214
  21.8 12.8 %collective-permute-start.4 = (bf16[96,2304]{1,0:T(8,128)(2,1)}, bf16[96,2304]{1,0:T(8,128)(2,1)S(1)}, u32[]{:S(2)}, u32[]{:S(2)}) collective-permute-start(bf16[96,2304]{1,0:T(8,128)(2,1)} %concatenate.78), channel_id=1, source_target_pairs={{0,2},{2,0},{1,3},{3,1},{4,6},{6,4},{5,7},{7,5},{8,10},{10,8},{9,1... | collective-permute-start | bytes 1327112 | tf_op jit(solution)/shard_map/ppermute | solution.py:189
  36.2 160.1 %all-gather.9.cloned.1.call-start = ((), (), s32[]{:S(2)}) async-start(), calls=%async_computation.5 | async-start | bytes 2654208 | tf_op jit(solution)/shard_map/all_gather | solution.py:152
  117.8 2.9 collective-permute-start.2
  123.2 3.2 collective-permute-start.3
  124.1 120.5 %all-gather.11.cloned.1.call-start = ((), (), s32[]{:S(2)}) async-start(), calls=%async_computation.6 | async-start | bytes 2654208 | tf_op jit(solution)/shard_map/all_gather | solution.py:155
  185.5 2.9 collective-permute-start.5
  185.6 8.2 %collective-permute-start.8 = (bf16[784,768]{1,0:T(8,128)(2,1)}, bf16[784,768]{1,0:T(8,128)(2,1)}, u32[]{:S(2)}, u32[]{:S(2)}) collective-permute-start(bf16[784,768]{1,0:T(8,128)(2,1)} %param.10), channel_id=1, source_target_pairs={{0,1},{1,0},{2,3},{3,2},{4,5},{5,4},{6,7},{7,6},{8,9},{9,8},{10,11... | collective-permute-start | bytes 3612680 | tf_op jit(solution)/shard_map/ppermute | solution.py:214
  190.2 6.1 collective-permute-start.6
  193.8 271.6 %reduce-scatter.6.cloned.1.call-start = ((), (), s32[]{:S(2)}) async-start(), calls=%async_computation.8 | async-start | bytes 2654208 | tf_op jit(solution)/shard_map/reduce_scatter | solution.py:163
  261.7 5.9 collective-permute-start.9
  267.5 2.9 collective-permute-start.7
  274.5 2.9 collective-permute-start.10
  350.7 168.7 %reduce-scatter.8.cloned.1.call-start = ((), (), s32[]{:S(2)}) async-start(), calls=%async_computation.9 | async-start | bytes 5308416 | tf_op jit(solution)/shard_map/reduce_scatter | solution.py:163
  368.3 222.8 %reduce-scatter.4.cloned.1.call-start = ((), (), s32[]{:S(2)}) async-start(), calls=%async_computation.7 | async-start | bytes 2654208 | tf_op jit(solution)/shard_map/reduce_scatter | solution.py:163
  374.8 2.9 collective-permute-start.11
  382.5 2.9 collective-permute-start.12
  458.8 2.9 collective-permute-start.13
  468.4 47.7 %collective-permute-start.15 = (bf16[96,768]{0,1:T(8,128)(2,1)S(1)}, bf16[96,768]{0,1:T(8,128)(2,1)S(1)}, u32[]{:S(2)}, u32[]{:S(2)}) collective-permute-start(bf16[96,768]{0,1:T(8,128)(2,1)S(1)} %pad_maximum_fusion.30), channel_id=1, source_target_pairs={{0,2},{2,0},{1,3},{3,1},{4,6},{6,4},{5,7},{7,5},{8,10},{10,8},{9,1... | collective-permute-start | bytes 442376 | tf_op jit(solution)/shard_map/ppermute | solution.py:189
  594.1 7.8 %collective-permute-start.14 = (bf16[96,768]{0,1:T(8,128)(2,1)S(1)}, bf16[96,768]{0,1:T(8,128)(2,1)S(1)}, u32[]{:S(2)}, u32[]{:S(2)}) collective-permute-start(bf16[96,768]{0,1:T(8,128)(2,1)S(1)} %pad_maximum_fusion.29), channel_id=1, source_target_pairs={{0,2},{2,0},{1,3},{3,1},{4,6},{6,4},{5,7},{7,5},{8,10},{10,8},{9,1... | collective-permute-start | bytes 442376 | tf_op jit(solution)/shard_map/ppermute | solution.py:189
  595.6 9.6 %collective-permute-start.16 = (bf16[96,1536]{1,0:T(8,128)(2,1)S(1)}, bf16[96,1536]{1,0:T(8,128)(2,1)S(1)}, u32[]{:S(2)}, u32[]{:S(2)}) collective-permute-start(bf16[96,1536]{1,0:T(8,128)(2,1)S(1)} %pad_maximum_fusion.27), channel_id=1, source_target_pairs={{0,2},{2,0},{1,3},{3,1},{4,6},{6,4},{5,7},{7,5},{8,10},{10,8},{9,1... | collective-permute-start | bytes 884744 | tf_op jit(solution)/shard_map/ppermute | solution.py:189
  (65 other events, 535.6 us)
Sparse Core Ops, SparseCore 0:
  19.0 53.2 all-gather.4
  75.1 50.3 all-gather.6
  128.2 50.3 all-gather.8
  194.0 50.5 all-gather.10
  350.8 68.2 reduce-scatter.5
  422.6 96.1 reduce-scatter.7
  522.3 68.7 reduce-scatter.3
